TPU v7x, 768 devices: a whole 4x8x12 slice. The times are simulated.
768 devices in a mesh: gx: 96 (over z, x, core), gy: 8 (over y).
Axes of the slice: x: 4, y: 8, z: 12, core: 2. Of those that a mesh axis runs over, the one named last changes fastest.
Arguments:
- populations: float32 [19, 3, 3072, 1024], P(None, None, 'gx', 'gy'), may hold values from 0.2 to 1
- solid_flag: int32 [3, 3072, 1024], P(None, 'gx', 'gy'), may hold values 0 or 1
- cell_patch: int32 [3, 3072, 1024], P(None, 'gx', 'gy'), may hold values from 0 to 512
- patch_zone: int32 [393216], P(('gx', 'gy')), may hold values from 0 to 98303, as said below
- old_pressure: float32 [98304], P(('gx', 'gy')), may hold values from -6 to 6
- leakage: float32 [98304], P(('gx', 'gy')), may hold values from 0.1 to 1
- conductance: float32 [6, 98304], P(None, ('gx', 'gy')), may hold values from 0.05 to 0.5
- neighbour: int32 [6, 98304], P(None, ('gx', 'gy')), may hold values from 0 to 127
Outputs:
- new_populations: float32 [19, 3, 3072, 1024], P(None, None, 'gx', 'gy')
- zone_pressure: float32 [98304], P(('gx', 'gy'))
- opening_pressure: float32 [393216], P(('gx', 'gy'))
Inputs may be any that keep to these rules, and one draw needn't show every extreme that they name: `patch_zone`: within each aligned block of 512 patches (one tile), at most 2 patches name zones of one block of 128 zones, and in every tile some block of zones receives exactly 2. `cell_patch`: the value 512 marks a cell in no opening.
All inputs are finite; a program needn't handle non-finite values. No bound on the sum of `solid_flag` on one device may be relied on, other than what follows from the above.
Results may differ from a plain program's by a relative error of at most 0.00002.
Values sent between devices are 32-bit elements; how exact they have to be, the bound alone decides.
No kernel may reach another device: no remote copies, remote signals or barrier semaphores. Data moves between devices by JAX's collectives and lax.ppermute only.
A program may use at most 32 MiB of HBM per device.

v0:
```python
import jax
import jax.numpy as jnp
import numpy as np
from jax import lax
from jax.sharding import PartitionSpec as P

DIRECTIONS = np.array(
    [
        [0, 0, 0],
        [1, 0, 0],
        [-1, 0, 0],
        [0, 1, 0],
        [0, -1, 0],
        [0, 0, 1],
        [0, 0, -1],
        [1, 1, 0],
        [-1, -1, 0],
        [1, -1, 0],
        [-1, 1, 0],
        [1, 0, 1],
        [-1, 0, -1],
        [1, 0, -1],
        [-1, 0, 1],
        [0, 1, 1],
        [0, -1, -1],
        [0, 1, -1],
        [0, -1, 1],
    ]
)
OPPOSITE = [0, 2, 1, 4, 3, 6, 5, 8, 7, 10, 9, 12, 11, 14, 13, 16, 15, 18, 17]
LATTICE_WEIGHTS = [1.0 / 3.0] + [1.0 / 18.0] * 6 + [1.0 / 36.0] * 12
OMEGA = 1.25
FACE_AREA = 0.25


def with_halo(cells, sides, width):
    for axis, dim in sides:
        count = lax.axis_size(axis)
        head = lax.slice_in_dim(cells, 0, width, axis=dim)
        tail = lax.slice_in_dim(cells, cells.shape[dim] - width, cells.shape[dim], axis=dim)
        cells = jnp.concatenate(
            [
                lax.ppermute(tail, axis, [(i, (i + 1) % count) for i in range(count)]),
                cells,
                lax.ppermute(head, axis, [((i + 1) % count, i) for i in range(count)]),
            ],
            axis=dim,
        )
    return cells


def moment(populations, component):
    total = jnp.zeros_like(populations[0])
    for direction in range(19):
        sign = int(DIRECTIONS[direction, component])
        if sign != 0:
            total = total + float(sign) * populations[direction]
    return total


def collide(populations):
    density = jnp.zeros_like(populations[0])
    for direction in range(19):
        density = density + populations[direction]
    velocity = [moment(populations, component) / density for component in range(3)]
    speed_sq = velocity[0] * velocity[0] + velocity[1] * velocity[1] + velocity[2] * velocity[2]
    relaxed = []
    for direction in range(19):
        along = jnp.zeros_like(density)
        for component in range(3):
            sign = int(DIRECTIONS[direction, component])
            if sign != 0:
                along = along + float(sign) * velocity[component]
        equilibrium = (
            LATTICE_WEIGHTS[direction]
            * density
            * (1.0 + 3.0 * along + 4.5 * along * along - 1.5 * speed_sq)
        )
        relaxed.append(populations[direction] - OMEGA * (populations[direction] - equilibrium))
    return jnp.stack(relaxed)


def stream(post_pad, flag_pad, relaxed, populations, solid_flag):
    depth, width_x, width_y = solid_flag.shape
    passed = []
    for direction in range(19):
        step_x = int(DIRECTIONS[direction, 0])
        step_y = int(DIRECTIONS[direction, 1])
        step_z = int(DIRECTIONS[direction, 2])
        source = post_pad[
            direction,
            1 - step_z : 1 - step_z + depth,
            1 - step_x : 1 - step_x + width_x,
            1 - step_y : 1 - step_y + width_y,
        ]
        open_source = flag_pad[
            1 - step_z : 1 - step_z + depth,
            1 - step_x : 1 - step_x + width_x,
            1 - step_y : 1 - step_y + width_y,
        ]
        pulled = open_source * source + (1.0 - open_source) * relaxed[OPPOSITE[direction]]
        passed.append(jnp.where(solid_flag == 1, populations[direction], pulled))
    return jnp.stack(passed)


def relax(inflow, old_pressure, leakage, conductance, neighbour):
    coupled = jnp.zeros_like(inflow)
    total = leakage
    for link in range(conductance.shape[0]):
        coupled = coupled + conductance[link] * old_pressure[neighbour[link]]
        total = total + conductance[link]
    return (inflow + coupled) / total


def on_device(
    populations, solid_flag, cell_patch, patch_zone, old_pressure, leakage, conductance, neighbour
):
    depth, width_x, width_y = solid_flag.shape
    relaxed = collide(populations)
    fluid = (1 - solid_flag).astype(jnp.float32)
    column = lax.axis_index("gy")
    lower_open = jnp.where(column > 0, 1.0, 0.0).astype(jnp.float32)
    upper_open = jnp.where(column < lax.axis_size("gy") - 1, 1.0, 0.0).astype(jnp.float32)
    places = jnp.arange(width_y + 2, dtype=jnp.int32)
    keeper = jnp.where(places == 0, lower_open, jnp.where(places == width_y + 1, upper_open, 1.0))
    stacked = jnp.concatenate([relaxed, fluid[None]], axis=0)
    widened = with_halo(stacked, (("gx", 2), ("gy", 3)), 1)
    widened = jnp.pad(widened, ((0, 0), (1, 1), (0, 0), (0, 0)))
    flag_pad = widened[19] * keeper
    post_pad = widened[:19]
    new_populations = stream(post_pad, flag_pad, relaxed, populations, solid_flag)
    momentum_x = moment(new_populations, 0)
    openings = patch_zone.shape[0]
    sums = jax.ops.segment_sum(
        momentum_x.reshape(-1), cell_patch.reshape(-1), num_segments=openings + 1
    )
    patch_flux = FACE_AREA * sums[:openings]
    zone_dev = old_pressure.shape[0]
    count_x = lax.axis_size("gx")
    count_y = lax.axis_size("gy")
    devices = count_x * count_y
    capacity = max(2, (2 * openings + devices - 1) // devices)
    owner_block = patch_zone // zone_dev
    local_zone = patch_zone - owner_block * zone_dev
    patch_order = jnp.arange(openings, dtype=jnp.int32)
    earlier_same = (owner_block[:, None] == owner_block[None, :]) & (
        patch_order[:, None] > patch_order[None, :]
    )
    slot_rank = jnp.sum(earlier_same.astype(jnp.int32), axis=1)
    slot_index = owner_block * capacity + slot_rank
    targets = jnp.arange(devices * capacity, dtype=jnp.int32)
    placed = slot_index[:, None] == targets[None, :]
    send_flux = jnp.sum(jnp.where(placed, patch_flux[:, None], 0.0), axis=0)
    send_zone = jnp.sum(jnp.where(placed, local_zone.astype(jnp.float32)[:, None], 0.0), axis=0)
    outgoing = jnp.stack([send_flux, send_zone]).reshape(2, count_x, count_y, capacity)
    arrived = lax.all_to_all(
        lax.all_to_all(outgoing, "gx", split_axis=1, concat_axis=1, tiled=True),
        "gy",
        split_axis=2,
        concat_axis=2,
        tiled=True,
    )
    arrived = arrived.reshape(2, devices * capacity)
    matched = arrived[1][None, :] == jnp.arange(zone_dev, dtype=jnp.float32)[:, None]
    inflow = jnp.sum(jnp.where(matched, arrived[0][None, :], 0.0), axis=1)
    zone_pressure = relax(inflow, old_pressure, leakage, conductance, neighbour)
    answered = jnp.sum(jnp.where(matched, zone_pressure[:, None], 0.0), axis=0).reshape(
        count_x, count_y, capacity
    )
    returned = lax.all_to_all(
        lax.all_to_all(answered, "gx", split_axis=0, concat_axis=0, tiled=True),
        "gy",
        split_axis=1,
        concat_axis=1,
        tiled=True,
    ).reshape(-1)
    opening_pressure = jnp.sum(jnp.where(placed, returned[None, :], 0.0), axis=1)
    return (new_populations, zone_pressure, opening_pressure)


def solution(mesh):
    placed = (
        P(None, None, "gx", "gy"),
        P(None, "gx", "gy"),
        P(None, "gx", "gy"),
        P(("gx", "gy")),
        P(("gx", "gy")),
        P(("gx", "gy")),
        P(None, ("gx", "gy")),
        P(None, ("gx", "gy")),
    )
    return jax.shard_map(
        on_device,
        mesh=mesh,
        in_specs=placed,
        out_specs=(P(None, None, "gx", "gy"), P(("gx", "gy")), P(("gx", "gy"))),
        check_vma=False,
    )
```

profile of v0, /device:TPU:1, one launch (start us, length us, event | category | flops | bytes accessed | tf_op | source)
XLA Modules:
  0.0 241.6 jit_solution(4356112992419163400)
XLA Ops:
  9.2 4.5 %collective-permute-start = (f32[20,3,1,128]{3,2,1,0:T(1,128)S(1)}, f32[20,3,1,128]{3,2,1,0:T(1,128)S(1)}, u32[]{:S(2)}, u32[]{:S(2)}) collective-permute-start(f32[20,3,1,128]{3,2,1,0:T(1,128)S(1)} %get-tuple-element.35), channel_id=1, source_target_pairs={{0,8},{8,16},{16,24},{24,32},{32,40},{40,48},{48,56},{56,64},{64,7... | collective-permute-start | bytes 92168 | tf_op jit(solution)/shard_map/ppermute | solution.py:43
  13.7 9.8 %collective-permute-start.1 = (f32[20,3,1,128]{3,2,1,0:T(1,128)S(1)}, f32[20,3,1,128]{3,2,1,0:T(1,128)S(1)}, u32[]{:S(2)}, u32[]{:S(2)}) collective-permute-start(f32[20,3,1,128]{3,2,1,0:T(1,128)S(1)} %get-tuple-element.36), channel_id=1, source_target_pairs={{8,0},{16,8},{24,16},{32,24},{40,32},{48,40},{56,48},{64,56},{72,6... | collective-permute-start | bytes 92168 | tf_op jit(solution)/shard_map/ppermute | solution.py:45
  28.0 1.8 copy.57
  30.9 2.0 collective-permute-start.3
  33.0 3.4 %collective-permute-start.2 = (f32[20,3,34,1]{2,3,1,0:T(1,128)S(1)}, f32[20,3,34,1]{2,3,1,0:T(1,128)S(1)}, u32[]{:S(2)}, u32[]{:S(2)}) collective-permute-start(f32[20,3,34,1]{2,3,1,0:T(1,128)S(1)} %copy.57), channel_id=1, source_target_pairs={{0,1},{1,2},{2,3},{3,4},{4,5},{5,6},{6,7},{7,0},{8,9},{9,10},{10,1... | collective-permute-start | bytes 24488 | tf_op jit(solution)/shard_map/ppermute | solution.py:43
  36.4 1.7 gather_fusion.1
  38.1 1.8 gather_fusion
  39.9 1.8 gather_fusion.3
  41.7 1.8 gather_fusion.2
  43.5 1.7 gather_fusion.5
  45.2 1.7 gather_fusion.4
  47.4 1.6 copy.60
  49.1 3.0 %select_maximum_fusion = f32[20,5,34,130]{3,2,1,0:T(8,128)S(1)} fusion(f32[20,3,34,1]{3,2,1,0:T(8,128)} %copy.60, f32[20,3,34,1]{3,2,1,0:T(8,128)S(1)} %copy.59, f32[20,3,1,128]{3,2,1,0:T(1,128)S(1)} %copy-done.16, f32[20,3,32,128]{3,2,1,0:T(8,128)S(1)} %constant_dynamic-update-slice_fusion, f32[20,3,1,128]{3,2,1,0:T(1,128)S(1)} %copy-done.12), kind=kLoop, calls=%fused_computation.9 | loop fusion | flops 5304000 | bytes 2828800 | tf_op jit(solution)/shard_map/concatenate | solution.py:41
  52.2 1.7 multiply_add_fusion
  54.3 85.9 %scatter_custom_fusion = f32[513]{0:T(1024)} fusion(s32[12288]{0:T(1024)} %bitcast.601, f32[12288]{0:T(1024)} %bitcast.600, f32[]{:T(128)} %constant.55.clone.1), kind=kCustom, calls=%fused_computation.489 | custom fusion | flops 12288 | bytes 2564 | tf_op jit(solution)/shard_map/scatter-add | solution.py:134
  140.9 2.0 select_reduce_fusion.2
  142.9 1.8 stack.108
  144.7 1.8 stack.109
  146.5 2.0 pad_maximum_fusion.1
  148.5 3.0 %copy.63 = f32[2,96,8,2]{2,3,0,1:T(2,128)} copy(f32[2,96,8,2]{3,2,1,0:T(8,128)} %pad_maximum_fusion.1) | data formatting | bytes 24576 | tf_op jit(solution)/shard_map/stack | solution.py:155
  151.5 16.8 %all-to-all-start = ((f32[2,96,8,2]{2,3,0,1:T(2,128)}), f32[2,96,8,2]{2,3,0,1:T(2,128)}, u32[]{:S(2)}, u32[]{:S(2)}) async-start(f32[2,96,8,2]{2,3,0,1:T(2,128)} %copy.63), calls=%async_computation | async-start | bytes 393216 | tf_op jit(solution)/shard_map/all_to_all | solution.py:157
  172.8 1.6 constant_dynamic-update-slice_fusion.35
  176.9 1.6 constant_dynamic-update-slice_fusion.32
  185.1 1.6 copy.64
  186.7 5.1 %all-to-all-start.1 = ((f32[2,96,8,2]{1,3,0,2:T(2,128)}), f32[2,96,8,2]{1,3,0,2:T(2,128)S(1)}, u32[]{:S(2)}, u32[]{:S(2)}) async-start(f32[2,96,8,2]{1,3,0,2:T(2,128)} %copy.64), calls=%async_computation.1 | async-start | bytes 32768 | tf_op jit(solution)/shard_map/all_to_all | solution.py:156
  191.8 1.6 constant_dynamic-update-slice_fusion.22
  193.4 5.0 %all-to-all-done.1 = f32[2,96,8,2]{1,3,0,2:T(2,128)S(1)} async-done(((f32[2,96,8,2]{1,3,0,2:T(2,128)}), f32[2,96,8,2]{1,3,0,2:T(2,128)S(1)}, u32[]{:S(2)}, u32[]{:S(2)}) %all-to-all-start.1) | async-done | bytes 12320 | tf_op jit(solution)/shard_map/all_to_all | solution.py:156
  201.4 14.6 %all-to-all-start.2 = ((f32[96,8,2]{1,2,0:T(2,128)}), f32[96,8,2]{1,2,0:T(2,128)S(1)}, u32[]{:S(2)}, u32[]{:S(2)}) async-start(f32[96,8,2]{1,2,0:T(2,128)} %copy.67), calls=%async_computation.2 | async-start | bytes 196608 | tf_op jit(solution)/shard_map/all_to_all | solution.py:171
  217.5 12.0 %all-to-all-done.2 = f32[96,8,2]{1,2,0:T(2,128)S(1)} async-done(((f32[96,8,2]{1,2,0:T(2,128)}), f32[96,8,2]{1,2,0:T(2,128)S(1)}, u32[]{:S(2)}, u32[]{:S(2)}) %all-to-all-start.2) | async-done | bytes 6176 | tf_op jit(solution)/shard_map/all_to_all | solution.py:171
  230.2 3.3 %all-to-all-start.3 = ((f32[96,8,2]{0,2,1:T(2,128)}), f32[96,8,2]{0,2,1:T(2,128)S(1)}, u32[]{:S(2)}, u32[]{:S(2)}) async-start(f32[96,8,2]{0,2,1:T(2,128)} %copy.68), calls=%async_computation.3 | async-start | bytes 16384 | tf_op jit(solution)/shard_map/all_to_all | solution.py:170
  233.5 1.6 constant_dynamic-update-slice_fusion.20
  235.2 4.9 %all-to-all-done.3 = f32[96,8,2]{0,2,1:T(2,128)S(1)} async-done(((f32[96,8,2]{0,2,1:T(2,128)}), f32[96,8,2]{0,2,1:T(2,128)S(1)}, u32[]{:S(2)}, u32[]{:S(2)}) %all-to-all-start.3) | async-done | bytes 6176 | tf_op jit(solution)/shard_map/all_to_all | solution.py:170
  (152 shorter events, 35.5 us)
Async XLA Ops:
  0.6 35.8 %copy-start = (f32[128]{0:T(128)S(1)}, f32[128]{0:T(128)}, u32[]{:S(2)}) copy-start(f32[128]{0:T(128)} %param.12) | copy-start | bytes 1540
  0.6 8.1 %copy-start.1 = (f32[19,3,32,128]{3,2,1,0:T(8,128)S(1)}, f32[19,3,32,128]{3,2,1,0:T(8,128)}, u32[]{:S(2)}) copy-start(f32[19,3,32,128]{3,2,1,0:T(8,128)} %param.8) | copy-start | bytes 2801668
  0.7 8.5 %copy-start.20 = (s32[3,32,128]{2,1,0:T(8,128)S(1)}, s32[3,32,128]{2,1,0:T(8,128)}, u32[]{:S(2)}) copy-start(s32[3,32,128]{2,1,0:T(8,128)} %param.9) | copy-start | bytes 147460
  2.1 22.2 %copy-start.30 = (s32[6,128]{1,0:T(8,128)S(1)}, s32[6,128]{1,0:T(8,128)}, u32[]{:S(2)}) copy-start(s32[6,128]{1,0:T(8,128)} %param.15) | copy-start | bytes 9220
  2.1 22.2 %copy-start.32 = (s32[512]{0:T(512)S(1)}, s32[512]{0:T(512)}, u32[]{:S(2)}) copy-start(s32[512]{0:T(512)} %param.11) | copy-start | bytes 6148
  9.2 16.0 %collective-permute-start = (f32[20,3,1,128]{3,2,1,0:T(1,128)S(1)}, f32[20,3,1,128]{3,2,1,0:T(1,128)S(1)}, u32[]{:S(2)}, u32[]{:S(2)}) collective-permute-start(f32[20,3,1,128]{3,2,1,0:T(1,128)S(1)} %get-tuple-element.35), channel_id=1, source_target_pairs={{0,8},{8,16},{16,24},{24,32},{32,40},{40,48},{48,56},{56,64},{64,7... | collective-permute-start | bytes 92168 | tf_op jit(solution)/shard_map/ppermute | solution.py:43
  13.7 11.5 %collective-permute-start.1 = (f32[20,3,1,128]{3,2,1,0:T(1,128)S(1)}, f32[20,3,1,128]{3,2,1,0:T(1,128)S(1)}, u32[]{:S(2)}, u32[]{:S(2)}) collective-permute-start(f32[20,3,1,128]{3,2,1,0:T(1,128)S(1)} %get-tuple-element.36), channel_id=1, source_target_pairs={{8,0},{16,8},{24,16},{32,24},{40,32},{48,40},{56,48},{64,56},{72,6... | collective-permute-start | bytes 92168 | tf_op jit(solution)/shard_map/ppermute | solution.py:45
  30.9 18.1 %copy-start.12 = (f32[20,3,1,128]{3,2,1,0:T(1,128)S(1)}, f32[20,3,1,128]{3,2,1,0:T(1,128)}, u32[]{:S(2)}) copy-start(f32[20,3,1,128]{3,2,1,0:T(1,128)} %copy-done.11) | copy-start | bytes 92164
  30.9 18.1 %copy-start.16 = (f32[20,3,1,128]{3,2,1,0:T(1,128)S(1)}, f32[20,3,1,128]{3,2,1,0:T(1,128)}, u32[]{:S(2)}) copy-start(f32[20,3,1,128]{3,2,1,0:T(1,128)} %copy-done.15) | copy-start | bytes 92164
  30.9 16.5 %collective-permute-start.3 = (f32[20,3,34,1]{2,3,1,0:T(1,128)}, f32[20,3,34,1]{2,3,1,0:T(1,128)S(1)}, u32[]{:S(2)}, u32[]{:S(2)}) collective-permute-start(f32[20,3,34,1]{2,3,1,0:T(1,128)} %copy.58), channel_id=1, source_target_pairs={{1,0},{2,1},{3,2},{4,3},{5,4},{6,5},{7,6},{0,7},{9,8},{10,9},{11,1... | collective-permute-start | bytes 24488 | tf_op jit(solution)/shard_map/ppermute | solution.py:45
  33.0 13.9 %collective-permute-start.2 = (f32[20,3,34,1]{2,3,1,0:T(1,128)S(1)}, f32[20,3,34,1]{2,3,1,0:T(1,128)S(1)}, u32[]{:S(2)}, u32[]{:S(2)}) collective-permute-start(f32[20,3,34,1]{2,3,1,0:T(1,128)S(1)} %copy.57), channel_id=1, source_target_pairs={{0,1},{1,2},{2,3},{3,4},{4,5},{5,6},{6,7},{7,0},{8,9},{9,10},{10,1... | collective-permute-start | bytes 24488 | tf_op jit(solution)/shard_map/ppermute | solution.py:43
  151.5 33.6 %all-to-all-start = ((f32[2,96,8,2]{2,3,0,1:T(2,128)}), f32[2,96,8,2]{2,3,0,1:T(2,128)}, u32[]{:S(2)}, u32[]{:S(2)}) async-start(f32[2,96,8,2]{2,3,0,1:T(2,128)} %copy.63), calls=%async_computation | async-start | bytes 393216 | tf_op jit(solution)/shard_map/all_to_all | solution.py:157
  169.9 8.6 %copy-start.29 = (f32[3,32,128]{2,1,0:T(8,128)S(1)}, f32[3,32,128]{2,1,0:T(8,128)}, u32[]{:S(2)}) copy-start(f32[3,32,128]{2,1,0:T(8,128)} %get-tuple-element.18) | copy-start | bytes 147460
  172.8 8.3 %copy-start.25 = (f32[3,32,128]{2,1,0:T(8,128)S(1)}, f32[3,32,128]{2,1,0:T(8,128)}, u32[]{:S(2)}) copy-start(f32[3,32,128]{2,1,0:T(8,128)} %get-tuple-element.14) | copy-start | bytes 147460
  172.8 8.9 %copy-start.24 = (f32[3,32,128]{2,1,0:T(8,128)S(1)}, f32[3,32,128]{2,1,0:T(8,128)}, u32[]{:S(2)}) copy-start(f32[3,32,128]{2,1,0:T(8,128)} %get-tuple-element.13) | copy-start | bytes 147460
  172.8 9.5 %copy-start.23 = (f32[3,32,128]{2,1,0:T(8,128)S(1)}, f32[3,32,128]{2,1,0:T(8,128)}, u32[]{:S(2)}) copy-start(f32[3,32,128]{2,1,0:T(8,128)} %get-tuple-element.12) | copy-start | bytes 147460
  172.8 10.2 %copy-start.22 = (f32[3,32,128]{2,1,0:T(8,128)S(1)}, f32[3,32,128]{2,1,0:T(8,128)}, u32[]{:S(2)}) copy-start(f32[3,32,128]{2,1,0:T(8,128)} %get-tuple-element.11) | copy-start | bytes 147460
  172.8 19.0 %copy-start.6 = (f32[3,32,128]{2,1,0:T(8,128)S(1)}, f32[3,32,128]{2,1,0:T(8,128)}, u32[]{:S(2)}) copy-start(f32[3,32,128]{2,1,0:T(8,128)} %get-tuple-element.23) | copy-start | bytes 147460
  172.8 19.0 %copy-start.8 = (f32[3,32,128]{2,1,0:T(8,128)S(1)}, f32[3,32,128]{2,1,0:T(8,128)}, u32[]{:S(2)}) copy-start(f32[3,32,128]{2,1,0:T(8,128)} %get-tuple-element.22) | copy-start | bytes 147460
  174.5 17.3 %copy-start.10 = (pred[3,32,128]{2,1,0:T(8,128)(4,1)S(1)}, pred[3,32,128]{2,1,0:T(8,128)(4,1)}, u32[]{:S(2)}) copy-start(pred[3,32,128]{2,1,0:T(8,128)(4,1)} %get-tuple-element.24) | copy-start | bytes 36868
  174.5 25.0 %copy-start.31 = (f32[6,128]{1,0:T(8,128)S(1)}, f32[6,128]{1,0:T(8,128)}, u32[]{:S(2)}) copy-start(f32[6,128]{1,0:T(8,128)} %param.14) | copy-start | bytes 9220
  174.5 25.0 %copy-start.34 = (f32[128]{0:T(128)S(1)}, f32[128]{0:T(128)}, u32[]{:S(2)}) copy-start(f32[128]{0:T(128)} %gather_fusion.1) | copy-start | bytes 1540
  174.5 25.0 %copy-start.35 = (f32[128]{0:T(128)S(1)}, f32[128]{0:T(128)}, u32[]{:S(2)}) copy-start(f32[128]{0:T(128)} %gather_fusion) | copy-start | bytes 1540
  174.5 25.0 %copy-start.36 = (f32[128]{0:T(128)S(1)}, f32[128]{0:T(128)}, u32[]{:S(2)}) copy-start(f32[128]{0:T(128)} %gather_fusion.3) | copy-start | bytes 1540
  174.5 25.0 %copy-start.37 = (f32[128]{0:T(128)S(1)}, f32[128]{0:T(128)}, u32[]{:S(2)}) copy-start(f32[128]{0:T(128)} %gather_fusion.2) | copy-start | bytes 1540
  174.5 25.0 %copy-start.38 = (f32[128]{0:T(128)S(1)}, f32[128]{0:T(128)}, u32[]{:S(2)}) copy-start(f32[128]{0:T(128)} %gather_fusion.5) | copy-start | bytes 1540
  174.5 25.0 %copy-start.39 = (f32[128]{0:T(128)S(1)}, f32[128]{0:T(128)}, u32[]{:S(2)}) copy-start(f32[128]{0:T(128)} %gather_fusion.4) | copy-start | bytes 1540
  174.5 25.0 %copy-start.40 = (f32[128]{0:T(128)S(1)}, f32[128]{0:T(128)}, u32[]{:S(2)}) copy-start(f32[128]{0:T(128)} %param.13) | copy-start | bytes 1540
  186.7 11.7 %all-to-all-start.1 = ((f32[2,96,8,2]{1,3,0,2:T(2,128)}), f32[2,96,8,2]{1,3,0,2:T(2,128)S(1)}, u32[]{:S(2)}, u32[]{:S(2)}) async-start(f32[2,96,8,2]{1,3,0,2:T(2,128)} %copy.64), calls=%async_computation.1 | async-start | bytes 32768 | tf_op jit(solution)/shard_map/all_to_all | solution.py:156
  199.6 42.0 %copy-start.33 = (f32[128]{0:T(128)}, f32[128]{0:T(128)S(1)}, u32[]{:S(2)}) copy-start(f32[128]{0:T(128)S(1)} %fusion.304) | copy-start | bytes 1540
  201.4 28.2 %all-to-all-start.2 = ((f32[96,8,2]{1,2,0:T(2,128)}), f32[96,8,2]{1,2,0:T(2,128)S(1)}, u32[]{:S(2)}, u32[]{:S(2)}) async-start(f32[96,8,2]{1,2,0:T(2,128)} %copy.67), calls=%async_computation.2 | async-start | bytes 196608 | tf_op jit(solution)/shard_map/all_to_all | solution.py:171
  230.2 9.9 %all-to-all-start.3 = ((f32[96,8,2]{0,2,1:T(2,128)}), f32[96,8,2]{0,2,1:T(2,128)S(1)}, u32[]{:S(2)}, u32[]{:S(2)}) async-start(f32[96,8,2]{0,2,1:T(2,128)} %copy.68), calls=%async_computation.3 | async-start | bytes 16384 | tf_op jit(solution)/shard_map/all_to_all | solution.py:170
  (17 other events, 78.6 us)
where the time goes:
time: 243 us; the launch traced here: 242 us
  other arithmetic  120 us (49%)
  starting transfers between devices  59.5 us (24%)
  local copies, waits for them, and re-layouts  38.4 us (16%)
  waiting for transfers between devices  21.9 us (9%)
    scatter-add x1, other arithmetic, on_device(): jax.ops.segment_sum(momentum_x.reshape(-1), cell_patch.reshape(-1), num_s...  85.9 us
    unnamed x27, other arithmetic  20.1 us
    all_to_all x1, starting transfers between devices, on_device(): lax.all_to_all(outgoing, 'gx', split_axis=1, concat_axis=1, tiled=True)  16.8 us
    all_to_all x1, starting transfers between devices, on_device(): lax.all_to_all(answered, 'gx', split_axis=0, concat_axis=0, tiled=True)  14.6 us
    all_to_all x1, waiting for transfers between devices, on_device(): lax.all_to_all(answered, 'gx', split_axis=0, concat_axis=0, tiled=True)  12 us
    ppermute x2, starting transfers between devices, with_halo(): lax.ppermute(head, axis, [((i + 1) % count, i) for i in range(count)])  11.8 us
    gather x6, local copies, waits for them, and re-layouts, relax(): coupled = coupled + conductance[link] * old_pressure[neighbour[link]]  10.5 us
    unnamed x92, local copies, waits for them, and re-layouts  9.57 us
  transfers between devices with their start and end apart: 8, of which 3 were waited for; matrix products, arithmetic and copies ran while one was open for 14% of the time, Pallas kernels for 0%

commit v1 on v0

--- a/solution.py
+++ b/solution.py
@@ -130,52 +130,65 @@
     post_pad = widened[:19]
     new_populations = stream(post_pad, flag_pad, relaxed, populations, solid_flag)
     momentum_x = moment(new_populations, 0)
-    openings = patch_zone.shape[0]
-    sums = jax.ops.segment_sum(
-        momentum_x.reshape(-1), cell_patch.reshape(-1), num_segments=openings + 1
-    )
-    patch_flux = FACE_AREA * sums[:openings]
+    patch_flux = patch_sums(momentum_x, cell_patch, patch_zone.shape[0])
     zone_dev = old_pressure.shape[0]
     count_x = lax.axis_size("gx")
     count_y = lax.axis_size("gy")
-    devices = count_x * count_y
-    capacity = max(2, (2 * openings + devices - 1) // devices)
+    blocks = count_x * count_y
+    own_block = lax.axis_index("gx") * count_y + lax.axis_index("gy")
     owner_block = patch_zone // zone_dev
     local_zone = patch_zone - owner_block * zone_dev
-    patch_order = jnp.arange(openings, dtype=jnp.int32)
-    earlier_same = (owner_block[:, None] == owner_block[None, :]) & (
-        patch_order[:, None] > patch_order[None, :]
-    )
-    slot_rank = jnp.sum(earlier_same.astype(jnp.int32), axis=1)
-    slot_index = owner_block * capacity + slot_rank
-    targets = jnp.arange(devices * capacity, dtype=jnp.int32)
-    placed = slot_index[:, None] == targets[None, :]
-    send_flux = jnp.sum(jnp.where(placed, patch_flux[:, None], 0.0), axis=0)
-    send_zone = jnp.sum(jnp.where(placed, local_zone.astype(jnp.float32)[:, None], 0.0), axis=0)
-    outgoing = jnp.stack([send_flux, send_zone]).reshape(2, count_x, count_y, capacity)
-    arrived = lax.all_to_all(
-        lax.all_to_all(outgoing, "gx", split_axis=1, concat_axis=1, tiled=True),
-        "gy",
-        split_axis=2,
-        concat_axis=2,
-        tiled=True,
-    )
-    arrived = arrived.reshape(2, devices * capacity)
-    matched = arrived[1][None, :] == jnp.arange(zone_dev, dtype=jnp.float32)[:, None]
-    inflow = jnp.sum(jnp.where(matched, arrived[0][None, :], 0.0), axis=1)
-    zone_pressure = relax(inflow, old_pressure, leakage, conductance, neighbour)
-    answered = jnp.sum(jnp.where(matched, zone_pressure[:, None], 0.0), axis=0).reshape(
-        count_x, count_y, capacity
-    )
-    returned = lax.all_to_all(
-        lax.all_to_all(answered, "gx", split_axis=0, concat_axis=0, tiled=True),
-        "gy",
-        split_axis=1,
-        concat_axis=1,
-        tiled=True,
-    ).reshape(-1)
-    opening_pressure = jnp.sum(jnp.where(placed, returned[None, :], 0.0), axis=1)
+    in_block = owner_block[:, None] == jnp.arange(blocks, dtype=jnp.int32)[None, :]
+    at_zone = local_zone[:, None] == jnp.arange(zone_dev, dtype=jnp.int32)[None, :]
+    contributed = jnp.einsum(
+        "pb,pl->bl",
+        in_block.astype(jnp.float32),
+        jnp.where(at_zone, patch_flux[:, None], 0.0),
+        precision=lax.Precision.HIGHEST,
+    )
+    coupled, total = couple(old_pressure, leakage, conductance, neighbour)
+    is_own = (jnp.arange(blocks, dtype=jnp.int32) == own_block)[:, None]
+    numer = contributed + jnp.where(is_own, coupled[None, :], 0.0)
+    denom = jnp.where(is_own, total[None, :], 0.0)
+    summed = lax.psum(jnp.stack([numer, denom]), ("gx", "gy"))
+    pressure = summed[0] / summed[1]
+    zone_pressure = lax.dynamic_index_in_dim(pressure, own_block, axis=0, keepdims=False)
+    picked = jnp.einsum(
+        "pb,bl->pl", in_block.astype(jnp.float32), pressure, precision=lax.Precision.HIGHEST
+    )
+    opening_pressure = jnp.sum(jnp.where(at_zone, picked, 0.0), axis=1)
     return (new_populations, zone_pressure, opening_pressure)
+
+
+def patch_sums(momentum_x, cell_patch, openings):
+    depth, width_x, width_y = cell_patch.shape
+    rows = depth * width_x
+    momentum = momentum_x.reshape(rows, width_y)
+    patch = cell_patch.reshape(rows, width_y)
+    lanes = 128
+    high = patch // lanes
+    low = patch - high * lanes
+    groups = openings // lanes
+    picked = jnp.where(
+        high[None] == jnp.arange(groups, dtype=jnp.int32)[:, None, None], momentum[None], 0.0
+    )
+    onehot = (low[:, :, None] == jnp.arange(lanes, dtype=jnp.int32)[None, None, :]).astype(
+        jnp.float32
+    )
+    sums = jnp.einsum("hry,ryl->hl", picked, onehot, precision=lax.Precision.HIGHEST)
+    return FACE_AREA * sums.reshape(openings)
+
+
+def couple(old_pressure, leakage, conductance, neighbour):
+    zone_dev = old_pressure.shape[0]
+    chosen = neighbour[:, :, None] == jnp.arange(zone_dev, dtype=jnp.int32)[None, None, :]
+    neighbour_pressure = jnp.sum(jnp.where(chosen, old_pressure[None, None, :], 0.0), axis=2)
+    coupled = jnp.zeros_like(old_pressure)
+    total = leakage
+    for link in range(conductance.shape[0]):
+        coupled = coupled + conductance[link] * neighbour_pressure[link]
+        total = total + conductance[link]
+    return coupled, total
 
 
 def solution(mesh):

time: 243 us -> 548 us (2.26)
  waiting for transfers between devices: 21.9 us -> 454 us
  other arithmetic: 120 us -> 34.6 us
  starting transfers between devices: 59.5 us -> 19.6 us
  local copies, waits for them, and re-layouts: 38.4 us -> 16.3 us
  between operations: 1.36 us -> 14.6 us
  matrix products: 0 us -> 8.37 us
    psum x0 -> x1, waiting for transfers between devices: none -> 451 us  [on_device(): summed = lax.psum(jnp.stack([numer, denom]), ('gx', 'gy'))]
    scatter-add x1 -> x0, other arithmetic: 85.9 us -> none  [on_device(): jax.ops.segment_sum(momentum_x.reshape(-1), cell_patch.reshape(-1), num_s...]
    all_to_all x4 -> x0, starting transfers between devices: 39.8 us -> none  [the longest x1 16.8 us: on_device(): lax.all_to_all(outgoing, 'gx', split_axis=1, concat_axis=1, tiled=True)]
    all_to_all x4 -> x0, waiting for transfers between devices: 21.9 us -> none  [the longest x1 12 us: on_device(): lax.all_to_all(answered, 'gx', split_axis=0, concat_axis=0, tiled=True)]
    gather x6 -> x0, local copies, waits for them, and re-layouts: 10.5 us -> none  [relax(): coupled = coupled + conductance[link] * old_pressure[neighbour[link]]]
    dot_general x0 -> x3, matrix products: none -> 8.37 us  [the longest x1 5.62 us: patch_sums(): jnp.einsum('hry,ryl->hl', picked, onehot, precision=lax.Precision.HIGHEST)]
    another operation x3 -> x0, local copies, waits for them, and re-layouts: 6.55 us -> none  [on_device(): jnp.stack([send_flux, send_zone]).reshape(2, count_x, count_y, capacity)]
  transfers between devices with their start and end apart: 8 -> 5, of which waited for: 3 -> 2; matrix products, arithmetic and copies ran while one was open for 14% -> 5% of each run, Pallas kernels for 0% -> 0%
where the time goes in v1:
time: 548 us; the launch traced here: 547 us
  waiting for transfers between devices  454 us (83%)
  other arithmetic  34.6 us (6%)
  starting transfers between devices  19.6 us (4%)
  local copies, waits for them, and re-layouts  16.3 us (3%)
  between operations  14.6 us (3%)
  matrix products  8.37 us (2%)
    psum x1, waiting for transfers between devices, on_device(): summed = lax.psum(jnp.stack([numer, denom]), ('gx', 'gy'))  451 us
    unnamed x27, other arithmetic  23.3 us
    ppermute x2, starting transfers between devices, with_halo(): lax.ppermute(head, axis, [((i + 1) % count, i) for i in range(count)])  11.7 us
  transfers between devices with their start and end apart: 5, of which 2 were waited for; matrix products, arithmetic and copies ran while one was open for 5% of the time, Pallas kernels for 0%

profile of v1, /device:TPU:1, one launch (start us, length us, event | category | flops | bytes accessed | tf_op | source)
XLA Modules:
  0.0 547.0 jit_solution(7806958661622197196)
XLA Ops:
  7.3 1.4 constant_dynamic-update-slice_fusion.19
  14.5 0.8 constant_dynamic-update-slice_fusion.11
  15.3 0.8 constant_dynamic-update-slice_fusion.10
  18.2 4.5 collective-permute-start
  22.7 9.8 %collective-permute-start.1 = (f32[20,3,1,128]{3,2,1,0:T(1,128)S(1)}, f32[20,3,1,128]{3,2,1,0:T(1,128)S(1)}, u32[]{:S(2)}, u32[]{:S(2)}) collective-permute-start(f32[20,3,1,128]{3,2,1,0:T(1,128)S(1)} %get-tuple-element.32), channel_id=1, source_target_pairs={{8,0},{16,8},{24,16},{32,24},{40,32},{48,40},{56,48},{64,56},{72,6... | collective-permute-start | bytes 92168 | tf_op jit(solution)/shard_map/ppermute | solution.py:45
  34.8 0.9 broadcast_select_fusion
  37.1 1.4 fusion.332
  38.6 1.8 copy.39
  40.4 1.1 copy.40
  41.5 1.9 collective-permute-start.3
  43.4 3.4 collective-permute-start.2
  46.8 2.5 collective-permute-done.2
  49.8 1.6 copy.42
  51.5 3.0 select_maximum_fusion
  54.6 1.3 multiply_add_fusion
  55.9 5.6 %fusion.10 = f32[512]{0:T(512)S(1)} fusion(s32[96,128]{1,0:T(8,128)S(1)} %copy-done.24, f32[96,128]{1,0:T(8,128)S(1)} %bitcast.575, s32[96,128]{1,0:T(8,128)S(1)} %copy-done.23), kind=kOutput, calls=%fused_computation.20 | convolution fusion | flops 77169152 | bytes 149504 | tf_op jit(solution)/shard_map/hry,ryl->hl/dot_general | solution.py:178
  61.5 1.1 fusion.5
  62.7 0.9 pad_maximum_fusion.1
  63.7 1.6 constant_dynamic-update-slice_fusion.38
  65.3 1.4 constant_dynamic-update-slice_fusion.37
  66.7 1.4 constant_dynamic-update-slice_fusion.36
  68.1 1.5 constant_dynamic-update-slice_fusion.35
  69.6 1.6 constant_dynamic-update-slice_fusion.34
  71.3 1.6 constant_dynamic-update-slice_fusion.33
  72.9 1.6 constant_dynamic-update-slice_fusion.32
  79.5 1.5 constant_dynamic-update-slice_fusion.23
  81.0 1.6 constant_dynamic-update-slice_fusion.22
  82.6 1.5 constant_dynamic-update-slice_fusion.21
  84.1 1.6 constant_dynamic-update-slice_fusion.20
  85.8 451.1 %all-reduce.3.cloned.1.call-done = f32[2,768,128]{2,1,0:T(8,128)} async-done(((f32[2,768,128]{2,1,0:T(8,128)}), f32[2,768,128]{2,1,0:T(8,128)}) %all-reduce.3.cloned.1.call-update) | async-done | bytes 786448 | tf_op jit(solution)/shard_map/psum | solution.py:153
  536.8 1.2 slice_divide_fusion
  538.0 1.6 fusion.7
  (109 shorter events, 17.6 us)
Async XLA Ops:
  7.2 10.7 %copy-start = (f32[19,3,32,128]{3,2,1,0:T(8,128)S(1)}, f32[19,3,32,128]{3,2,1,0:T(8,128)}, u32[]{:S(2)}) copy-start(f32[19,3,32,128]{3,2,1,0:T(8,128)} %param.8) | copy-start | bytes 2801668
  7.2 10.9 %copy-start.12 = (s32[3,32,128]{2,1,0:T(8,128)S(1)}, s32[3,32,128]{2,1,0:T(8,128)}, u32[]{:S(2)}) copy-start(s32[3,32,128]{2,1,0:T(8,128)} %param.9) | copy-start | bytes 147460
  7.2 26.0 %copy-start.25 = (f32[6,128]{1,0:T(8,128)S(1)}, f32[6,128]{1,0:T(8,128)}, u32[]{:S(2)}) copy-start(f32[6,128]{1,0:T(8,128)} %param.14) | copy-start | bytes 9220
  7.2 26.0 %copy-start.31 = (f32[128]{0:T(128)S(1)}, f32[128]{0:T(128)}, u32[]{:S(2)}) copy-start(f32[128]{0:T(128)} %param.13) | copy-start | bytes 1540
  7.2 26.0 %copy-start.26 = (s32[6,128]{1,0:T(8,128)S(1)}, s32[6,128]{1,0:T(8,128)}, u32[]{:S(2)}) copy-start(s32[6,128]{1,0:T(8,128)} %param.15) | copy-start | bytes 9220
  7.2 26.0 %copy-start.30 = (f32[128]{0:T(128)S(1)}, f32[128]{0:T(128)}, u32[]{:S(2)}) copy-start(f32[128]{0:T(128)} %param.12) | copy-start | bytes 1540
  7.2 26.9 %copy-start.22 = (s32[3,32,128]{2,1,0:T(8,128)S(1)}, s32[3,32,128]{2,1,0:T(8,128)}, u32[]{:S(2)}) copy-start(s32[3,32,128]{2,1,0:T(8,128)} %param.10) | copy-start | bytes 147460
  7.2 28.5 %copy-start.27 = (s32[512]{0:T(512)S(1)}, s32[512]{0:T(512)}, u32[]{:S(2)}) copy-start(s32[512]{0:T(512)} %param.11) | copy-start | bytes 6148
  7.3 529.6 %all-reduce.3.cloned.1.call-start = ((), (), s32[]{:S(2)}) async-start(), calls=%async_computation | async-start | bytes 1572864 | tf_op jit(solution)/shard_map/psum | solution.py:153
  18.2 17.5 %collective-permute-start = (f32[20,3,1,128]{3,2,1,0:T(1,128)S(1)}, f32[20,3,1,128]{3,2,1,0:T(1,128)S(1)}, u32[]{:S(2)}, u32[]{:S(2)}) collective-permute-start(f32[20,3,1,128]{3,2,1,0:T(1,128)S(1)} %get-tuple-element.31), channel_id=1, source_target_pairs={{0,8},{8,16},{16,24},{24,32},{32,40},{40,48},{48,56},{56,64},{64,7... | collective-permute-start | bytes 92168 | tf_op jit(solution)/shard_map/ppermute | solution.py:43
  22.7 13.1 %collective-permute-start.1 = (f32[20,3,1,128]{3,2,1,0:T(1,128)S(1)}, f32[20,3,1,128]{3,2,1,0:T(1,128)S(1)}, u32[]{:S(2)}, u32[]{:S(2)}) collective-permute-start(f32[20,3,1,128]{3,2,1,0:T(1,128)S(1)} %get-tuple-element.32), channel_id=1, source_target_pairs={{8,0},{16,8},{24,16},{32,24},{40,32},{48,40},{56,48},{64,56},{72,6... | collective-permute-start | bytes 92168 | tf_op jit(solution)/shard_map/ppermute | solution.py:45
  41.5 8.3 %collective-permute-start.3 = (f32[20,3,34,1]{2,3,1,0:T(1,128)}, f32[20,3,34,1]{2,3,1,0:T(1,128)S(1)}, u32[]{:S(2)}, u32[]{:S(2)}) collective-permute-start(f32[20,3,34,1]{2,3,1,0:T(1,128)} %copy.40), channel_id=1, source_target_pairs={{1,0},{2,1},{3,2},{4,3},{5,4},{6,5},{7,6},{0,7},{9,8},{10,9},{11,1... | collective-permute-start | bytes 24488 | tf_op jit(solution)/shard_map/ppermute | solution.py:45
  43.4 5.8 %collective-permute-start.2 = (f32[20,3,34,1]{2,3,1,0:T(1,128)S(1)}, f32[20,3,34,1]{2,3,1,0:T(1,128)S(1)}, u32[]{:S(2)}, u32[]{:S(2)}) collective-permute-start(f32[20,3,34,1]{2,3,1,0:T(1,128)S(1)} %copy.39), channel_id=1, source_target_pairs={{0,1},{1,2},{2,3},{3,4},{4,5},{5,6},{6,7},{7,0},{8,9},{9,10},{10,1... | collective-permute-start | bytes 24488 | tf_op jit(solution)/shard_map/ppermute | solution.py:43
  51.4 3.1 copy-start.8
  51.4 3.1 copy-start.10
  51.4 3.1 copy-start.11
  51.4 3.1 copy-start.13
  54.4 7.1 %copy-start.2 = (f32[20,5,34,130]{3,2,1,0:T(8,128)}, f32[20,5,34,130]{3,2,1,0:T(8,128)S(1)}, u32[]{:S(2)}) copy-start(f32[20,5,34,130]{3,2,1,0:T(8,128)S(1)} %select_maximum_fusion) | copy-start | bytes 5304004
  54.5 7.0 %copy-start.29 = (pred[768]{0:T(1024)(128)(4,1)S(1)}, pred[768]{0:T(1024)(128)(4,1)}, u32[]{:S(2)}) copy-start(pred[768]{0:T(1024)(128)(4,1)} %copy-done.28) | copy-start | bytes 2308
  54.5 7.0 %copy-start.32 = (f32[128]{0:T(128)S(1)}, f32[128]{0:T(128)}, u32[]{:S(2)}) copy-start(f32[128]{0:T(128)} %add_bitcast_fusion) | copy-start | bytes 1540
  54.6 8.1 %copy-start.5 = (f32[1,768,128]{2,1,0:T(8,128)S(1)}, f32[1,768,128]{2,1,0:T(8,128)}, u32[]{:S(2)}) copy-start(f32[1,768,128]{2,1,0:T(8,128)} %broadcast_select_fusion) | copy-start | bytes 1179652
  63.6 7.6 %copy-start.3 = (f32[3,32,128]{2,1,0:T(8,128)S(1)}, f32[3,32,128]{2,1,0:T(8,128)}, u32[]{:S(2)}) copy-start(f32[3,32,128]{2,1,0:T(8,128)} %get-tuple-element.19) | copy-start | bytes 147460
  63.6 7.6 %copy-start.6 = (pred[3,32,128]{2,1,0:T(8,128)(4,1)S(1)}, pred[3,32,128]{2,1,0:T(8,128)(4,1)}, u32[]{:S(2)}) copy-start(pred[3,32,128]{2,1,0:T(8,128)(4,1)} %get-tuple-element.20) | copy-start | bytes 36868
  63.6 10.9 %copy-start.21 = (f32[3,32,128]{2,1,0:T(8,128)S(1)}, f32[3,32,128]{2,1,0:T(8,128)}, u32[]{:S(2)}) copy-start(f32[3,32,128]{2,1,0:T(8,128)} %get-tuple-element.14) | copy-start | bytes 147460
  63.6 11.5 %copy-start.20 = (f32[3,32,128]{2,1,0:T(8,128)S(1)}, f32[3,32,128]{2,1,0:T(8,128)}, u32[]{:S(2)}) copy-start(f32[3,32,128]{2,1,0:T(8,128)} %get-tuple-element.13) | copy-start | bytes 147460
  63.7 12.1 %copy-start.19 = (f32[3,32,128]{2,1,0:T(8,128)S(1)}, f32[3,32,128]{2,1,0:T(8,128)}, u32[]{:S(2)}) copy-start(f32[3,32,128]{2,1,0:T(8,128)} %get-tuple-element.12) | copy-start | bytes 147460
  63.7 12.7 %copy-start.18 = (f32[3,32,128]{2,1,0:T(8,128)S(1)}, f32[3,32,128]{2,1,0:T(8,128)}, u32[]{:S(2)}) copy-start(f32[3,32,128]{2,1,0:T(8,128)} %get-tuple-element.11) | copy-start | bytes 147460
  63.7 13.3 %copy-start.17 = (f32[3,32,128]{2,1,0:T(8,128)S(1)}, f32[3,32,128]{2,1,0:T(8,128)}, u32[]{:S(2)}) copy-start(f32[3,32,128]{2,1,0:T(8,128)} %get-tuple-element.10) | copy-start | bytes 147460
  63.7 14.0 %copy-start.16 = (f32[3,32,128]{2,1,0:T(8,128)S(1)}, f32[3,32,128]{2,1,0:T(8,128)}, u32[]{:S(2)}) copy-start(f32[3,32,128]{2,1,0:T(8,128)} %get-tuple-element.9) | copy-start | bytes 147460
  63.7 14.6 %copy-start.15 = (f32[3,32,128]{2,1,0:T(8,128)S(1)}, f32[3,32,128]{2,1,0:T(8,128)}, u32[]{:S(2)}) copy-start(f32[3,32,128]{2,1,0:T(8,128)} %get-tuple-element.8) | copy-start | bytes 147460
  63.7 15.2 %copy-start.14 = (f32[3,32,128]{2,1,0:T(8,128)S(1)}, f32[3,32,128]{2,1,0:T(8,128)}, u32[]{:S(2)}) copy-start(f32[3,32,128]{2,1,0:T(8,128)} %get-tuple-element.7) | copy-start | bytes 147460
  63.7 15.8 %copy-start.4 = (f32[3,32,128]{2,1,0:T(8,128)S(1)}, f32[3,32,128]{2,1,0:T(8,128)}, u32[]{:S(2)}) copy-start(f32[3,32,128]{2,1,0:T(8,128)} %get-tuple-element.18) | copy-start | bytes 147460
  (6 other events, 9.6 us)
Sparse Core Ops, SparseCore 0:
  63.7 473.0 all-reduce.2

commit v2 on v1

--- a/solution.py
+++ b/solution.py
@@ -132,31 +132,36 @@
     momentum_x = moment(new_populations, 0)
     patch_flux = patch_sums(momentum_x, cell_patch, patch_zone.shape[0])
     zone_dev = old_pressure.shape[0]
-    count_x = lax.axis_size("gx")
-    count_y = lax.axis_size("gy")
-    blocks = count_x * count_y
-    own_block = lax.axis_index("gx") * count_y + lax.axis_index("gy")
+    openings = patch_zone.shape[0]
+    devices = lax.axis_size("gx") * lax.axis_size("gy")
+    capacity = max(2, (2 * openings + devices - 1) // devices)
     owner_block = patch_zone // zone_dev
     local_zone = patch_zone - owner_block * zone_dev
-    in_block = owner_block[:, None] == jnp.arange(blocks, dtype=jnp.int32)[None, :]
-    at_zone = local_zone[:, None] == jnp.arange(zone_dev, dtype=jnp.int32)[None, :]
-    contributed = jnp.einsum(
-        "pb,pl->bl",
-        in_block.astype(jnp.float32),
-        jnp.where(at_zone, patch_flux[:, None], 0.0),
-        precision=lax.Precision.HIGHEST,
-    )
+    patch_order = jnp.arange(openings, dtype=jnp.int32)
+    earlier_same = (owner_block[:, None] == owner_block[None, :]) & (
+        patch_order[:, None] > patch_order[None, :]
+    )
+    slot_rank = jnp.sum(earlier_same.astype(jnp.int32), axis=1)
+    slot_index = owner_block * capacity + slot_rank
+    targets = jnp.arange(devices * capacity, dtype=jnp.int32)
+    placed = slot_index[:, None] == targets[None, :]
+    send_flux = jnp.sum(jnp.where(placed, patch_flux[:, None], 0.0), axis=0)
+    send_zone = jnp.sum(jnp.where(placed, local_zone.astype(jnp.float32)[:, None], 0.0), axis=0)
+    outgoing = jnp.stack([send_flux, send_zone]).reshape(2, devices, capacity)
+    arrived = lax.all_to_all(
+        outgoing, ("gx", "gy"), split_axis=1, concat_axis=1, tiled=True
+    ).reshape(2, devices * capacity)
+    matched = arrived[1][None, :] == jnp.arange(zone_dev, dtype=jnp.float32)[:, None]
+    inflow = jnp.sum(jnp.where(matched, arrived[0][None, :], 0.0), axis=1)
     coupled, total = couple(old_pressure, leakage, conductance, neighbour)
-    is_own = (jnp.arange(blocks, dtype=jnp.int32) == own_block)[:, None]
-    numer = contributed + jnp.where(is_own, coupled[None, :], 0.0)
-    denom = jnp.where(is_own, total[None, :], 0.0)
-    summed = lax.psum(jnp.stack([numer, denom]), ("gx", "gy"))
-    pressure = summed[0] / summed[1]
-    zone_pressure = lax.dynamic_index_in_dim(pressure, own_block, axis=0, keepdims=False)
-    picked = jnp.einsum(
-        "pb,bl->pl", in_block.astype(jnp.float32), pressure, precision=lax.Precision.HIGHEST
-    )
-    opening_pressure = jnp.sum(jnp.where(at_zone, picked, 0.0), axis=1)
+    zone_pressure = (inflow + coupled) / total
+    answered = jnp.sum(jnp.where(matched, zone_pressure[:, None], 0.0), axis=0).reshape(
+        devices, capacity
+    )
+    returned = lax.all_to_all(
+        answered, ("gx", "gy"), split_axis=0, concat_axis=0, tiled=True
+    ).reshape(-1)
+    opening_pressure = jnp.sum(jnp.where(placed, returned[None, :], 0.0), axis=1)
     return (new_populations, zone_pressure, opening_pressure)
 
 

time: 548 us -> 177 us (0.32)
  waiting for transfers between devices: 454 us -> 41.7 us
  starting transfers between devices: 19.6 us -> 65.5 us
  between operations: 14.6 us -> 1.18 us
  local copies, waits for them, and re-layouts: 16.3 us -> 26.4 us
    psum x1 -> x0, waiting for transfers between devices: 451 us -> none  [on_device(): summed = lax.psum(jnp.stack([numer, denom]), ('gx', 'gy'))]
    all_to_all x0 -> x2, starting transfers between devices: none -> 45.9 us  [the longest x1 29.7 us: on_device(): lax.all_to_all(outgoing, ('gx', 'gy'), split_axis=1, concat_axis=1, tiled...]
    all_to_all x0 -> x2, waiting for transfers between devices: none -> 39.2 us  [the longest x1 23.9 us: on_device(): lax.all_to_all(answered, ('gx', 'gy'), split_axis=0, concat_axis=0, tiled...]
  transfers between devices with their start and end apart: 5 -> 6, of which waited for: 2 -> 3; matrix products, arithmetic and copies ran while one was open for 5% -> 14% of each run, Pallas kernels for 0% -> 0%
where the time goes in v2:
time: 177 us; the launch traced here: 176 us
  starting transfers between devices  65.5 us (37%)
  waiting for transfers between devices  41.7 us (24%)
  other arithmetic  35.9 us (20%)
  local copies, waits for them, and re-layouts  26.4 us (15%)
  matrix products  5.54 us (3%)
    all_to_all x1, starting transfers between devices, on_device(): lax.all_to_all(outgoing, ('gx', 'gy'), split_axis=1, concat_axis=1, tiled...  29.7 us
    all_to_all x1, waiting for transfers between devices, on_device(): lax.all_to_all(answered, ('gx', 'gy'), split_axis=0, concat_axis=0, tiled...  23.9 us
    unnamed x27, other arithmetic  20.1 us
    all_to_all x1, starting transfers between devices, on_device(): lax.all_to_all(answered, ('gx', 'gy'), split_axis=0, concat_axis=0, tiled...  16.3 us
    all_to_all x1, waiting for transfers between devices, on_device(): lax.all_to_all(outgoing, ('gx', 'gy'), split_axis=1, concat_axis=1, tiled...  15.3 us
    ppermute x2, starting transfers between devices, with_halo(): lax.ppermute(head, axis, [((i + 1) % count, i) for i in range(count)])  11.7 us
    unnamed x90, local copies, waits for them, and re-layouts  9.48 us
    ppermute x2, starting transfers between devices, with_halo(): lax.ppermute(tail, axis, [(i, (i + 1) % count) for i in range(count)])  7.86 us
  transfers between devices with their start and end apart: 6, of which 3 were waited for; matrix products, arithmetic and copies ran while one was open for 14% of the time, Pallas kernels for 0%

profile of v2, /device:TPU:1, one launch (start us, length us, event | category | flops | bytes accessed | tf_op | source)
XLA Modules:
  0.0 176.2 jit_solution(8151255488674843836)
XLA Ops:
  0.7 1.4 constant_dynamic-update-slice_fusion.19
  9.2 4.5 %collective-permute-start = (f32[20,3,1,128]{3,2,1,0:T(1,128)S(1)}, f32[20,3,1,128]{3,2,1,0:T(1,128)S(1)}, u32[]{:S(2)}, u32[]{:S(2)}) collective-permute-start(f32[20,3,1,128]{3,2,1,0:T(1,128)S(1)} %get-tuple-element.37), channel_id=1, source_target_pairs={{0,8},{8,16},{16,24},{24,32},{32,40},{40,48},{48,56},{56,64},{64,7... | collective-permute-start | bytes 92168 | tf_op jit(solution)/shard_map/ppermute | solution.py:43
  13.7 9.8 %collective-permute-start.1 = (f32[20,3,1,128]{3,2,1,0:T(1,128)S(1)}, f32[20,3,1,128]{3,2,1,0:T(1,128)S(1)}, u32[]{:S(2)}, u32[]{:S(2)}) collective-permute-start(f32[20,3,1,128]{3,2,1,0:T(1,128)S(1)} %get-tuple-element.38), channel_id=1, source_target_pairs={{8,0},{16,8},{24,16},{32,24},{40,32},{48,40},{56,48},{64,56},{72,6... | collective-permute-start | bytes 92168 | tf_op jit(solution)/shard_map/ppermute | solution.py:45
  28.7 1.4 fusion.326
  30.1 1.8 %copy.47 = f32[20,3,34,1]{2,3,1,0:T(1,128)S(1)} copy(f32[20,3,34,1]{3,2,1,0:T(8,128)} %get-tuple-element.35) | data formatting | bytes 16320 | tf_op jit(solution)/shard_map/slice | solution.py:40
  33.0 1.9 %collective-permute-start.3 = (f32[20,3,34,1]{2,3,1,0:T(1,128)}, f32[20,3,34,1]{2,3,1,0:T(1,128)S(1)}, u32[]{:S(2)}, u32[]{:S(2)}) collective-permute-start(f32[20,3,34,1]{2,3,1,0:T(1,128)} %copy.48), channel_id=1, source_target_pairs={{1,0},{2,1},{3,2},{4,3},{5,4},{6,5},{7,6},{0,7},{9,8},{10,9},{11,1... | collective-permute-start | bytes 24488 | tf_op jit(solution)/shard_map/ppermute | solution.py:45
  35.0 3.4 %collective-permute-start.2 = (f32[20,3,34,1]{2,3,1,0:T(1,128)S(1)}, f32[20,3,34,1]{2,3,1,0:T(1,128)S(1)}, u32[]{:S(2)}, u32[]{:S(2)}) collective-permute-start(f32[20,3,34,1]{2,3,1,0:T(1,128)S(1)} %copy.47), channel_id=1, source_target_pairs={{0,1},{1,2},{2,3},{3,4},{4,5},{5,6},{6,7},{7,0},{8,9},{9,10},{10,1... | collective-permute-start | bytes 24488 | tf_op jit(solution)/shard_map/ppermute | solution.py:43
  38.3 2.5 %collective-permute-done.2 = f32[20,3,34,1]{2,3,1,0:T(1,128)S(1)} collective-permute-done((f32[20,3,34,1]{2,3,1,0:T(1,128)S(1)}, f32[20,3,34,1]{2,3,1,0:T(1,128)S(1)}, u32[]{:S(2)}, u32[]{:S(2)}) %collective-permute-start.2) | collective-permute-done | bytes 8192 | tf_op jit(solution)/shard_map/ppermute | solution.py:43
  41.4 1.6 copy.50
  43.0 3.0 %select_maximum_fusion = f32[20,5,34,130]{3,2,1,0:T(8,128)S(1)} fusion(f32[20,3,34,1]{3,2,1,0:T(8,128)} %copy.50, f32[20,3,34,1]{3,2,1,0:T(8,128)S(1)} %copy.49, f32[20,3,1,128]{3,2,1,0:T(1,128)} %copy-done.13, f32[20,3,32,128]{3,2,1,0:T(8,128)S(1)} %constant_dynamic-update-slice_fusion, f32[20,3,1,128]{3,2,1,0:T(1,128)} %copy-done.10), kind=kLoop, calls=%fused_computation.4 | loop fusion | flops 5304000 | bytes 2828800 | tf_op jit(solution)/shard_map/concatenate | solution.py:41
  46.1 1.7 multiply_add_fusion
  48.1 5.5 %fusion.5 = f32[512]{0:T(512)S(1)} fusion(s32[96,128]{1,0:T(8,128)S(1)} %copy-done.29, f32[96,128]{1,0:T(8,128)S(1)} %bitcast.611, s32[96,128]{1,0:T(8,128)S(1)} %copy-done.28), kind=kOutput, calls=%fused_computation.17 | convolution fusion | flops 77169152 | bytes 149504 | tf_op jit(solution)/shard_map/hry,ryl->hl/dot_general | solution.py:183
  53.6 1.4 select_reduce_fusion.2
  55.0 1.8 %stack.108 = f32[1,768,2]{2,1,0:T(8,128)} reshape(f32[1536]{0:T(1024)} %get-tuple-element.8) | data formatting | bytes 12288 | tf_op jit(solution)/shard_map/stack | solution.py:150
  57.9 1.2 pad_maximum_fusion.1
  59.0 1.5 copy.53
  60.6 29.7 %all-to-all-start = ((f32[2,768,2]{2,0,1:T(2,128)}), f32[2,768,2]{2,0,1:T(2,128)}, u32[]{:S(2)}, u32[]{:S(2)}) async-start(f32[2,768,2]{2,0,1:T(2,128)} %copy.53), calls=%async_computation | async-start | bytes 1572864 | tf_op jit(solution)/shard_map/all_to_all | solution.py:151
  90.3 1.5 constant_dynamic-update-slice_fusion.38
  91.8 1.4 constant_dynamic-update-slice_fusion.37
  93.2 1.4 constant_dynamic-update-slice_fusion.36
  94.7 1.6 constant_dynamic-update-slice_fusion.35
  97.1 1.6 constant_dynamic-update-slice_fusion.33
  98.7 1.6 constant_dynamic-update-slice_fusion.32
  105.4 1.5 constant_dynamic-update-slice_fusion.23
  106.9 1.6 constant_dynamic-update-slice_fusion.22
  108.5 1.5 constant_dynamic-update-slice_fusion.21
  110.0 15.3 %all-to-all-done = f32[2,768,2]{2,0,1:T(2,128)} async-done(((f32[2,768,2]{2,0,1:T(2,128)}), f32[2,768,2]{2,0,1:T(2,128)}, u32[]{:S(2)}, u32[]{:S(2)}) %all-to-all-start) | async-done | bytes 12320 | tf_op jit(solution)/shard_map/all_to_all | solution.py:151
  125.3 3.7 %slice_reduce_fusion.1 = (f32[768,2]{1,0:T(8,128)S(1)}, f32[768,2]{1,0:T(8,128)S(1)}) fusion(f32[2,768,2]{2,0,1:T(2,128)} %all-to-all-done), kind=kLoop, calls=%fused_computation.26 | loop fusion | bytes 24576 | tf_op jit(solution)/shard_map/slice | solution.py:154
  130.9 16.3 %all-to-all-start.1 = ((f32[768,1,2]{2,1,0:T(1,128)}), f32[768,1,2]{2,1,0:T(1,128)S(1)}, u32[]{:S(2)}, u32[]{:S(2)}) async-start(f32[768,1,2]{2,1,0:T(1,128)} %bitcast.75), calls=%async_computation.1 | async-start | bytes 786432 | tf_op jit(solution)/shard_map/all_to_all | solution.py:161
  147.2 1.6 constant_dynamic-update-slice_fusion.20
  148.9 23.9 %all-to-all-done.1 = f32[768,1,2]{2,1,0:T(1,128)S(1)} async-done(((f32[768,1,2]{2,1,0:T(1,128)}), f32[768,1,2]{2,1,0:T(1,128)S(1)}, u32[]{:S(2)}, u32[]{:S(2)}) %all-to-all-start.1) | async-done | bytes 6176 | tf_op jit(solution)/shard_map/all_to_all | solution.py:161
  173.3 1.6 reduce.11
  (133 shorter events, 24.8 us)
Async XLA Ops:
  0.6 8.1 %copy-start = (f32[19,3,32,128]{3,2,1,0:T(8,128)S(1)}, f32[19,3,32,128]{3,2,1,0:T(8,128)}, u32[]{:S(2)}) copy-start(f32[19,3,32,128]{3,2,1,0:T(8,128)} %param.8) | copy-start | bytes 2801668
  0.6 8.5 %copy-start.17 = (s32[3,32,128]{2,1,0:T(8,128)S(1)}, s32[3,32,128]{2,1,0:T(8,128)}, u32[]{:S(2)}) copy-start(s32[3,32,128]{2,1,0:T(8,128)} %param.9) | copy-start | bytes 147460
  2.0 22.2 %copy-start.36 = (s32[512]{0:T(512)S(1)}, s32[512]{0:T(512)}, u32[]{:S(2)}) copy-start(s32[512]{0:T(512)} %param.11) | copy-start | bytes 6148
  2.1 23.6 %copy-start.27 = (s32[3,32,128]{2,1,0:T(8,128)S(1)}, s32[3,32,128]{2,1,0:T(8,128)}, u32[]{:S(2)}) copy-start(s32[3,32,128]{2,1,0:T(8,128)} %param.10) | copy-start | bytes 147460
  2.9 23.5 %copy-start.34 = (s32[6,128]{1,0:T(8,128)S(1)}, s32[6,128]{1,0:T(8,128)}, u32[]{:S(2)}) copy-start(s32[6,128]{1,0:T(8,128)} %param.15) | copy-start | bytes 9220
  2.9 23.5 %copy-start.38 = (f32[128]{0:T(128)S(1)}, f32[128]{0:T(128)}, u32[]{:S(2)}) copy-start(f32[128]{0:T(128)} %param.12) | copy-start | bytes 1540
  9.2 18.1 %collective-permute-start = (f32[20,3,1,128]{3,2,1,0:T(1,128)S(1)}, f32[20,3,1,128]{3,2,1,0:T(1,128)S(1)}, u32[]{:S(2)}, u32[]{:S(2)}) collective-permute-start(f32[20,3,1,128]{3,2,1,0:T(1,128)S(1)} %get-tuple-element.37), channel_id=1, source_target_pairs={{0,8},{8,16},{16,24},{24,32},{32,40},{40,48},{48,56},{56,64},{64,7... | collective-permute-start | bytes 92168 | tf_op jit(solution)/shard_map/ppermute | solution.py:43
  13.7 13.6 %collective-permute-start.1 = (f32[20,3,1,128]{3,2,1,0:T(1,128)S(1)}, f32[20,3,1,128]{3,2,1,0:T(1,128)S(1)}, u32[]{:S(2)}, u32[]{:S(2)}) collective-permute-start(f32[20,3,1,128]{3,2,1,0:T(1,128)S(1)} %get-tuple-element.38), channel_id=1, source_target_pairs={{8,0},{16,8},{24,16},{32,24},{40,32},{48,40},{56,48},{64,56},{72,6... | collective-permute-start | bytes 92168 | tf_op jit(solution)/shard_map/ppermute | solution.py:45
  33.0 8.3 %collective-permute-start.3 = (f32[20,3,34,1]{2,3,1,0:T(1,128)}, f32[20,3,34,1]{2,3,1,0:T(1,128)S(1)}, u32[]{:S(2)}, u32[]{:S(2)}) collective-permute-start(f32[20,3,34,1]{2,3,1,0:T(1,128)} %copy.48), channel_id=1, source_target_pairs={{1,0},{2,1},{3,2},{4,3},{5,4},{6,5},{7,6},{0,7},{9,8},{10,9},{11,1... | collective-permute-start | bytes 24488 | tf_op jit(solution)/shard_map/ppermute | solution.py:45
  35.0 5.8 %collective-permute-start.2 = (f32[20,3,34,1]{2,3,1,0:T(1,128)S(1)}, f32[20,3,34,1]{2,3,1,0:T(1,128)S(1)}, u32[]{:S(2)}, u32[]{:S(2)}) collective-permute-start(f32[20,3,34,1]{2,3,1,0:T(1,128)S(1)} %copy.47), channel_id=1, source_target_pairs={{0,1},{1,2},{2,3},{3,4},{4,5},{5,6},{6,7},{7,0},{8,9},{9,10},{10,1... | collective-permute-start | bytes 24488 | tf_op jit(solution)/shard_map/ppermute | solution.py:43
  46.1 7.5 %copy-start.30 = (s32[512]{0:T(512)S(1)}, s32[512]{0:T(512)}, u32[]{:S(2)}) copy-start(s32[512]{0:T(512)} %multiply_add_fusion.1) | copy-start | bytes 6148
  46.1 7.5 %copy-start.33 = (f32[512]{0:T(512)S(1)}, f32[512]{0:T(512)}, u32[]{:S(2)}) copy-start(f32[512]{0:T(512)} %get-tuple-element.10) | copy-start | bytes 6148
  60.6 64.7 %all-to-all-start = ((f32[2,768,2]{2,0,1:T(2,128)}), f32[2,768,2]{2,0,1:T(2,128)}, u32[]{:S(2)}, u32[]{:S(2)}) async-start(f32[2,768,2]{2,0,1:T(2,128)} %copy.53), calls=%async_computation | async-start | bytes 1572864 | tf_op jit(solution)/shard_map/all_to_all | solution.py:151
  90.2 6.0 %copy-start.2 = (f32[20,3,34,1]{3,2,1,0:T(8,128)S(1)}, f32[20,3,34,1]{3,2,1,0:T(8,128)}, u32[]{:S(2)}) copy-start(f32[20,3,34,1]{3,2,1,0:T(8,128)} %copy.50) | copy-start | bytes 24484
  90.3 6.8 %copy-start.4 = (f32[3,32,128]{2,1,0:T(8,128)S(1)}, f32[3,32,128]{2,1,0:T(8,128)}, u32[]{:S(2)}) copy-start(f32[3,32,128]{2,1,0:T(8,128)} %get-tuple-element.25) | copy-start | bytes 147460
  91.8 8.6 %copy-start.26 = (f32[3,32,128]{2,1,0:T(8,128)S(1)}, f32[3,32,128]{2,1,0:T(8,128)}, u32[]{:S(2)}) copy-start(f32[3,32,128]{2,1,0:T(8,128)} %get-tuple-element.20) | copy-start | bytes 147460
  93.2 7.7 %copy-start.25 = (f32[3,32,128]{2,1,0:T(8,128)S(1)}, f32[3,32,128]{2,1,0:T(8,128)}, u32[]{:S(2)}) copy-start(f32[3,32,128]{2,1,0:T(8,128)} %get-tuple-element.19) | copy-start | bytes 147460
  94.7 6.9 %copy-start.24 = (f32[3,32,128]{2,1,0:T(8,128)S(1)}, f32[3,32,128]{2,1,0:T(8,128)}, u32[]{:S(2)}) copy-start(f32[3,32,128]{2,1,0:T(8,128)} %get-tuple-element.18) | copy-start | bytes 147460
  94.7 7.6 %copy-start.23 = (f32[3,32,128]{2,1,0:T(8,128)S(1)}, f32[3,32,128]{2,1,0:T(8,128)}, u32[]{:S(2)}) copy-start(f32[3,32,128]{2,1,0:T(8,128)} %get-tuple-element.17) | copy-start | bytes 147460
  94.7 8.2 %copy-start.22 = (f32[3,32,128]{2,1,0:T(8,128)S(1)}, f32[3,32,128]{2,1,0:T(8,128)}, u32[]{:S(2)}) copy-start(f32[3,32,128]{2,1,0:T(8,128)} %get-tuple-element.16) | copy-start | bytes 147460
  94.7 8.8 %copy-start.21 = (f32[3,32,128]{2,1,0:T(8,128)S(1)}, f32[3,32,128]{2,1,0:T(8,128)}, u32[]{:S(2)}) copy-start(f32[3,32,128]{2,1,0:T(8,128)} %get-tuple-element.15) | copy-start | bytes 147460
  94.7 9.4 %copy-start.20 = (f32[3,32,128]{2,1,0:T(8,128)S(1)}, f32[3,32,128]{2,1,0:T(8,128)}, u32[]{:S(2)}) copy-start(f32[3,32,128]{2,1,0:T(8,128)} %get-tuple-element.14) | copy-start | bytes 147460
  94.7 10.1 %copy-start.19 = (f32[3,32,128]{2,1,0:T(8,128)S(1)}, f32[3,32,128]{2,1,0:T(8,128)}, u32[]{:S(2)}) copy-start(f32[3,32,128]{2,1,0:T(8,128)} %get-tuple-element.13) | copy-start | bytes 147460
  97.1 32.6 %copy-start.32 = (f32[6,128]{1,0:T(8,128)S(1)}, f32[6,128]{1,0:T(8,128)}, u32[]{:S(2)}) copy-start(f32[6,128]{1,0:T(8,128)} %select_reduce_fusion.5) | copy-start | bytes 9220
  97.1 32.6 %copy-start.35 = (f32[6,128]{1,0:T(8,128)S(1)}, f32[6,128]{1,0:T(8,128)}, u32[]{:S(2)}) copy-start(f32[6,128]{1,0:T(8,128)} %param.14) | copy-start | bytes 9220
  97.1 32.6 %copy-start.39 = (f32[128]{0:T(128)S(1)}, f32[128]{0:T(128)}, u32[]{:S(2)}) copy-start(f32[128]{0:T(128)} %param.13) | copy-start | bytes 1540
  98.7 48.5 %copy-start.5 = (f32[3,32,128]{2,1,0:T(8,128)S(1)}, f32[3,32,128]{2,1,0:T(8,128)}, u32[]{:S(2)}) copy-start(f32[3,32,128]{2,1,0:T(8,128)} %get-tuple-element.25) | copy-start | bytes 147460
  98.7 48.5 %copy-start.7 = (f32[3,32,128]{2,1,0:T(8,128)S(1)}, f32[3,32,128]{2,1,0:T(8,128)}, u32[]{:S(2)}) copy-start(f32[3,32,128]{2,1,0:T(8,128)} %get-tuple-element.24) | copy-start | bytes 147460
  98.7 48.5 %copy-start.9 = (pred[3,32,128]{2,1,0:T(8,128)(4,1)S(1)}, pred[3,32,128]{2,1,0:T(8,128)(4,1)}, u32[]{:S(2)}) copy-start(pred[3,32,128]{2,1,0:T(8,128)(4,1)} %get-tuple-element.26) | copy-start | bytes 36868
  106.9 68.3 %copy-start.31 = (s32[512]{0:T(512)S(1)}, s32[512]{0:T(512)}, u32[]{:S(2)}) copy-start(s32[512]{0:T(512)} %multiply_add_fusion.1) | copy-start | bytes 6148
  129.7 46.5 %copy-start.37 = (f32[128]{0:T(128)}, f32[128]{0:T(128)S(1)}, u32[]{:S(2)}) copy-start(f32[128]{0:T(128)S(1)} %fusion.308) | copy-start | bytes 1540
  130.9 41.8 %all-to-all-start.1 = ((f32[768,1,2]{2,1,0:T(1,128)}), f32[768,1,2]{2,1,0:T(1,128)S(1)}, u32[]{:S(2)}, u32[]{:S(2)}) async-start(f32[768,1,2]{2,1,0:T(1,128)} %bitcast.75), calls=%async_computation.1 | async-start | bytes 786432 | tf_op jit(solution)/shard_map/all_to_all | solution.py:161
  (14 other events, 47.0 us)

commit v3 on v2

--- a/solution.py
+++ b/solution.py
@@ -147,19 +147,29 @@
     placed = slot_index[:, None] == targets[None, :]
     send_flux = jnp.sum(jnp.where(placed, patch_flux[:, None], 0.0), axis=0)
     send_zone = jnp.sum(jnp.where(placed, local_zone.astype(jnp.float32)[:, None], 0.0), axis=0)
-    outgoing = jnp.stack([send_flux, send_zone]).reshape(2, devices, capacity)
+    count_x = lax.axis_size("gx")
+    count_y = lax.axis_size("gy")
+    outgoing = jnp.stack([send_flux, send_zone]).reshape(2, count_x, count_y, capacity)
     arrived = lax.all_to_all(
-        outgoing, ("gx", "gy"), split_axis=1, concat_axis=1, tiled=True
+        lax.all_to_all(outgoing, "gx", split_axis=1, concat_axis=1, tiled=True),
+        "gy",
+        split_axis=2,
+        concat_axis=2,
+        tiled=True,
     ).reshape(2, devices * capacity)
     matched = arrived[1][None, :] == jnp.arange(zone_dev, dtype=jnp.float32)[:, None]
     inflow = jnp.sum(jnp.where(matched, arrived[0][None, :], 0.0), axis=1)
     coupled, total = couple(old_pressure, leakage, conductance, neighbour)
     zone_pressure = (inflow + coupled) / total
     answered = jnp.sum(jnp.where(matched, zone_pressure[:, None], 0.0), axis=0).reshape(
-        devices, capacity
+        count_x, count_y, capacity
     )
     returned = lax.all_to_all(
-        answered, ("gx", "gy"), split_axis=0, concat_axis=0, tiled=True
+        lax.all_to_all(answered, "gx", split_axis=0, concat_axis=0, tiled=True),
+        "gy",
+        split_axis=1,
+        concat_axis=1,
+        tiled=True,
     ).reshape(-1)
     opening_pressure = jnp.sum(jnp.where(placed, returned[None, :], 0.0), axis=1)
     return (new_populations, zone_pressure, opening_pressure)

time: 177 us -> 152 us (0.86)
  waiting for transfers between devices: 41.7 us -> 24.4 us
  starting transfers between devices: 65.5 us -> 57.5 us
    all_to_all x2 -> x4, waiting for transfers between devices: 39.2 us -> 21.9 us  [the longest x1 12 us: on_device(): lax.all_to_all(answered, 'gx', split_axis=0, concat_axis=0, tiled=True)]
    all_to_all x2 -> x4, starting transfers between devices: 45.9 us -> 37.9 us  [the longest x1 16.2 us: on_device(): lax.all_to_all(outgoing, 'gx', split_axis=1, concat_axis=1, tiled=True)]
    slice x1 -> x2, local copies, waits for them, and re-layouts: 3.69 us -> 0.23 us  [on_device(): arrived[1][None, :] == jnp.arange(zone_dev, dtype=jnp.float32)[:, None]]
  transfers between devices with their start and end apart: 6 -> 8, of which waited for: 3 -> 4; matrix products, arithmetic and copies ran while one was open for 14% -> 17% of each run, Pallas kernels for 0% -> 0%
where the time goes in v3:
time: 152 us; the launch traced here: 151 us
  starting transfers between devices  57.5 us (38%)
  other arithmetic  35.2 us (23%)
  local copies, waits for them, and re-layouts  27.2 us (18%)
  waiting for transfers between devices  24.4 us (16%)
  matrix products  5.54 us (4%)
    unnamed x27, other arithmetic  20.1 us
    all_to_all x1, starting transfers between devices, on_device(): lax.all_to_all(outgoing, 'gx', split_axis=1, concat_axis=1, tiled=True)  16.2 us
    all_to_all x1, starting transfers between devices, on_device(): lax.all_to_all(answered, 'gx', split_axis=0, concat_axis=0, tiled=True)  14.6 us
    all_to_all x1, waiting for transfers between devices, on_device(): lax.all_to_all(answered, 'gx', split_axis=0, concat_axis=0, tiled=True)  12 us
    ppermute x2, starting transfers between devices, with_halo(): lax.ppermute(head, axis, [((i + 1) % count, i) for i in range(count)])  11.7 us
    unnamed x90, local copies, waits for them, and re-layouts  9.53 us
    ppermute x2, starting transfers between devices, with_halo(): lax.ppermute(tail, axis, [(i, (i + 1) % count) for i in range(count)])  7.86 us
    another operation x3, local copies, waits for them, and re-layouts, on_device(): jnp.stack([send_flux, send_zone]).reshape(2, count_x, count_y, capacity)  5.83 us
  transfers between devices with their start and end apart: 8, of which 4 were waited for; matrix products, arithmetic and copies ran while one was open for 17% of the time, Pallas kernels for 0%

profile of v3, /device:TPU:1, one launch (start us, length us, event | category | flops | bytes accessed | tf_op | source)
XLA Modules:
  0.0 150.9 jit_solution(2566990795416547707)
XLA Ops:
  9.2 4.5 %collective-permute-start = (f32[20,3,1,128]{3,2,1,0:T(1,128)S(1)}, f32[20,3,1,128]{3,2,1,0:T(1,128)S(1)}, u32[]{:S(2)}, u32[]{:S(2)}) collective-permute-start(f32[20,3,1,128]{3,2,1,0:T(1,128)S(1)} %get-tuple-element.35), channel_id=1, source_target_pairs={{0,8},{8,16},{16,24},{24,32},{32,40},{40,48},{48,56},{56,64},{64,7... | collective-permute-start | bytes 92168 | tf_op jit(solution)/shard_map/ppermute | solution.py:43
  13.7 9.8 %collective-permute-start.1 = (f32[20,3,1,128]{3,2,1,0:T(1,128)S(1)}, f32[20,3,1,128]{3,2,1,0:T(1,128)S(1)}, u32[]{:S(2)}, u32[]{:S(2)}) collective-permute-start(f32[20,3,1,128]{3,2,1,0:T(1,128)S(1)} %get-tuple-element.36), channel_id=1, source_target_pairs={{8,0},{16,8},{24,16},{32,24},{40,32},{48,40},{56,48},{64,56},{72,6... | collective-permute-start | bytes 92168 | tf_op jit(solution)/shard_map/ppermute | solution.py:45
  28.7 1.4 fusion.326
  30.1 1.8 %copy.57 = f32[20,3,34,1]{2,3,1,0:T(1,128)S(1)} copy(f32[20,3,34,1]{3,2,1,0:T(8,128)} %get-tuple-element.33) | data formatting | bytes 16320 | tf_op jit(solution)/shard_map/slice | solution.py:40
  33.0 1.9 %collective-permute-start.3 = (f32[20,3,34,1]{2,3,1,0:T(1,128)}, f32[20,3,34,1]{2,3,1,0:T(1,128)S(1)}, u32[]{:S(2)}, u32[]{:S(2)}) collective-permute-start(f32[20,3,34,1]{2,3,1,0:T(1,128)} %copy.58), channel_id=1, source_target_pairs={{1,0},{2,1},{3,2},{4,3},{5,4},{6,5},{7,6},{0,7},{9,8},{10,9},{11,1... | collective-permute-start | bytes 24488 | tf_op jit(solution)/shard_map/ppermute | solution.py:45
  34.9 3.4 %collective-permute-start.2 = (f32[20,3,34,1]{2,3,1,0:T(1,128)S(1)}, f32[20,3,34,1]{2,3,1,0:T(1,128)S(1)}, u32[]{:S(2)}, u32[]{:S(2)}) collective-permute-start(f32[20,3,34,1]{2,3,1,0:T(1,128)S(1)} %copy.57), channel_id=1, source_target_pairs={{0,1},{1,2},{2,3},{3,4},{4,5},{5,6},{6,7},{7,0},{8,9},{9,10},{10,1... | collective-permute-start | bytes 24488 | tf_op jit(solution)/shard_map/ppermute | solution.py:43
  38.3 2.5 %collective-permute-done.2 = f32[20,3,34,1]{2,3,1,0:T(1,128)S(1)} collective-permute-done((f32[20,3,34,1]{2,3,1,0:T(1,128)S(1)}, f32[20,3,34,1]{2,3,1,0:T(1,128)S(1)}, u32[]{:S(2)}, u32[]{:S(2)}) %collective-permute-start.2) | collective-permute-done | bytes 8192 | tf_op jit(solution)/shard_map/ppermute | solution.py:43
  41.3 1.6 %copy.60 = f32[20,3,34,1]{3,2,1,0:T(8,128)} copy(f32[20,3,34,1]{2,3,1,0:T(1,128)S(1)} %collective-permute-done.3) | data formatting | bytes 16320 | tf_op jit(solution)/shard_map/ppermute | solution.py:45
  43.0 3.0 %select_maximum_fusion = f32[20,5,34,130]{3,2,1,0:T(8,128)S(1)} fusion(f32[20,3,34,1]{3,2,1,0:T(8,128)} %copy.60, f32[20,3,34,1]{3,2,1,0:T(8,128)S(1)} %copy.59, f32[20,3,1,128]{3,2,1,0:T(1,128)} %copy-done.13, f32[20,3,32,128]{3,2,1,0:T(8,128)S(1)} %constant_dynamic-update-slice_fusion, f32[20,3,1,128]{3,2,1,0:T(1,128)} %copy-done.10), kind=kLoop, calls=%fused_computation.4 | loop fusion | flops 5304000 | bytes 2828800 | tf_op jit(solution)/shard_map/concatenate | solution.py:41
  46.1 1.7 %multiply_add_fusion = (f32[3,32,128]{2,1,0:T(8,128)S(1)}, f32[3,32,128]{2,1,0:T(8,128)}, f32[3,32,128]{2,1,0:T(8,128)}, f32[3,32,128]{2,1,0:T(8,128)}, f32[3,32...) fusion(f32[3,32,128]{2,1,0:T(8,128)S(1)} %copy-done.16, ...), kind=kLoop, calls=%fused_computation.474 | loop fusion | flops 2789376 | bytes 3481536 | tf_op jit(solution)/shard_map/add | solution.py:57
  48.1 5.5 %fusion.5 = f32[512]{0:T(512)S(1)} fusion(s32[96,128]{1,0:T(8,128)S(1)} %copy-done.29, f32[96,128]{1,0:T(8,128)S(1)} %bitcast.614, s32[96,128]{1,0:T(8,128)S(1)} %copy-done.28), kind=kOutput, calls=%fused_computation.17 | convolution fusion | flops 77169152 | bytes 149504 | tf_op jit(solution)/shard_map/hry,ryl->hl/dot_general | solution.py:193
  55.0 1.8 %stack.108 = f32[1,96,8,2]{3,2,1,0:T(8,128)} reshape(f32[1536]{0:T(1024)} %get-tuple-element.6) | data formatting | bytes 12288 | tf_op jit(solution)/shard_map/stack | solution.py:152
  57.9 2.0 %pad_maximum_fusion.1 = f32[2,96,8,2]{3,2,1,0:T(8,128)} fusion(f32[1,96,8,2]{3,2,1,0:T(8,128)} %stack.109, f32[1,96,8,2]{3,2,1,0:T(8,128)} %stack.108), kind=kLoop, calls=%fused_computation.21 | loop fusion | flops 3072 | bytes 24576 | tf_op jit(solution)/shard_map/stack | solution.py:152
  59.9 3.0 %copy.63 = f32[2,96,8,2]{2,3,0,1:T(2,128)} copy(f32[2,96,8,2]{3,2,1,0:T(8,128)} %pad_maximum_fusion.1) | data formatting | bytes 24576 | tf_op jit(solution)/shard_map/stack | solution.py:152
  62.9 16.2 %all-to-all-start = ((f32[2,96,8,2]{2,3,0,1:T(2,128)}), f32[2,96,8,2]{2,3,0,1:T(2,128)}, u32[]{:S(2)}, u32[]{:S(2)}) async-start(f32[2,96,8,2]{2,3,0,1:T(2,128)} %copy.63), calls=%async_computation | async-start | bytes 393216 | tf_op jit(solution)/shard_map/all_to_all | solution.py:154
  79.2 1.5 constant_dynamic-update-slice_fusion.38
  80.7 1.4 constant_dynamic-update-slice_fusion.37
  82.1 1.4 constant_dynamic-update-slice_fusion.36
  83.6 1.6 %constant_dynamic-update-slice_fusion.35 = f32[19,3,32,128]{3,2,1,0:T(8,128)} fusion(f32[19,3,32,128]{3,2,1,0:T(8,128)} %constant_dynamic-update-slice_fusion.36, pred[3,32,128]{2,1,0:T(8,128)(4,1)} %get-tuple-element.24, f32[20,3,34,1]{3,2,1,0:T(8,128)S(1)} %copy.59, f32[20,3,1,128]{3,2,1,0:T(1,128)} %copy-done.13, ...), kind=kLoop, calls=%fused_computation.69 | loop fusion | flops 245760 | bytes 1408992
  86.0 1.6 %constant_dynamic-update-slice_fusion.33 = f32[19,3,32,128]{3,2,1,0:T(8,128)} fusion(f32[19,3,32,128]{3,2,1,0:T(8,128)} %constant_dynamic-update-slice_fusion.34, pred[3,32,128]{2,1,0:T(8,128)(4,1)S(1)} %copy-done.8, f32[20,5,34,130]{3,2,1,0:T(8,128)} %copy-done.3, f32[3,32,128]{2,1,0:T(8,128)S(1)} %get-tuple-element.21, f32[3,32,128]{2,1,0:T(8,128)S(1)} %copy-done.4, ...), kind=kLoop, calls=%fused_computation.67 | loop fusion | flops 208896 | bytes 405504
  87.7 1.6 %constant_dynamic-update-slice_fusion.32 = f32[19,3,32,128]{3,2,1,0:T(8,128)} fusion(f32[19,3,32,128]{3,2,1,0:T(8,128)} %constant_dynamic-update-slice_fusion.33, pred[3,32,128]{2,1,0:T(8,128)(4,1)S(1)} %copy-done.8, f32[3,32,128]{2,1,0:T(8,128)S(1)} %get-tuple-element.21, f32[3,32,128]{2,1,0:T(8,128)S(1)} %copy-done.4, f32[20,5,34,130]{3,2,1,0:T(8,128)} %copy-done.3, ...), kind=kLoop, calls=%fused_computation.66 | loop fusion | flops 196608 | bytes 405504
  94.3 1.5 constant_dynamic-update-slice_fusion.23
  95.8 1.6 %copy.64 = f32[2,96,8,2]{1,3,0,2:T(2,128)} copy(f32[2,96,8,2]{2,3,0,1:T(2,128)} %all-to-all-done) | data formatting | bytes 24576 | tf_op jit(solution)/shard_map/all_to_all | solution.py:154
  97.4 3.8 %all-to-all-start.1 = ((f32[2,96,8,2]{1,3,0,2:T(2,128)}), f32[2,96,8,2]{1,3,0,2:T(2,128)S(1)}, u32[]{:S(2)}, u32[]{:S(2)}) async-start(f32[2,96,8,2]{1,3,0,2:T(2,128)} %copy.64), calls=%async_computation.1 | async-start | bytes 32768 | tf_op jit(solution)/shard_map/all_to_all | solution.py:153
  101.3 1.6 %constant_dynamic-update-slice_fusion.22 = f32[19,3,32,128]{3,2,1,0:T(8,128)} fusion(f32[19,3,32,128]{3,2,1,0:T(8,128)} %constant_dynamic-update-slice_fusion.23, pred[3,32,128]{2,1,0:T(8,128)(4,1)S(1)} %copy-done.9, f32[3,32,128]{2,1,0:T(8,128)S(1)} %get-tuple-element.21, f32[20,5,34,130]{3,2,1,0:T(8,128)} %copy-done.3, f32[3,32,128]{2,1,0:T(8,128)S(1)} %copy-done.7, ...), kind=kLoop, calls=%fused_computation.56 | loop fusion | flops 208896 | bytes 454656
  102.9 5.0 %all-to-all-done.1 = f32[2,96,8,2]{1,3,0,2:T(2,128)S(1)} async-done(((f32[2,96,8,2]{1,3,0,2:T(2,128)}), f32[2,96,8,2]{1,3,0,2:T(2,128)S(1)}, u32[]{:S(2)}, u32[]{:S(2)}) %all-to-all-start.1) | async-done | bytes 12320 | tf_op jit(solution)/shard_map/all_to_all | solution.py:153
  110.8 14.6 %all-to-all-start.2 = ((f32[96,8,2]{1,2,0:T(2,128)}), f32[96,8,2]{1,2,0:T(2,128)S(1)}, u32[]{:S(2)}, u32[]{:S(2)}) async-start(f32[96,8,2]{1,2,0:T(2,128)} %copy.67), calls=%async_computation.2 | async-start | bytes 196608 | tf_op jit(solution)/shard_map/all_to_all | solution.py:168
  125.4 1.5 constant_dynamic-update-slice_fusion.21
  126.9 12.0 %all-to-all-done.2 = f32[96,8,2]{1,2,0:T(2,128)S(1)} async-done(((f32[96,8,2]{1,2,0:T(2,128)}), f32[96,8,2]{1,2,0:T(2,128)S(1)}, u32[]{:S(2)}, u32[]{:S(2)}) %all-to-all-start.2) | async-done | bytes 6176 | tf_op jit(solution)/shard_map/all_to_all | solution.py:168
  139.6 3.3 %all-to-all-start.3 = ((f32[96,8,2]{0,2,1:T(2,128)}), f32[96,8,2]{0,2,1:T(2,128)S(1)}, u32[]{:S(2)}, u32[]{:S(2)}) async-start(f32[96,8,2]{0,2,1:T(2,128)} %copy.68), calls=%async_computation.3 | async-start | bytes 16384 | tf_op jit(solution)/shard_map/all_to_all | solution.py:167
  142.9 1.6 %constant_dynamic-update-slice_fusion.20 = f32[19,3,32,128]{3,2,1,0:T(8,128)} fusion(f32[19,3,32,128]{3,2,1,0:T(8,128)} %constant_dynamic-update-slice_fusion.21, pred[3,32,128]{2,1,0:T(8,128)(4,1)S(1)} %copy-done.9, f32[3,32,128]{2,1,0:T(8,128)S(1)} %get-tuple-element.21, f32[20,5,34,130]{3,2,1,0:T(8,128)} %copy-done.3, f32[3,32,128]{2,1,0:T(8,128)S(1)} %copy-done.7, ...), kind=kLoop, calls=%fused_computation.54 | loop fusion | flops 221184 | bytes 454656 | tf_op jit(solution)/shard_map/stack | solution.py:103
  144.5 4.9 %all-to-all-done.3 = f32[96,8,2]{0,2,1:T(2,128)S(1)} async-done(((f32[96,8,2]{0,2,1:T(2,128)}), f32[96,8,2]{0,2,1:T(2,128)S(1)}, u32[]{:S(2)}, u32[]{:S(2)}) %all-to-all-start.3) | async-done | bytes 6176 | tf_op jit(solution)/shard_map/all_to_all | solution.py:167
  (141 shorter events, 28.9 us)
Async XLA Ops:
  0.6 8.1 %copy-start = (f32[19,3,32,128]{3,2,1,0:T(8,128)S(1)}, f32[19,3,32,128]{3,2,1,0:T(8,128)}, u32[]{:S(2)}) copy-start(f32[19,3,32,128]{3,2,1,0:T(8,128)} %param.8) | copy-start | bytes 2801668
  0.6 8.5 %copy-start.17 = (s32[3,32,128]{2,1,0:T(8,128)S(1)}, s32[3,32,128]{2,1,0:T(8,128)}, u32[]{:S(2)}) copy-start(s32[3,32,128]{2,1,0:T(8,128)} %param.9) | copy-start | bytes 147460
  2.0 22.2 %copy-start.36 = (s32[512]{0:T(512)S(1)}, s32[512]{0:T(512)}, u32[]{:S(2)}) copy-start(s32[512]{0:T(512)} %param.11) | copy-start | bytes 6148
  2.1 23.6 %copy-start.27 = (s32[3,32,128]{2,1,0:T(8,128)S(1)}, s32[3,32,128]{2,1,0:T(8,128)}, u32[]{:S(2)}) copy-start(s32[3,32,128]{2,1,0:T(8,128)} %param.10) | copy-start | bytes 147460
  2.9 23.5 %copy-start.34 = (s32[6,128]{1,0:T(8,128)S(1)}, s32[6,128]{1,0:T(8,128)}, u32[]{:S(2)}) copy-start(s32[6,128]{1,0:T(8,128)} %param.15) | copy-start | bytes 9220
  2.9 23.5 %copy-start.38 = (f32[128]{0:T(128)S(1)}, f32[128]{0:T(128)}, u32[]{:S(2)}) copy-start(f32[128]{0:T(128)} %param.12) | copy-start | bytes 1540
  9.2 18.0 %collective-permute-start = (f32[20,3,1,128]{3,2,1,0:T(1,128)S(1)}, f32[20,3,1,128]{3,2,1,0:T(1,128)S(1)}, u32[]{:S(2)}, u32[]{:S(2)}) collective-permute-start(f32[20,3,1,128]{3,2,1,0:T(1,128)S(1)} %get-tuple-element.35), channel_id=1, source_target_pairs={{0,8},{8,16},{16,24},{24,32},{32,40},{40,48},{48,56},{56,64},{64,7... | collective-permute-start | bytes 92168 | tf_op jit(solution)/shard_map/ppermute | solution.py:43
  13.7 13.5 %collective-permute-start.1 = (f32[20,3,1,128]{3,2,1,0:T(1,128)S(1)}, f32[20,3,1,128]{3,2,1,0:T(1,128)S(1)}, u32[]{:S(2)}, u32[]{:S(2)}) collective-permute-start(f32[20,3,1,128]{3,2,1,0:T(1,128)S(1)} %get-tuple-element.36), channel_id=1, source_target_pairs={{8,0},{16,8},{24,16},{32,24},{40,32},{48,40},{56,48},{64,56},{72,6... | collective-permute-start | bytes 92168 | tf_op jit(solution)/shard_map/ppermute | solution.py:45
  33.0 8.3 %collective-permute-start.3 = (f32[20,3,34,1]{2,3,1,0:T(1,128)}, f32[20,3,34,1]{2,3,1,0:T(1,128)S(1)}, u32[]{:S(2)}, u32[]{:S(2)}) collective-permute-start(f32[20,3,34,1]{2,3,1,0:T(1,128)} %copy.58), channel_id=1, source_target_pairs={{1,0},{2,1},{3,2},{4,3},{5,4},{6,5},{7,6},{0,7},{9,8},{10,9},{11,1... | collective-permute-start | bytes 24488 | tf_op jit(solution)/shard_map/ppermute | solution.py:45
  34.9 5.8 %collective-permute-start.2 = (f32[20,3,34,1]{2,3,1,0:T(1,128)S(1)}, f32[20,3,34,1]{2,3,1,0:T(1,128)S(1)}, u32[]{:S(2)}, u32[]{:S(2)}) collective-permute-start(f32[20,3,34,1]{2,3,1,0:T(1,128)S(1)} %copy.57), channel_id=1, source_target_pairs={{0,1},{1,2},{2,3},{3,4},{4,5},{5,6},{6,7},{7,0},{8,9},{9,10},{10,1... | collective-permute-start | bytes 24488 | tf_op jit(solution)/shard_map/ppermute | solution.py:43
  46.1 7.6 %copy-start.30 = (s32[512]{0:T(512)S(1)}, s32[512]{0:T(512)}, u32[]{:S(2)}) copy-start(s32[512]{0:T(512)} %multiply_add_fusion.1) | copy-start | bytes 6148
  46.1 7.6 %copy-start.33 = (f32[512]{0:T(512)S(1)}, f32[512]{0:T(512)}, u32[]{:S(2)}) copy-start(f32[512]{0:T(512)} %get-tuple-element.8) | copy-start | bytes 6148
  62.9 32.9 %all-to-all-start = ((f32[2,96,8,2]{2,3,0,1:T(2,128)}), f32[2,96,8,2]{2,3,0,1:T(2,128)}, u32[]{:S(2)}, u32[]{:S(2)}) async-start(f32[2,96,8,2]{2,3,0,1:T(2,128)} %copy.63), calls=%async_computation | async-start | bytes 393216 | tf_op jit(solution)/shard_map/all_to_all | solution.py:154
  80.7 8.6 %copy-start.26 = (f32[3,32,128]{2,1,0:T(8,128)S(1)}, f32[3,32,128]{2,1,0:T(8,128)}, u32[]{:S(2)}) copy-start(f32[3,32,128]{2,1,0:T(8,128)} %get-tuple-element.18) | copy-start | bytes 147460
  82.1 7.8 %copy-start.25 = (f32[3,32,128]{2,1,0:T(8,128)S(1)}, f32[3,32,128]{2,1,0:T(8,128)}, u32[]{:S(2)}) copy-start(f32[3,32,128]{2,1,0:T(8,128)} %get-tuple-element.17) | copy-start | bytes 147460
  83.5 7.0 %copy-start.24 = (f32[3,32,128]{2,1,0:T(8,128)S(1)}, f32[3,32,128]{2,1,0:T(8,128)}, u32[]{:S(2)}) copy-start(f32[3,32,128]{2,1,0:T(8,128)} %get-tuple-element.16) | copy-start | bytes 147460
  83.5 7.6 %copy-start.23 = (f32[3,32,128]{2,1,0:T(8,128)S(1)}, f32[3,32,128]{2,1,0:T(8,128)}, u32[]{:S(2)}) copy-start(f32[3,32,128]{2,1,0:T(8,128)} %get-tuple-element.15) | copy-start | bytes 147460
  83.6 8.2 %copy-start.22 = (f32[3,32,128]{2,1,0:T(8,128)S(1)}, f32[3,32,128]{2,1,0:T(8,128)}, u32[]{:S(2)}) copy-start(f32[3,32,128]{2,1,0:T(8,128)} %get-tuple-element.14) | copy-start | bytes 147460
  83.6 8.9 %copy-start.21 = (f32[3,32,128]{2,1,0:T(8,128)S(1)}, f32[3,32,128]{2,1,0:T(8,128)}, u32[]{:S(2)}) copy-start(f32[3,32,128]{2,1,0:T(8,128)} %get-tuple-element.13) | copy-start | bytes 147460
  83.6 9.5 %copy-start.20 = (f32[3,32,128]{2,1,0:T(8,128)S(1)}, f32[3,32,128]{2,1,0:T(8,128)}, u32[]{:S(2)}) copy-start(f32[3,32,128]{2,1,0:T(8,128)} %get-tuple-element.12) | copy-start | bytes 147460
  83.6 10.1 %copy-start.19 = (f32[3,32,128]{2,1,0:T(8,128)S(1)}, f32[3,32,128]{2,1,0:T(8,128)}, u32[]{:S(2)}) copy-start(f32[3,32,128]{2,1,0:T(8,128)} %get-tuple-element.11) | copy-start | bytes 147460
  83.6 17.6 %copy-start.5 = (f32[3,32,128]{2,1,0:T(8,128)S(1)}, f32[3,32,128]{2,1,0:T(8,128)}, u32[]{:S(2)}) copy-start(f32[3,32,128]{2,1,0:T(8,128)} %get-tuple-element.23) | copy-start | bytes 147460
  83.6 17.6 %copy-start.7 = (f32[3,32,128]{2,1,0:T(8,128)S(1)}, f32[3,32,128]{2,1,0:T(8,128)}, u32[]{:S(2)}) copy-start(f32[3,32,128]{2,1,0:T(8,128)} %get-tuple-element.22) | copy-start | bytes 147460
  85.2 16.0 %copy-start.9 = (pred[3,32,128]{2,1,0:T(8,128)(4,1)S(1)}, pred[3,32,128]{2,1,0:T(8,128)(4,1)}, u32[]{:S(2)}) copy-start(pred[3,32,128]{2,1,0:T(8,128)(4,1)} %get-tuple-element.24) | copy-start | bytes 36868
  85.3 23.7 %copy-start.32 = (f32[6,128]{1,0:T(8,128)S(1)}, f32[6,128]{1,0:T(8,128)}, u32[]{:S(2)}) copy-start(f32[6,128]{1,0:T(8,128)} %select_reduce_fusion.5) | copy-start | bytes 9220
  85.3 23.7 %copy-start.35 = (f32[6,128]{1,0:T(8,128)S(1)}, f32[6,128]{1,0:T(8,128)}, u32[]{:S(2)}) copy-start(f32[6,128]{1,0:T(8,128)} %param.14) | copy-start | bytes 9220
  85.3 23.7 %copy-start.39 = (f32[128]{0:T(128)S(1)}, f32[128]{0:T(128)}, u32[]{:S(2)}) copy-start(f32[128]{0:T(128)} %param.13) | copy-start | bytes 1540
  91.2 58.7 %copy-start.31 = (s32[512]{0:T(512)S(1)}, s32[512]{0:T(512)}, u32[]{:S(2)}) copy-start(s32[512]{0:T(512)} %multiply_add_fusion.1) | copy-start | bytes 6148
  97.4 10.4 %all-to-all-start.1 = ((f32[2,96,8,2]{1,3,0,2:T(2,128)}), f32[2,96,8,2]{1,3,0,2:T(2,128)S(1)}, u32[]{:S(2)}, u32[]{:S(2)}) async-start(f32[2,96,8,2]{1,3,0,2:T(2,128)} %copy.64), calls=%async_computation.1 | async-start | bytes 32768 | tf_op jit(solution)/shard_map/all_to_all | solution.py:153
  109.0 41.9 %copy-start.37 = (f32[128]{0:T(128)}, f32[128]{0:T(128)S(1)}, u32[]{:S(2)}) copy-start(f32[128]{0:T(128)S(1)} %fusion.308) | copy-start | bytes 1540
  110.8 28.2 %all-to-all-start.2 = ((f32[96,8,2]{1,2,0:T(2,128)}), f32[96,8,2]{1,2,0:T(2,128)S(1)}, u32[]{:S(2)}, u32[]{:S(2)}) async-start(f32[96,8,2]{1,2,0:T(2,128)} %copy.67), calls=%async_computation.2 | async-start | bytes 196608 | tf_op jit(solution)/shard_map/all_to_all | solution.py:168
  139.6 9.8 %all-to-all-start.3 = ((f32[96,8,2]{0,2,1:T(2,128)}), f32[96,8,2]{0,2,1:T(2,128)S(1)}, u32[]{:S(2)}, u32[]{:S(2)}) async-start(f32[96,8,2]{0,2,1:T(2,128)} %copy.68), calls=%async_computation.3 | async-start | bytes 16384 | tf_op jit(solution)/shard_map/all_to_all | solution.py:167
  (16 other events, 60.3 us)

commit v4 on v3

--- a/solution.py
+++ b/solution.py
@@ -2,6 +2,8 @@
 import jax.numpy as jnp
 import numpy as np
 from jax import lax
+from jax.experimental import pallas as pl
+from jax.experimental.pallas import tpu as pltpu
 from jax.sharding import PartitionSpec as P
 
 DIRECTIONS = np.array(
@@ -112,24 +114,55 @@
     return (inflow + coupled) / total
 
 
+def exchange_halos(populations, fluid):
+    count_x = lax.axis_size("gx")
+    count_y = lax.axis_size("gy")
+    stacked_x = [
+        jnp.concatenate([populations[:, :, at, None, :], fluid[None, :, at, None, :]], axis=0)
+        for at in (0, -1)
+    ]
+    stacked_y = [
+        jnp.concatenate([populations[:, :, :, at, None], fluid[None, :, :, at, None]], axis=0)
+        for at in (0, -1)
+    ]
+    corner = {
+        (cx, cy): jnp.concatenate(
+            [populations[:, :, cx, None, cy, None], fluid[None, :, cx, None, cy, None]], axis=0
+        )
+        for cx in (0, -1)
+        for cy in (0, -1)
+    }
+    ring_up = [(i, (i + 1) % count_x) for i in range(count_x)]
+    ring_down = [((i + 1) % count_x, i) for i in range(count_x)]
+    line_up = [(j, j + 1) for j in range(count_y - 1)]
+    line_down = [(j + 1, j) for j in range(count_y - 1)]
+
+    def diagonal(step_x, step_y):
+        pairs = []
+        for i in range(count_x):
+            for j in range(count_y):
+                if 0 <= j + step_y < count_y:
+                    pairs.append((i * count_y + j, ((i + step_x) % count_x) * count_y + j + step_y))
+        return pairs
+
+    both = ("gx", "gy")
+    x_low = lax.ppermute(stacked_x[1], "gx", ring_up)
+    x_high = lax.ppermute(stacked_x[0], "gx", ring_down)
+    y_low = lax.ppermute(stacked_y[1], "gy", line_up)
+    y_high = lax.ppermute(stacked_y[0], "gy", line_down)
+    c_ll = lax.ppermute(corner[(-1, -1)], both, diagonal(1, 1))
+    c_hl = lax.ppermute(corner[(0, -1)], both, diagonal(-1, 1))
+    c_lh = lax.ppermute(corner[(-1, 0)], both, diagonal(1, -1))
+    c_hh = lax.ppermute(corner[(0, 0)], both, diagonal(-1, -1))
+    return (x_low, x_high, y_low, y_high, c_ll, c_hl, c_lh, c_hh)
+
+
 def on_device(
     populations, solid_flag, cell_patch, patch_zone, old_pressure, leakage, conductance, neighbour
 ):
-    depth, width_x, width_y = solid_flag.shape
-    relaxed = collide(populations)
     fluid = (1 - solid_flag).astype(jnp.float32)
-    column = lax.axis_index("gy")
-    lower_open = jnp.where(column > 0, 1.0, 0.0).astype(jnp.float32)
-    upper_open = jnp.where(column < lax.axis_size("gy") - 1, 1.0, 0.0).astype(jnp.float32)
-    places = jnp.arange(width_y + 2, dtype=jnp.int32)
-    keeper = jnp.where(places == 0, lower_open, jnp.where(places == width_y + 1, upper_open, 1.0))
-    stacked = jnp.concatenate([relaxed, fluid[None]], axis=0)
-    widened = with_halo(stacked, (("gx", 2), ("gy", 3)), 1)
-    widened = jnp.pad(widened, ((0, 0), (1, 1), (0, 0), (0, 0)))
-    flag_pad = widened[19] * keeper
-    post_pad = widened[:19]
-    new_populations = stream(post_pad, flag_pad, relaxed, populations, solid_flag)
-    momentum_x = moment(new_populations, 0)
+    halos = exchange_halos(populations, fluid)
+    new_populations, momentum_x = lbm_step(populations, solid_flag, halos)
     patch_flux = patch_sums(momentum_x, cell_patch, patch_zone.shape[0])
     zone_dev = old_pressure.shape[0]
     openings = patch_zone.shape[0]
@@ -206,6 +239,141 @@
     return coupled, total
 
 
+def collide_list(planes):
+    density = jnp.zeros_like(planes[0])
+    for direction in range(19):
+        density = density + planes[direction]
+    velocity = []
+    for component in range(3):
+        total = jnp.zeros_like(planes[0])
+        for direction in range(19):
+            sign = int(DIRECTIONS[direction, component])
+            if sign != 0:
+                total = total + float(sign) * planes[direction]
+        velocity.append(total / density)
+    speed_sq = velocity[0] * velocity[0] + velocity[1] * velocity[1] + velocity[2] * velocity[2]
+    relaxed = []
+    for direction in range(19):
+        along = jnp.zeros_like(density)
+        for component in range(3):
+            sign = int(DIRECTIONS[direction, component])
+            if sign != 0:
+                along = along + float(sign) * velocity[component]
+        equilibrium = (
+            LATTICE_WEIGHTS[direction]
+            * density
+            * (1.0 + 3.0 * along + 4.5 * along * along - 1.5 * speed_sq)
+        )
+        relaxed.append(planes[direction] - OMEGA * (planes[direction] - equilibrium))
+    return relaxed
+
+
+def shift_x(plane, step, edge, xi, width_x):
+    if step == 1:
+        return jnp.where(xi == 0, edge, pltpu.roll(plane, 1, 0))
+    if step == -1:
+        return jnp.where(xi == width_x - 1, edge, pltpu.roll(plane, width_x - 1, 0))
+    return plane
+
+
+def shift_plane(plane, step_x, step_y, row, column, corner, xi, yi, width_x, width_y):
+    moved = shift_x(plane, step_x, row, xi, width_x)
+    if step_y == 0:
+        return moved
+    edge = shift_x(column, step_x, corner, xi, width_x)
+    if step_y == 1:
+        return jnp.where(yi == 0, edge, pltpu.roll(moved, 1, 1))
+    return jnp.where(yi == width_y - 1, edge, pltpu.roll(moved, width_y - 1, 1))
+
+
+def lbm_kernel(
+    pop_ref, solid_ref, xlo_ref, xhi_ref, ylo_ref, yhi_ref,
+    cll_ref, chl_ref, clh_ref, chh_ref,
+    new_ref, mom_ref, rel_ref,
+):
+    _, depth, width_x, width_y = pop_ref.shape
+    shape = (width_x, width_y)
+    xi = lax.broadcasted_iota(jnp.int32, shape, 0)
+    yi = lax.broadcasted_iota(jnp.int32, shape, 1)
+    for level in range(depth):
+        relaxed = collide_list([pop_ref[d, level] for d in range(19)])
+        for d in range(19):
+            rel_ref[d, level] = relaxed[d]
+
+    def halo(ref):
+        values = [ref[d] for d in range(20)]
+        return collide_list(values[:19]), values[19]
+
+    xlo, xlo_f = halo(xlo_ref)
+    xhi, xhi_f = halo(xhi_ref)
+    ylo, ylo_f = halo(ylo_ref)
+    yhi, yhi_f = halo(yhi_ref)
+    cll, cll_f = halo(cll_ref)
+    chl, chl_f = halo(chl_ref)
+    clh, clh_f = halo(clh_ref)
+    chh, chh_f = halo(chh_ref)
+
+    def pieces(step_x, step_y, level, direction):
+        if direction is None:
+            x_lo, x_hi, y_lo, y_hi = xlo_f, xhi_f, ylo_f, yhi_f
+            c_ll, c_hl, c_lh, c_hh = cll_f, chl_f, clh_f, chh_f
+        else:
+            x_lo, x_hi, y_lo, y_hi = xlo[direction], xhi[direction], ylo[direction], yhi[direction]
+            c_ll, c_hl, c_lh, c_hh = cll[direction], chl[direction], clh[direction], chh[direction]
+        row = x_lo[level] if step_x == 1 else x_hi[level]
+        column = y_lo[level] if step_y == 1 else y_hi[level]
+        if step_y == 1:
+            corner = c_ll[level] if step_x == 1 else c_hl[level]
+        else:
+            corner = c_lh[level] if step_x == 1 else c_hh[level]
+        row = jnp.broadcast_to(row, shape)
+        column = jnp.broadcast_to(column, shape)
+        corner = jnp.broadcast_to(corner, shape)
+        return row, column, corner
+
+    for level in range(depth):
+        solid = solid_ref[level] == 1
+        momentum = jnp.zeros(shape, jnp.float32)
+        for d in range(19):
+            step_x, step_y, step_z = (int(v) for v in DIRECTIONS[d])
+            source_level = level - step_z
+            kept = pop_ref[d, level]
+            bounced = rel_ref[OPPOSITE[d], level]
+            if 0 <= source_level < depth:
+                row, column, corner = pieces(step_x, step_y, source_level, d)
+                source = shift_plane(
+                    rel_ref[d, source_level], step_x, step_y, row, column, corner,
+                    xi, yi, width_x, width_y,
+                )
+                frow, fcolumn, fcorner = pieces(step_x, step_y, source_level, None)
+                fluid = 1.0 - solid_ref[source_level].astype(jnp.float32)
+                open_source = shift_plane(
+                    fluid, step_x, step_y, frow, fcolumn, fcorner,
+                    xi, yi, width_x, width_y,
+                )
+                pulled = jnp.where(open_source > 0.5, source, bounced)
+            else:
+                pulled = bounced
+            value = jnp.where(solid, kept, pulled)
+            new_ref[d, level] = value
+            if step_x != 0:
+                momentum = momentum + float(step_x) * value
+        mom_ref[level] = momentum
+
+
+def lbm_step(populations, solid_flag, halos, interpret=False):
+    depth, width_x, width_y = solid_flag.shape
+    return pl.pallas_call(
+        lbm_kernel,
+        out_shape=(
+            jax.ShapeDtypeStruct(populations.shape, jnp.float32),
+            jax.ShapeDtypeStruct(solid_flag.shape, jnp.float32),
+        ),
+        scratch_shapes=[pltpu.VMEM(populations.shape, jnp.float32)],
+        interpret=interpret,
+    )(populations, solid_flag, *halos)
+
+
 def solution(mesh):
     placed = (
         P(None, None, "gx", "gy"),

time: 152 us -> 141 us (0.928)
  blocking collectives: 0 us -> 56.7 us
  other arithmetic: 35.2 us -> 3.92 us
  waiting for transfers between devices: 24.4 us -> 8.39 us
  starting transfers between devices: 57.5 us -> 44.7 us
  local copies, waits for them, and re-layouts: 27.2 us -> 14.5 us
  Pallas kernels: 0 us -> 4.22 us
    all_to_all x0 -> x3, blocking collectives: none -> 56.7 us  [the longest x1 27.5 us: on_device(): lax.all_to_all(outgoing, 'gx', split_axis=1, concat_axis=1, tiled=True)]
    all_to_all x3 -> x0, starting transfers between devices: 34.1 us -> none  [the longest x1 16.2 us: on_device(): lax.all_to_all(outgoing, 'gx', split_axis=1, concat_axis=1, tiled=True)]
    unnamed x27 -> x0, other arithmetic: 20.1 us -> none
    all_to_all x3 -> x0, waiting for transfers between devices: 16.9 us -> none  [the longest x1 12 us: on_device(): lax.all_to_all(answered, 'gx', split_axis=0, concat_axis=0, tiled=True)]
    ppermute x4 -> x8, starting transfers between devices: 19.6 us -> 32.5 us  [the longest x1 11.7 us: exchange_halos(): c_hl = lax.ppermute(corner[0, -1], both, diagonal(-1, 1))]
    all_to_all x1, starting transfers between devices: 3.8 us -> 12.2 us  [on_device(): lax.all_to_all(lax.all_to_all(outgoing, 'gx', split_axis=1, concat_axis=1...]
    unnamed x90 -> x28, local copies, waits for them, and re-layouts: 9.53 us -> 2.05 us
    pallas_call x0 -> x1, Pallas kernels: none -> 4.22 us  [lbm_step(): pl.pallas_call(lbm_kernel, out_shape=(jax.ShapeDtypeStruct(populations.sh...]
  transfers between devices with their start and end apart: 8 -> 9, of which waited for: 4 -> 2; matrix products, arithmetic and copies ran while one was open for 17% -> 5% of each run, Pallas kernels for 0% -> 0%
where the time goes in v4:
time: 141 us; the launch traced here: 140 us
  blocking collectives  56.7 us (40%)
  starting transfers between devices  44.7 us (32%)
  local copies, waits for them, and re-layouts  14.5 us (10%)
  waiting for transfers between devices  8.39 us (6%)
  matrix products  6.52 us (5%)
  Pallas kernels  4.22 us (3%)
  other arithmetic  3.92 us (3%)
    all_to_all x1, blocking collectives, on_device(): lax.all_to_all(outgoing, 'gx', split_axis=1, concat_axis=1, tiled=True)  27.5 us
    all_to_all x1, blocking collectives, on_device(): lax.all_to_all(answered, 'gx', split_axis=0, concat_axis=0, tiled=True)  20.2 us
    all_to_all x1, starting transfers between devices, on_device(): lax.all_to_all(lax.all_to_all(outgoing, 'gx', split_axis=1, concat_axis=1...  12.2 us
    ppermute x1, starting transfers between devices, exchange_halos(): c_hl = lax.ppermute(corner[0, -1], both, diagonal(-1, 1))  11.7 us
    all_to_all x1, blocking collectives, on_device(): lax.all_to_all(lax.all_to_all(answered, 'gx', split_axis=0, concat_axis=0...  8.94 us
    dot_general x1, matrix products, patch_sums(): jnp.einsum('hry,ryl->hl', picked, onehot, precision=lax.Precision.HIGHEST)  6.52 us
    all_to_all x1, waiting for transfers between devices, on_device(): lax.all_to_all(lax.all_to_all(outgoing, 'gx', split_axis=1, concat_axis=1...  6.31 us
    ppermute x1, starting transfers between devices, exchange_halos(): x_high = lax.ppermute(stacked_x[0], 'gx', ring_down)  5.98 us
  transfers between devices with their start and end apart: 9, of which 2 were waited for; matrix products, arithmetic and copies ran while one was open for 5% of the time, Pallas kernels for 0%

profile of v4, /device:TPU:1, one launch (start us, length us, event | category | flops | bytes accessed | tf_op | source)
XLA Modules:
  0.0 140.0 jit_solution(477445804336660302)
XLA Ops:
  0.6 0.8 subtract_convert_fusion
  1.5 1.5 %fusion.23 = (f32[19,3,1,1]{3,2,1,0:T(1,128)S(1)}, f32[19,3,1,1]{3,2,1,0:T(1,128)S(1)}, f32[19,3,1,1]{3,2,1,0:T(1,128)S(1)}, f32[19,3,1,1]{3,2,1,0:T(1,128)S(1)}) fusion(f32[19,3,32,128]{3,2,1,0:T(8,128)} %pop_ref.1), kind=kLoop, calls=%fused_computation.82 | loop fusion | bytes 1824 | tf_op jit(solution)/shard_map/slice | solution.py:130
  3.0 5.5 %collective-permute-start.4 = (f32[20,3,1,1]{3,2,1,0:T(1,128)S(1)}, f32[20,3,1,1]{3,2,1,0:T(1,128)S(1)}, u32[]{:S(2)}, u32[]{:S(2)}) collective-permute-start(f32[20,3,1,1]{3,2,1,0:T(1,128)S(1)} %pad_maximum_fusion.5), channel_id=1, source_target_pairs={{0,9},{1,10},{2,11},{3,12},{4,13},{5,14},{6,15},{8,17},{9,18},{10,... | collective-permute-start | bytes 728 | tf_op jit(solution)/shard_map/ppermute | solution.py:153
  8.7 1.9 %fusion.24 = (f32[19,3,32,1]{3,2,1,0:T(8,128)S(1)}, f32[19,3,32,1]{3,2,1,0:T(8,128)S(1)}) fusion(f32[19,3,32,128]{3,2,1,0:T(8,128)} %pop_ref.1), kind=kLoop, calls=%fused_computation.83 | loop fusion | bytes 29184 | tf_op jit(solution)/shard_map/slice | solution.py:125
  10.6 0.4 copy.67
  11.1 3.2 %collective-permute-start.2 = (f32[20,3,32,1]{2,3,1,0:T(1,128)S(1)}, f32[20,3,32,1]{2,3,1,0:T(1,128)S(1)}, u32[]{:S(2)}, u32[]{:S(2)}) collective-permute-start(f32[20,3,32,1]{2,3,1,0:T(1,128)S(1)} %pad_maximum_fusion.3), channel_id=1, source_target_pairs={{0,1},{1,2},{2,3},{3,4},{4,5},{5,6},{6,7},{8,9},{9,10},{10,11},{11... | collective-permute-start | bytes 23048 | tf_op jit(solution)/shard_map/ppermute | solution.py:151
  14.3 0.4 copy.68
  14.7 1.3 collective-permute-start.3
  16.0 1.1 fusion.25
  17.2 2.2 %collective-permute-start = (f32[20,3,1,128]{3,2,1,0:T(1,128)S(1)}, f32[20,3,1,128]{3,2,1,0:T(1,128)S(1)}, u32[]{:S(2)}, u32[]{:S(2)}) collective-permute-start(f32[20,3,1,128]{3,2,1,0:T(1,128)S(1)} %pad_maximum_fusion.1), channel_id=1, source_target_pairs={{0,8},{8,16},{16,24},{24,32},{32,40},{40,48},{48,56},{56,64},{64,7... | collective-permute-start | bytes 92168 | tf_op jit(solution)/shard_map/ppermute | solution.py:149
  19.4 6.0 %collective-permute-start.1 = (f32[20,3,1,128]{3,2,1,0:T(1,128)S(1)}, f32[20,3,1,128]{3,2,1,0:T(1,128)S(1)}, u32[]{:S(2)}, u32[]{:S(2)}) collective-permute-start(f32[20,3,1,128]{3,2,1,0:T(1,128)S(1)} %pad_maximum_fusion.2), channel_id=1, source_target_pairs={{8,0},{16,8},{24,16},{32,24},{40,32},{48,40},{56,48},{64,56},{72,6... | collective-permute-start | bytes 92168 | tf_op jit(solution)/shard_map/ppermute | solution.py:150
  25.9 11.7 %collective-permute-start.5 = (f32[20,3,1,1]{3,2,1,0:T(1,128)S(1)}, f32[20,3,1,1]{3,2,1,0:T(1,128)S(1)}, u32[]{:S(2)}, u32[]{:S(2)}) collective-permute-start(f32[20,3,1,1]{3,2,1,0:T(1,128)S(1)} %pad_maximum_fusion.6), channel_id=1, source_target_pairs={{0,761},{1,762},{2,763},{3,764},{4,765},{5,766},{6,767},{8,1},{9,2... | collective-permute-start | bytes 728 | tf_op jit(solution)/shard_map/ppermute | solution.py:154
  37.7 1.3 collective-permute-start.6
  39.0 1.3 collective-permute-start.7
  40.3 1.4 copy.58.ylo_ref
  41.6 1.4 %copy.59.yhi_ref = f32[20,3,32,1]{3,2,1,0:T(8,128)} copy(f32[20,3,32,1]{2,3,1,0:T(1,128)S(1)} %collective-permute-done.3) | data formatting | bytes 15360 | tf_op jit(solution)/shard_map/ppermute | solution.py:152
  43.1 2.1 %collective-permute-done.6.clh_ref = f32[20,3,1,1]{3,2,1,0:T(1,128)S(1)} collective-permute-done((f32[20,3,1,1]{3,2,1,0:T(1,128)S(1)}, f32[20,3,1,1]{3,2,1,0:T(1,128)S(1)}, u32[]{:S(2)}, u32[]{:S(2)}) %collective-permute-start.6) | collective-permute-done | bytes 272 | tf_op jit(solution)/shard_map/ppermute | solution.py:155
  45.2 0.6 copy-done.5
  45.8 0.6 copy-done.3
  46.4 4.2 %shard_map.103 = (f32[19,3,32,128]{3,2,1,0:T(8,128)}, f32[3,32,128]{2,1,0:T(8,128)}) custom-call(f32[19,3,32,128]{3,2,1,0:T(8,128)} %pop_ref.1, s32[3,32,128]{2,1,0:T(8,128)} %solid_ref.1, f32[20,3,1,128]{3,2,1,0:T(1,128)} %copy-done.2, f32[20,3,1,128]{3,2,1,0:T(1,128)} %copy-done.3, f32[20,3,32,1]{3,2,1,0:T(8,128)} %copy.58.ylo_ref, ...), custom_call_target="tpu_custom_call" | custom-call | tf_op jit(solution)/shard_map/pallas_call | solution.py:366
  50.6 6.5 %fusion.4 = f32[512]{0:T(512)S(1)} fusion(s32[96,128]{1,0:T(8,128)S(1)} %get-tuple-element.22, f32[96,128]{1,0:T(8,128)} %bitcast.114, s32[96,128]{1,0:T(8,128)S(1)} %get-tuple-element.21), kind=kOutput, calls=%fused_computation.9 | convolution fusion | flops 77169152 | bytes 149504 | tf_op jit(solution)/shard_map/hry,ryl->hl/dot_general | solution.py:226
  57.2 0.8 select_reduce_fusion.2
  58.3 0.3 stack.9
  58.7 1.2 copy.60
  59.9 27.5 %all_to_all.20 = f32[2,96,8,2]{2,3,0,1:T(2,128)S(1)} all-to-all(f32[2,96,8,2]{2,3,0,1:T(2,128)S(1)} %copy.60), channel_id=1, replica_groups=mesh['gx'=96,'gy'=8] {'gx'}, dimensions={1} | all-to-all | bytes 24576 | tf_op jit(solution)/shard_map/all_to_all | solution.py:187
  87.4 0.7 copy.61
  88.1 12.2 %all-to-all-start.1 = ((f32[2,96,8,2]{1,3,0,2:T(2,128)}), f32[2,96,8,2]{1,3,0,2:T(2,128)S(1)}, u32[]{:S(2)}, u32[]{:S(2)}) async-start(f32[2,96,8,2]{1,3,0,2:T(2,128)} %copy.61), calls=%async_computation.1 | async-start | bytes 32768 | tf_op jit(solution)/shard_map/all_to_all | solution.py:186
  100.6 6.3 %all-to-all-done.1 = f32[2,96,8,2]{1,3,0,2:T(2,128)S(1)} async-done(((f32[2,96,8,2]{1,3,0,2:T(2,128)}), f32[2,96,8,2]{1,3,0,2:T(2,128)S(1)}, u32[]{:S(2)}, u32[]{:S(2)}) %all-to-all-start.1) | async-done | bytes 12320 | tf_op jit(solution)/shard_map/all_to_all | solution.py:186
  108.6 0.6 copy.64
  109.2 20.2 %all_to_all.21 = f32[96,8,2]{1,2,0:T(2,128)S(1)} all-to-all(f32[96,8,2]{1,2,0:T(2,128)S(1)} %copy.64), channel_id=1, replica_groups=mesh['gx'=96,'gy'=8] {'gx'}, dimensions={0} | all-to-all | bytes 12288 | tf_op jit(solution)/shard_map/all_to_all | solution.py:201
  129.5 8.9 %all_to_all.22 = f32[96,8,2]{0,2,1:T(2,128)S(1)} all-to-all(f32[96,8,2]{0,2,1:T(2,128)S(1)} %copy.65), channel_id=1, replica_groups=mesh['gx'=96,'gy'=8] {'gy'}, dimensions={1} | all-to-all | bytes 12288 | tf_op jit(solution)/shard_map/all_to_all | solution.py:200
  138.9 1.1 select_reduce_fusion
  (63 shorter events, 3.7 us)
Async XLA Ops:
  3.0 22.8 %collective-permute-start.4 = (f32[20,3,1,1]{3,2,1,0:T(1,128)S(1)}, f32[20,3,1,1]{3,2,1,0:T(1,128)S(1)}, u32[]{:S(2)}, u32[]{:S(2)}) collective-permute-start(f32[20,3,1,1]{3,2,1,0:T(1,128)S(1)} %pad_maximum_fusion.5), channel_id=1, source_target_pairs={{0,9},{1,10},{2,11},{3,12},{4,13},{5,14},{6,15},{8,17},{9,18},{10,... | collective-permute-start | bytes 728 | tf_op jit(solution)/shard_map/ppermute | solution.py:153
  10.6 14.8 %copy-start = (s32[3,32,128]{2,1,0:T(8,128)S(1)}, s32[3,32,128]{2,1,0:T(8,128)}, u32[]{:S(2)}) copy-start(s32[3,32,128]{2,1,0:T(8,128)} %param.10) | copy-start | bytes 147460
  11.0 14.5 %copy-start.9 = (s32[512]{0:T(512)S(1)}, s32[512]{0:T(512)}, u32[]{:S(2)}) copy-start(s32[512]{0:T(512)} %param.11) | copy-start | bytes 6148
  11.1 26.6 %collective-permute-start.2 = (f32[20,3,32,1]{2,3,1,0:T(1,128)S(1)}, f32[20,3,32,1]{2,3,1,0:T(1,128)S(1)}, u32[]{:S(2)}, u32[]{:S(2)}) collective-permute-start(f32[20,3,32,1]{2,3,1,0:T(1,128)S(1)} %pad_maximum_fusion.3), channel_id=1, source_target_pairs={{0,1},{1,2},{2,3},{3,4},{4,5},{5,6},{6,7},{8,9},{9,10},{10,11},{11... | collective-permute-start | bytes 23048 | tf_op jit(solution)/shard_map/ppermute | solution.py:151
  14.7 24.2 %collective-permute-start.3 = (f32[20,3,32,1]{2,3,1,0:T(1,128)S(1)}, f32[20,3,32,1]{2,3,1,0:T(1,128)S(1)}, u32[]{:S(2)}, u32[]{:S(2)}) collective-permute-start(f32[20,3,32,1]{2,3,1,0:T(1,128)S(1)} %pad_maximum_fusion.4), channel_id=1, source_target_pairs={{1,0},{2,1},{3,2},{4,3},{5,4},{6,5},{7,6},{9,8},{10,9},{11,10},{12... | collective-permute-start | bytes 23048 | tf_op jit(solution)/shard_map/ppermute | solution.py:152
  17.2 28.0 %collective-permute-start = (f32[20,3,1,128]{3,2,1,0:T(1,128)S(1)}, f32[20,3,1,128]{3,2,1,0:T(1,128)S(1)}, u32[]{:S(2)}, u32[]{:S(2)}) collective-permute-start(f32[20,3,1,128]{3,2,1,0:T(1,128)S(1)} %pad_maximum_fusion.1), channel_id=1, source_target_pairs={{0,8},{8,16},{16,24},{24,32},{32,40},{40,48},{48,56},{56,64},{64,7... | collective-permute-start | bytes 92168 | tf_op jit(solution)/shard_map/ppermute | solution.py:149
  19.4 25.8 %collective-permute-start.1 = (f32[20,3,1,128]{3,2,1,0:T(1,128)S(1)}, f32[20,3,1,128]{3,2,1,0:T(1,128)S(1)}, u32[]{:S(2)}, u32[]{:S(2)}) collective-permute-start(f32[20,3,1,128]{3,2,1,0:T(1,128)S(1)} %pad_maximum_fusion.2), channel_id=1, source_target_pairs={{8,0},{16,8},{24,16},{32,24},{40,32},{48,40},{56,48},{64,56},{72,6... | collective-permute-start | bytes 92168 | tf_op jit(solution)/shard_map/ppermute | solution.py:150
  25.9 17.2 %copy-start.1 = (f32[20,3,1,1]{3,2,1,0:T(1,128)}, f32[20,3,1,1]{3,2,1,0:T(1,128)S(1)}, u32[]{:S(2)}) copy-start(f32[20,3,1,1]{3,2,1,0:T(1,128)S(1)} %collective-permute-done.4.cll_ref) | copy-start | bytes 724
  25.9 17.2 %collective-permute-start.5 = (f32[20,3,1,1]{3,2,1,0:T(1,128)S(1)}, f32[20,3,1,1]{3,2,1,0:T(1,128)S(1)}, u32[]{:S(2)}, u32[]{:S(2)}) collective-permute-start(f32[20,3,1,1]{3,2,1,0:T(1,128)S(1)} %pad_maximum_fusion.6), channel_id=1, source_target_pairs={{0,761},{1,762},{2,763},{3,764},{4,765},{5,766},{6,767},{8,1},{9,2... | collective-permute-start | bytes 728 | tf_op jit(solution)/shard_map/ppermute | solution.py:154
  37.7 7.5 %collective-permute-start.6 = (f32[20,3,1,1]{3,2,1,0:T(1,128)S(1)}, f32[20,3,1,1]{3,2,1,0:T(1,128)S(1)}, u32[]{:S(2)}, u32[]{:S(2)}) collective-permute-start(f32[20,3,1,1]{3,2,1,0:T(1,128)S(1)} %pad_maximum_fusion.7), channel_id=1, source_target_pairs={{1,8},{2,9},{3,10},{4,11},{5,12},{6,13},{7,14},{9,16},{10,17},{11,... | collective-permute-start | bytes 728 | tf_op jit(solution)/shard_map/ppermute | solution.py:155
  39.0 6.2 %collective-permute-start.7 = (f32[20,3,1,1]{3,2,1,0:T(1,128)S(1)}, f32[20,3,1,1]{3,2,1,0:T(1,128)S(1)}, u32[]{:S(2)}, u32[]{:S(2)}) collective-permute-start(f32[20,3,1,1]{3,2,1,0:T(1,128)S(1)} %pad_maximum_fusion.8), channel_id=1, source_target_pairs={{1,760},{2,761},{3,762},{4,763},{5,764},{6,765},{7,766},{9,0},{10,... | collective-permute-start | bytes 728 | tf_op jit(solution)/shard_map/ppermute | solution.py:156
  43.1 2.1 %copy-start.4 = (f32[20,3,1,1]{3,2,1,0:T(1,128)}, f32[20,3,1,1]{3,2,1,0:T(1,128)S(1)}, u32[]{:S(2)}) copy-start(f32[20,3,1,1]{3,2,1,0:T(1,128)S(1)} %collective-permute-done.5.chl_ref) | copy-start | bytes 724
  45.2 0.6 copy-start.5
  45.2 0.6 copy-start.6
  45.2 0.6 copy-start.2
  45.8 0.6 copy-start.3
  58.7 41.6 %copy-start.7 = (s32[6,128]{1,0:T(8,128)S(1)}, s32[6,128]{1,0:T(8,128)}, u32[]{:S(2)}) copy-start(s32[6,128]{1,0:T(8,128)} %param.15) | copy-start | bytes 9220
  58.7 41.6 %copy-start.11 = (f32[128]{0:T(128)S(1)}, f32[128]{0:T(128)}, u32[]{:S(2)}) copy-start(f32[128]{0:T(128)} %param.12) | copy-start | bytes 1540
  87.4 20.6 %copy-start.8 = (f32[6,128]{1,0:T(8,128)S(1)}, f32[6,128]{1,0:T(8,128)}, u32[]{:S(2)}) copy-start(f32[6,128]{1,0:T(8,128)} %param.14) | copy-start | bytes 9220
  87.4 20.6 %copy-start.12 = (f32[128]{0:T(128)S(1)}, f32[128]{0:T(128)}, u32[]{:S(2)}) copy-start(f32[128]{0:T(128)} %param.13) | copy-start | bytes 1540
  88.1 18.8 %all-to-all-start.1 = ((f32[2,96,8,2]{1,3,0,2:T(2,128)}), f32[2,96,8,2]{1,3,0,2:T(2,128)S(1)}, u32[]{:S(2)}, u32[]{:S(2)}) async-start(f32[2,96,8,2]{1,3,0,2:T(2,128)} %copy.61), calls=%async_computation.1 | async-start | bytes 32768 | tf_op jit(solution)/shard_map/all_to_all | solution.py:186
  108.0 30.9 %copy-start.10 = (f32[128]{0:T(128)}, f32[128]{0:T(128)S(1)}, u32[]{:S(2)}) copy-start(f32[128]{0:T(128)S(1)} %fusion.17) | copy-start | bytes 1540

commit v5 on v4

--- a/solution.py
+++ b/solution.py
@@ -182,27 +182,19 @@
     send_zone = jnp.sum(jnp.where(placed, local_zone.astype(jnp.float32)[:, None], 0.0), axis=0)
     count_x = lax.axis_size("gx")
     count_y = lax.axis_size("gy")
-    outgoing = jnp.stack([send_flux, send_zone]).reshape(2, count_x, count_y, capacity)
-    arrived = lax.all_to_all(
-        lax.all_to_all(outgoing, "gx", split_axis=1, concat_axis=1, tiled=True),
-        "gy",
-        split_axis=2,
-        concat_axis=2,
-        tiled=True,
-    ).reshape(2, devices * capacity)
-    matched = arrived[1][None, :] == jnp.arange(zone_dev, dtype=jnp.float32)[:, None]
-    inflow = jnp.sum(jnp.where(matched, arrived[0][None, :], 0.0), axis=1)
+    outgoing = jnp.stack([send_flux, send_zone]).reshape(2, count_x, count_y * capacity)
+    arrived = lax.all_to_all(outgoing, "gx", split_axis=1, concat_axis=1, tiled=True)
+    arrived = arrived.reshape(2, count_x, count_y, capacity)
+    zones = jnp.arange(zone_dev, dtype=jnp.float32)
+    matched = arrived[1][..., None] == zones
+    gathered = jnp.sum(jnp.where(matched, arrived[0][..., None], 0.0), axis=(0, 2))
+    inflow = lax.psum_scatter(gathered, "gy", scatter_dimension=0, tiled=True).reshape(zone_dev)
     coupled, total = couple(old_pressure, leakage, conductance, neighbour)
     zone_pressure = (inflow + coupled) / total
-    answered = jnp.sum(jnp.where(matched, zone_pressure[:, None], 0.0), axis=0).reshape(
-        count_x, count_y, capacity
-    )
+    row_pressure = lax.all_gather(zone_pressure, "gy", axis=0, tiled=False)
+    answered = jnp.sum(jnp.where(matched, row_pressure[None, :, None, :], 0.0), axis=3)
     returned = lax.all_to_all(
-        lax.all_to_all(answered, "gx", split_axis=0, concat_axis=0, tiled=True),
-        "gy",
-        split_axis=1,
-        concat_axis=1,
-        tiled=True,
+        answered.reshape(count_x, count_y * capacity), "gx", split_axis=0, concat_axis=0, tiled=True
     ).reshape(-1)
     opening_pressure = jnp.sum(jnp.where(placed, returned[None, :], 0.0), axis=1)
     return (new_populations, zone_pressure, opening_pressure)

time: 141 us -> 144 us (1.021)
  waiting for transfers between devices: 8.39 us -> 14 us
  blocking collectives: 56.7 us -> 54.3 us
  other arithmetic: 3.92 us -> 6 us
  local copies, waits for them, and re-layouts: 14.5 us -> 12.9 us
    all_to_all x3 -> x1, blocking collectives: 56.7 us -> 24.5 us  [on_device(): lax.all_to_all(answered.reshape(count_x, count_y * capacity), 'gx', split...]
    unnamed x0 -> x1, blocking collectives: none -> 18.1 us
    all_gather x0 -> x1, blocking collectives: none -> 11.7 us  [on_device(): row_pressure = lax.all_gather(zone_pressure, 'gy', axis=0, tiled=False)]
    all_to_all x1, waiting for transfers between devices: 6.31 us -> 11.9 us  [on_device(): lax.all_to_all(outgoing, 'gx', split_axis=1, concat_axis=1, tiled=True)]
    unnamed x28 -> x31, local copies, waits for them, and re-layouts: 2.05 us -> 3.44 us
  transfers between devices with their start and end apart: 9 -> 9, of which waited for: 2 -> 2; matrix products, arithmetic and copies ran while one was open for 5% -> 6% of each run, Pallas kernels for 0% -> 0%
where the time goes in v5:
time: 144 us; the launch traced here: 143 us
  blocking collectives  54.3 us (38%)
  starting transfers between devices  43.9 us (30%)
  waiting for transfers between devices  14 us (10%)
  local copies, waits for them, and re-layouts  12.9 us (9%)
  matrix products  6.53 us (5%)
  other arithmetic  6 us (4%)
  Pallas kernels  4.22 us (3%)
    all_to_all x1, blocking collectives, on_device(): lax.all_to_all(answered.reshape(count_x, count_y * capacity), 'gx', split...  24.5 us
    unnamed x1, blocking collectives  18.1 us
    all_to_all x1, waiting for transfers between devices, on_device(): lax.all_to_all(outgoing, 'gx', split_axis=1, concat_axis=1, tiled=True)  11.9 us
    ppermute x1, starting transfers between devices, exchange_halos(): c_hl = lax.ppermute(corner[0, -1], both, diagonal(-1, 1))  11.7 us
    all_gather x1, blocking collectives, on_device(): row_pressure = lax.all_gather(zone_pressure, 'gy', axis=0, tiled=False)  11.7 us
    all_to_all x1, starting transfers between devices, on_device(): lax.all_to_all(outgoing, 'gx', split_axis=1, concat_axis=1, tiled=True)  11.4 us
    dot_general x1, matrix products, patch_sums(): jnp.einsum('hry,ryl->hl', picked, onehot, precision=lax.Precision.HIGHEST)  6.53 us
    ppermute x1, starting transfers between devices, exchange_halos(): x_high = lax.ppermute(stacked_x[0], 'gx', ring_down)  5.98 us
  transfers between devices with their start and end apart: 9, of which 2 were waited for; matrix products, arithmetic and copies ran while one was open for 6% of the time, Pallas kernels for 0%

profile of v5, /device:TPU:1, one launch (start us, length us, event | category | flops | bytes accessed | tf_op | source)
XLA Modules:
  0.0 143.0 jit_solution(7853622931367920274)
XLA Ops:
  0.6 0.8 subtract_convert_fusion
  1.5 1.5 %fusion.23 = (f32[19,3,1,1]{3,2,1,0:T(1,128)S(1)}, f32[19,3,1,1]{3,2,1,0:T(1,128)S(1)}, f32[19,3,1,1]{3,2,1,0:T(1,128)S(1)}, f32[19,3,1,1]{3,2,1,0:T(1,128)S(1)}) fusion(f32[19,3,32,128]{3,2,1,0:T(8,128)} %pop_ref.1), kind=kLoop, calls=%fused_computation.83 | loop fusion | bytes 1824 | tf_op jit(solution)/shard_map/slice | solution.py:130
  3.0 5.5 %collective-permute-start.4 = (f32[20,3,1,1]{3,2,1,0:T(1,128)S(1)}, f32[20,3,1,1]{3,2,1,0:T(1,128)S(1)}, u32[]{:S(2)}, u32[]{:S(2)}) collective-permute-start(f32[20,3,1,1]{3,2,1,0:T(1,128)S(1)} %pad_maximum_fusion.5), channel_id=1, source_target_pairs={{0,9},{1,10},{2,11},{3,12},{4,13},{5,14},{6,15},{8,17},{9,18},{10,... | collective-permute-start | bytes 728 | tf_op jit(solution)/shard_map/ppermute | solution.py:153
  8.7 1.9 %fusion.24 = (f32[19,3,32,1]{3,2,1,0:T(8,128)S(1)}, f32[19,3,32,1]{3,2,1,0:T(8,128)S(1)}) fusion(f32[19,3,32,128]{3,2,1,0:T(8,128)} %pop_ref.1), kind=kLoop, calls=%fused_computation.84 | loop fusion | bytes 29184 | tf_op jit(solution)/shard_map/slice | solution.py:125
  11.1 3.2 %collective-permute-start.2 = (f32[20,3,32,1]{2,3,1,0:T(1,128)S(1)}, f32[20,3,32,1]{2,3,1,0:T(1,128)S(1)}, u32[]{:S(2)}, u32[]{:S(2)}) collective-permute-start(f32[20,3,32,1]{2,3,1,0:T(1,128)S(1)} %pad_maximum_fusion.3), channel_id=1, source_target_pairs={{0,1},{1,2},{2,3},{3,4},{4,5},{5,6},{6,7},{8,9},{9,10},{10,11},{11... | collective-permute-start | bytes 23048 | tf_op jit(solution)/shard_map/ppermute | solution.py:151
  14.7 1.3 collective-permute-start.3
  16.0 1.1 fusion.25
  17.2 2.2 %collective-permute-start = (f32[20,3,1,128]{3,2,1,0:T(1,128)S(1)}, f32[20,3,1,128]{3,2,1,0:T(1,128)S(1)}, u32[]{:S(2)}, u32[]{:S(2)}) collective-permute-start(f32[20,3,1,128]{3,2,1,0:T(1,128)S(1)} %pad_maximum_fusion.1), channel_id=1, source_target_pairs={{0,8},{8,16},{16,24},{24,32},{32,40},{40,48},{48,56},{56,64},{64,7... | collective-permute-start | bytes 92168 | tf_op jit(solution)/shard_map/ppermute | solution.py:149
  19.4 6.0 %collective-permute-start.1 = (f32[20,3,1,128]{3,2,1,0:T(1,128)S(1)}, f32[20,3,1,128]{3,2,1,0:T(1,128)S(1)}, u32[]{:S(2)}, u32[]{:S(2)}) collective-permute-start(f32[20,3,1,128]{3,2,1,0:T(1,128)S(1)} %pad_maximum_fusion.2), channel_id=1, source_target_pairs={{8,0},{16,8},{24,16},{32,24},{40,32},{48,40},{56,48},{64,56},{72,6... | collective-permute-start | bytes 92168 | tf_op jit(solution)/shard_map/ppermute | solution.py:150
  25.9 11.7 %collective-permute-start.5 = (f32[20,3,1,1]{3,2,1,0:T(1,128)S(1)}, f32[20,3,1,1]{3,2,1,0:T(1,128)S(1)}, u32[]{:S(2)}, u32[]{:S(2)}) collective-permute-start(f32[20,3,1,1]{3,2,1,0:T(1,128)S(1)} %pad_maximum_fusion.6), channel_id=1, source_target_pairs={{0,761},{1,762},{2,763},{3,764},{4,765},{5,766},{6,767},{8,1},{9,2... | collective-permute-start | bytes 728 | tf_op jit(solution)/shard_map/ppermute | solution.py:154
  37.7 1.3 collective-permute-start.6
  39.0 1.3 collective-permute-start.7
  40.3 1.4 copy.62.ylo_ref
  41.7 1.4 copy.63.yhi_ref
  43.1 2.1 %collective-permute-done.6.clh_ref = f32[20,3,1,1]{3,2,1,0:T(1,128)S(1)} collective-permute-done((f32[20,3,1,1]{3,2,1,0:T(1,128)S(1)}, f32[20,3,1,1]{3,2,1,0:T(1,128)S(1)}, u32[]{:S(2)}, u32[]{:S(2)}) %collective-permute-start.6) | collective-permute-done | bytes 272 | tf_op jit(solution)/shard_map/ppermute | solution.py:155
  45.2 0.6 copy-done.5
  45.8 0.6 copy-done.3
  46.4 4.2 %shard_map.103 = (f32[19,3,32,128]{3,2,1,0:T(8,128)}, f32[3,32,128]{2,1,0:T(8,128)}) custom-call(f32[19,3,32,128]{3,2,1,0:T(8,128)} %pop_ref.1, s32[3,32,128]{2,1,0:T(8,128)} %solid_ref.1, f32[20,3,1,128]{3,2,1,0:T(1,128)} %copy-done.2, f32[20,3,1,128]{3,2,1,0:T(1,128)} %copy-done.3, f32[20,3,32,1]{3,2,1,0:T(8,128)} %copy.62.ylo_ref, ...), custom_call_target="tpu_custom_call" | custom-call | tf_op jit(solution)/shard_map/pallas_call | solution.py:358
  50.6 6.5 %fusion.4 = f32[512]{0:T(512)S(1)} fusion(s32[96,128]{1,0:T(8,128)S(1)} %get-tuple-element.24, f32[96,128]{1,0:T(8,128)} %bitcast.125, s32[96,128]{1,0:T(8,128)S(1)} %get-tuple-element.23), kind=kOutput, calls=%fused_computation.9 | convolution fusion | flops 77169152 | bytes 149504 | tf_op jit(solution)/shard_map/hry,ryl->hl/dot_general | solution.py:218
  57.2 0.8 select_reduce_fusion.2
  58.2 0.7 copy.64
  58.9 11.4 %all-to-all-start = ((f32[2,96,16]{2,0,1:T(2,128)}), f32[2,96,16]{2,0,1:T(2,128)S(1)}, u32[]{:S(2)}, u32[]{:S(2)}) async-start(f32[2,96,16]{2,0,1:T(2,128)} %copy.64), calls=%async_computation | async-start | bytes 196608 | tf_op jit(solution)/shard_map/all_to_all | solution.py:186
  70.6 1.3 dynamic-slice
  71.9 11.9 %all-to-all-done = f32[2,96,16]{2,0,1:T(2,128)S(1)} async-done(((f32[2,96,16]{2,0,1:T(2,128)}), f32[2,96,16]{2,0,1:T(2,128)S(1)}, u32[]{:S(2)}, u32[]{:S(2)}) %all-to-all-start) | async-done | bytes 12320 | tf_op jit(solution)/shard_map/all_to_all | solution.py:186
  84.8 18.1 %all-reduce = f32[8,128]{1,0:T(8,128)S(1)} all-reduce(f32[8,128]{1,0:T(8,128)S(1)} %select_reduce_fusion.4), channel_id=3, replica_groups=mesh['gx'=96,'gy'=8] {'gy'}, use_global_device_ids=true, to_apply=%region_4.5.clone | all-reduce | flops 1024 | bytes 8192
  102.9 0.7 fusion.16
  103.6 11.7 %all-gather.1 = f32[8,1,128]{2,1,0:T(1,128)S(1)} all-gather(f32[1,1,128]{2,1,0:T(1,128)S(1)} %bitcast.124), channel_id=2, replica_groups=mesh['gx'=96,'gy'=8] {'gy'}, dimensions={0}, use_global_device_ids=true | all-gather | bytes 4608 | tf_op jit(solution)/shard_map/all_gather | solution.py:194
  115.3 0.6 select_reduce_fusion.3
  116.0 24.5 %all_to_all.14 = f32[96,1,16]{2,1,0:T(1,128)S(1)} all-to-all(f32[96,1,16]{2,1,0:T(1,128)S(1)} %copy.70), channel_id=1, replica_groups=mesh['gx'=96,'gy'=8] {'gx'}, dimensions={0} | all-to-all | bytes 12288 | tf_op jit(solution)/shard_map/all_to_all | solution.py:196
  140.6 0.5 broadcast.102
  141.1 0.8 reduce.7
  141.9 1.1 select_reduce_fusion
  (63 shorter events, 3.4 us)
Async XLA Ops:
  3.0 22.8 %collective-permute-start.4 = (f32[20,3,1,1]{3,2,1,0:T(1,128)S(1)}, f32[20,3,1,1]{3,2,1,0:T(1,128)S(1)}, u32[]{:S(2)}, u32[]{:S(2)}) collective-permute-start(f32[20,3,1,1]{3,2,1,0:T(1,128)S(1)} %pad_maximum_fusion.5), channel_id=1, source_target_pairs={{0,9},{1,10},{2,11},{3,12},{4,13},{5,14},{6,15},{8,17},{9,18},{10,... | collective-permute-start | bytes 728 | tf_op jit(solution)/shard_map/ppermute | solution.py:153
  10.6 14.8 %copy-start = (s32[3,32,128]{2,1,0:T(8,128)S(1)}, s32[3,32,128]{2,1,0:T(8,128)}, u32[]{:S(2)}) copy-start(s32[3,32,128]{2,1,0:T(8,128)} %param.10) | copy-start | bytes 147460
  11.0 14.5 %copy-start.9 = (s32[512]{0:T(512)S(1)}, s32[512]{0:T(512)}, u32[]{:S(2)}) copy-start(s32[512]{0:T(512)} %param.11) | copy-start | bytes 6148
  11.1 26.6 %collective-permute-start.2 = (f32[20,3,32,1]{2,3,1,0:T(1,128)S(1)}, f32[20,3,32,1]{2,3,1,0:T(1,128)S(1)}, u32[]{:S(2)}, u32[]{:S(2)}) collective-permute-start(f32[20,3,32,1]{2,3,1,0:T(1,128)S(1)} %pad_maximum_fusion.3), channel_id=1, source_target_pairs={{0,1},{1,2},{2,3},{3,4},{4,5},{5,6},{6,7},{8,9},{9,10},{10,11},{11... | collective-permute-start | bytes 23048 | tf_op jit(solution)/shard_map/ppermute | solution.py:151
  14.7 24.2 %collective-permute-start.3 = (f32[20,3,32,1]{2,3,1,0:T(1,128)S(1)}, f32[20,3,32,1]{2,3,1,0:T(1,128)S(1)}, u32[]{:S(2)}, u32[]{:S(2)}) collective-permute-start(f32[20,3,32,1]{2,3,1,0:T(1,128)S(1)} %pad_maximum_fusion.4), channel_id=1, source_target_pairs={{1,0},{2,1},{3,2},{4,3},{5,4},{6,5},{7,6},{9,8},{10,9},{11,10},{12... | collective-permute-start | bytes 23048 | tf_op jit(solution)/shard_map/ppermute | solution.py:152
  17.2 28.0 %collective-permute-start = (f32[20,3,1,128]{3,2,1,0:T(1,128)S(1)}, f32[20,3,1,128]{3,2,1,0:T(1,128)S(1)}, u32[]{:S(2)}, u32[]{:S(2)}) collective-permute-start(f32[20,3,1,128]{3,2,1,0:T(1,128)S(1)} %pad_maximum_fusion.1), channel_id=1, source_target_pairs={{0,8},{8,16},{16,24},{24,32},{32,40},{40,48},{48,56},{56,64},{64,7... | collective-permute-start | bytes 92168 | tf_op jit(solution)/shard_map/ppermute | solution.py:149
  19.4 25.8 %collective-permute-start.1 = (f32[20,3,1,128]{3,2,1,0:T(1,128)S(1)}, f32[20,3,1,128]{3,2,1,0:T(1,128)S(1)}, u32[]{:S(2)}, u32[]{:S(2)}) collective-permute-start(f32[20,3,1,128]{3,2,1,0:T(1,128)S(1)} %pad_maximum_fusion.2), channel_id=1, source_target_pairs={{8,0},{16,8},{24,16},{32,24},{40,32},{48,40},{56,48},{64,56},{72,6... | collective-permute-start | bytes 92168 | tf_op jit(solution)/shard_map/ppermute | solution.py:150
  25.9 17.2 %copy-start.1 = (f32[20,3,1,1]{3,2,1,0:T(1,128)}, f32[20,3,1,1]{3,2,1,0:T(1,128)S(1)}, u32[]{:S(2)}) copy-start(f32[20,3,1,1]{3,2,1,0:T(1,128)S(1)} %collective-permute-done.4.cll_ref) | copy-start | bytes 724
  25.9 17.2 %collective-permute-start.5 = (f32[20,3,1,1]{3,2,1,0:T(1,128)S(1)}, f32[20,3,1,1]{3,2,1,0:T(1,128)S(1)}, u32[]{:S(2)}, u32[]{:S(2)}) collective-permute-start(f32[20,3,1,1]{3,2,1,0:T(1,128)S(1)} %pad_maximum_fusion.6), channel_id=1, source_target_pairs={{0,761},{1,762},{2,763},{3,764},{4,765},{5,766},{6,767},{8,1},{9,2... | collective-permute-start | bytes 728 | tf_op jit(solution)/shard_map/ppermute | solution.py:154
  37.7 7.5 %collective-permute-start.6 = (f32[20,3,1,1]{3,2,1,0:T(1,128)S(1)}, f32[20,3,1,1]{3,2,1,0:T(1,128)S(1)}, u32[]{:S(2)}, u32[]{:S(2)}) collective-permute-start(f32[20,3,1,1]{3,2,1,0:T(1,128)S(1)} %pad_maximum_fusion.7), channel_id=1, source_target_pairs={{1,8},{2,9},{3,10},{4,11},{5,12},{6,13},{7,14},{9,16},{10,17},{11,... | collective-permute-start | bytes 728 | tf_op jit(solution)/shard_map/ppermute | solution.py:155
  39.0 6.2 %collective-permute-start.7 = (f32[20,3,1,1]{3,2,1,0:T(1,128)S(1)}, f32[20,3,1,1]{3,2,1,0:T(1,128)S(1)}, u32[]{:S(2)}, u32[]{:S(2)}) collective-permute-start(f32[20,3,1,1]{3,2,1,0:T(1,128)S(1)} %pad_maximum_fusion.8), channel_id=1, source_target_pairs={{1,760},{2,761},{3,762},{4,763},{5,764},{6,765},{7,766},{9,0},{10,... | collective-permute-start | bytes 728 | tf_op jit(solution)/shard_map/ppermute | solution.py:156
  43.1 2.1 %copy-start.4 = (f32[20,3,1,1]{3,2,1,0:T(1,128)}, f32[20,3,1,1]{3,2,1,0:T(1,128)S(1)}, u32[]{:S(2)}) copy-start(f32[20,3,1,1]{3,2,1,0:T(1,128)S(1)} %collective-permute-done.5.chl_ref) | copy-start | bytes 724
  45.2 0.6 copy-start.5
  45.2 0.6 copy-start.6
  45.2 0.6 copy-start.2
  45.8 0.6 copy-start.3
  50.6 19.6 %copy-start.7 = (s32[6,128]{1,0:T(8,128)S(1)}, s32[6,128]{1,0:T(8,128)}, u32[]{:S(2)}) copy-start(s32[6,128]{1,0:T(8,128)} %param.15) | copy-start | bytes 9220
  50.6 19.6 %copy-start.11 = (f32[128]{0:T(128)S(1)}, f32[128]{0:T(128)}, u32[]{:S(2)}) copy-start(f32[128]{0:T(128)} %param.12) | copy-start | bytes 1540
  57.2 45.7 %copy-start.8 = (f32[6,128]{1,0:T(8,128)S(1)}, f32[6,128]{1,0:T(8,128)}, u32[]{:S(2)}) copy-start(f32[6,128]{1,0:T(8,128)} %param.14) | copy-start | bytes 9220
  57.2 45.7 %copy-start.12 = (f32[128]{0:T(128)S(1)}, f32[128]{0:T(128)}, u32[]{:S(2)}) copy-start(f32[128]{0:T(128)} %param.13) | copy-start | bytes 1540
  58.9 24.9 %all-to-all-start = ((f32[2,96,16]{2,0,1:T(2,128)}), f32[2,96,16]{2,0,1:T(2,128)S(1)}, u32[]{:S(2)}, u32[]{:S(2)}) async-start(f32[2,96,16]{2,0,1:T(2,128)} %copy.64), calls=%async_computation | async-start | bytes 196608 | tf_op jit(solution)/shard_map/all_to_all | solution.py:186
  103.6 39.4 %copy-start.10 = (f32[128]{0:T(128)}, f32[128]{0:T(128)S(1)}, u32[]{:S(2)}) copy-start(f32[128]{0:T(128)S(1)} %fusion.16) | copy-start | bytes 1540

commit v6 on v4

--- a/solution.py
+++ b/solution.py
@@ -217,14 +217,21 @@
     high = patch // lanes
     low = patch - high * lanes
     groups = openings // lanes
+    upper = lax.reduce_precision(momentum, exponent_bits=8, mantissa_bits=7)
+    rest = momentum - upper
+    middle = lax.reduce_precision(rest, exponent_bits=8, mantissa_bits=7)
+    lower = rest - middle
+    parts = jnp.stack([upper, middle, lower])
     picked = jnp.where(
-        high[None] == jnp.arange(groups, dtype=jnp.int32)[:, None, None], momentum[None], 0.0
+        high[None, None] == jnp.arange(groups, dtype=jnp.int32)[None, :, None, None],
+        parts[:, None],
+        0.0,
+    ).astype(jnp.bfloat16)
+    onehot = (low[:, :, None] == jnp.arange(lanes, dtype=jnp.int32)[None, None, :]).astype(
+        jnp.bfloat16
     )
-    onehot = (low[:, :, None] == jnp.arange(lanes, dtype=jnp.int32)[None, None, :]).astype(
-        jnp.float32
-    )
-    sums = jnp.einsum("hry,ryl->hl", picked, onehot, precision=lax.Precision.HIGHEST)
-    return FACE_AREA * sums.reshape(openings)
+    sums = jnp.einsum("khry,ryl->khl", picked, onehot, preferred_element_type=jnp.float32)
+    return FACE_AREA * (sums[0] + sums[1] + sums[2]).reshape(openings)
 
 
 def couple(old_pressure, leakage, conductance, neighbour):

time: 141 us -> 137 us (0.972)
  matrix products: 6.52 us -> 1.97 us
    dot_general x1, matrix products: 6.52 us -> 1.97 us  [patch_sums(): jnp.einsum('khry,ryl->khl', picked, onehot, preferred_element_type=jnp.fl...]
  transfers between devices with their start and end apart: 9 -> 9, of which waited for: 2 -> 2; matrix products, arithmetic and copies ran while one was open for 5% -> 6% of each run, Pallas kernels for 0% -> 0%
where the time goes in v6:
time: 137 us; the launch traced here: 136 us
  blocking collectives  56.7 us (41%)
  starting transfers between devices  44.7 us (33%)
  local copies, waits for them, and re-layouts  14.5 us (11%)
  waiting for transfers between devices  8.39 us (6%)
  other arithmetic  4.82 us (4%)
  Pallas kernels  4.22 us (3%)
  matrix products  1.97 us (1%)
    all_to_all x1, blocking collectives, on_device(): lax.all_to_all(outgoing, 'gx', split_axis=1, concat_axis=1, tiled=True)  27.5 us
    all_to_all x1, blocking collectives, on_device(): lax.all_to_all(answered, 'gx', split_axis=0, concat_axis=0, tiled=True)  20.2 us
    all_to_all x1, starting transfers between devices, on_device(): lax.all_to_all(lax.all_to_all(outgoing, 'gx', split_axis=1, concat_axis=1...  12.2 us
    ppermute x1, starting transfers between devices, exchange_halos(): c_hl = lax.ppermute(corner[0, -1], both, diagonal(-1, 1))  11.7 us
    all_to_all x1, blocking collectives, on_device(): lax.all_to_all(lax.all_to_all(answered, 'gx', split_axis=0, concat_axis=0...  8.94 us
    all_to_all x1, waiting for transfers between devices, on_device(): lax.all_to_all(lax.all_to_all(outgoing, 'gx', split_axis=1, concat_axis=1...  6.31 us
    ppermute x1, starting transfers between devices, exchange_halos(): x_high = lax.ppermute(stacked_x[0], 'gx', ring_down)  5.98 us
    ppermute x1, starting transfers between devices, exchange_halos(): c_ll = lax.ppermute(corner[-1, -1], both, diagonal(1, 1))  5.51 us
  transfers between devices with their start and end apart: 9, of which 2 were waited for; matrix products, arithmetic and copies ran while one was open for 6% of the time, Pallas kernels for 0%

profile of v6, /device:TPU:1, one launch (start us, length us, event | category | flops | bytes accessed | tf_op | source)
XLA Modules:
  0.0 136.3 jit_solution(7768561405350170481)
XLA Ops:
  0.6 0.8 subtract_convert_fusion
  1.5 1.5 %fusion.28 = (f32[19,3,1,1]{3,2,1,0:T(1,128)S(1)}, f32[19,3,1,1]{3,2,1,0:T(1,128)S(1)}, f32[19,3,1,1]{3,2,1,0:T(1,128)S(1)}, f32[19,3,1,1]{3,2,1,0:T(1,128)S(1)}) fusion(f32[19,3,32,128]{3,2,1,0:T(8,128)} %pop_ref.1), kind=kLoop, calls=%fused_computation.90 | loop fusion | bytes 1824 | tf_op jit(solution)/shard_map/slice | solution.py:130
  3.0 5.5 %collective-permute-start.4 = (f32[20,3,1,1]{3,2,1,0:T(1,128)S(1)}, f32[20,3,1,1]{3,2,1,0:T(1,128)S(1)}, u32[]{:S(2)}, u32[]{:S(2)}) collective-permute-start(f32[20,3,1,1]{3,2,1,0:T(1,128)S(1)} %pad_maximum_fusion.6), channel_id=1, source_target_pairs={{0,9},{1,10},{2,11},{3,12},{4,13},{5,14},{6,15},{8,17},{9,18},{10,... | collective-permute-start | bytes 728 | tf_op jit(solution)/shard_map/ppermute | solution.py:153
  8.7 1.9 %fusion.29 = (f32[19,3,32,1]{3,2,1,0:T(8,128)S(1)}, f32[19,3,32,1]{3,2,1,0:T(8,128)S(1)}) fusion(f32[19,3,32,128]{3,2,1,0:T(8,128)} %pop_ref.1), kind=kLoop, calls=%fused_computation.91 | loop fusion | bytes 29184 | tf_op jit(solution)/shard_map/slice | solution.py:125
  10.6 0.4 copy.68
  11.1 3.2 %collective-permute-start.2 = (f32[20,3,32,1]{2,3,1,0:T(1,128)S(1)}, f32[20,3,32,1]{2,3,1,0:T(1,128)S(1)}, u32[]{:S(2)}, u32[]{:S(2)}) collective-permute-start(f32[20,3,32,1]{2,3,1,0:T(1,128)S(1)} %pad_maximum_fusion.4), channel_id=1, source_target_pairs={{0,1},{1,2},{2,3},{3,4},{4,5},{5,6},{6,7},{8,9},{9,10},{10,11},{11... | collective-permute-start | bytes 23048 | tf_op jit(solution)/shard_map/ppermute | solution.py:151
  14.3 0.4 copy.69
  14.7 1.3 collective-permute-start.3
  16.0 1.1 fusion.30
  17.2 2.2 %collective-permute-start = (f32[20,3,1,128]{3,2,1,0:T(1,128)S(1)}, f32[20,3,1,128]{3,2,1,0:T(1,128)S(1)}, u32[]{:S(2)}, u32[]{:S(2)}) collective-permute-start(f32[20,3,1,128]{3,2,1,0:T(1,128)S(1)} %pad_maximum_fusion.2), channel_id=1, source_target_pairs={{0,8},{8,16},{16,24},{24,32},{32,40},{40,48},{48,56},{56,64},{64,7... | collective-permute-start | bytes 92168 | tf_op jit(solution)/shard_map/ppermute | solution.py:149
  19.4 6.0 %collective-permute-start.1 = (f32[20,3,1,128]{3,2,1,0:T(1,128)S(1)}, f32[20,3,1,128]{3,2,1,0:T(1,128)S(1)}, u32[]{:S(2)}, u32[]{:S(2)}) collective-permute-start(f32[20,3,1,128]{3,2,1,0:T(1,128)S(1)} %pad_maximum_fusion.3), channel_id=1, source_target_pairs={{8,0},{16,8},{24,16},{32,24},{40,32},{48,40},{56,48},{64,56},{72,6... | collective-permute-start | bytes 92168 | tf_op jit(solution)/shard_map/ppermute | solution.py:150
  26.0 11.7 %collective-permute-start.5 = (f32[20,3,1,1]{3,2,1,0:T(1,128)S(1)}, f32[20,3,1,1]{3,2,1,0:T(1,128)S(1)}, u32[]{:S(2)}, u32[]{:S(2)}) collective-permute-start(f32[20,3,1,1]{3,2,1,0:T(1,128)S(1)} %pad_maximum_fusion.7), channel_id=1, source_target_pairs={{0,761},{1,762},{2,763},{3,764},{4,765},{5,766},{6,767},{8,1},{9,2... | collective-permute-start | bytes 728 | tf_op jit(solution)/shard_map/ppermute | solution.py:154
  37.7 1.3 collective-permute-start.6
  39.0 1.3 collective-permute-start.7
  40.3 1.4 %copy.58.ylo_ref = f32[20,3,32,1]{3,2,1,0:T(8,128)} copy(f32[20,3,32,1]{2,3,1,0:T(1,128)S(1)} %collective-permute-done.2) | data formatting | bytes 15360 | tf_op jit(solution)/shard_map/ppermute | solution.py:151
  41.7 1.4 %copy.59.yhi_ref = f32[20,3,32,1]{3,2,1,0:T(8,128)} copy(f32[20,3,32,1]{2,3,1,0:T(1,128)S(1)} %collective-permute-done.3) | data formatting | bytes 15360 | tf_op jit(solution)/shard_map/ppermute | solution.py:152
  43.2 2.1 %collective-permute-done.6.clh_ref = f32[20,3,1,1]{3,2,1,0:T(1,128)S(1)} collective-permute-done((f32[20,3,1,1]{3,2,1,0:T(1,128)S(1)}, f32[20,3,1,1]{3,2,1,0:T(1,128)S(1)}, u32[]{:S(2)}, u32[]{:S(2)}) %collective-permute-start.6) | collective-permute-done | bytes 272 | tf_op jit(solution)/shard_map/ppermute | solution.py:155
  45.3 0.6 copy-done.5
  45.9 0.6 copy-done.3
  46.5 4.2 %shard_map.103 = (f32[19,3,32,128]{3,2,1,0:T(8,128)}, f32[3,32,128]{2,1,0:T(8,128)}) custom-call(f32[19,3,32,128]{3,2,1,0:T(8,128)} %pop_ref.1, s32[3,32,128]{2,1,0:T(8,128)} %solid_ref.1, f32[20,3,1,128]{3,2,1,0:T(1,128)} %copy-done.2, f32[20,3,1,128]{3,2,1,0:T(1,128)} %copy-done.3, f32[20,3,32,1]{3,2,1,0:T(8,128)} %copy.58.ylo_ref, ...), custom_call_target="tpu_custom_call" | custom-call | tf_op jit(solution)/shard_map/pallas_call | solution.py:373
  50.7 0.8 bitcast_reduce-precision_fusion
  51.5 2.0 %fusion.4 = f32[3,4,128]{2,1,0:T(4,128)S(1)} fusion(s32[96,128]{1,0:T(8,128)S(1)} %get-tuple-element.22, bf16[3,96,128]{2,1,0:T(8,128)(2,1)S(1)} %pad_maximum_fusion.1, pred[4,96,128]{2,0,1:T(4,128)(4,1)S(1)} %iota_compare_fusion.5), kind=kOutput, calls=%fused_computation.8 | convolution fusion | flops 39469056 | bytes 178176 | tf_op jit(solution)/shard_map/khry,ryl->khl/dot_general | solution.py:233
  53.5 0.8 select_reduce_fusion.2
  55.0 1.2 copy.60
  56.3 27.5 %all_to_all.20 = f32[2,96,8,2]{2,3,0,1:T(2,128)S(1)} all-to-all(f32[2,96,8,2]{2,3,0,1:T(2,128)S(1)} %copy.60), channel_id=1, replica_groups=mesh['gx'=96,'gy'=8] {'gx'}, dimensions={1} | all-to-all | bytes 24576 | tf_op jit(solution)/shard_map/all_to_all | solution.py:187
  83.8 0.7 copy.61
  84.5 12.2 %all-to-all-start.1 = ((f32[2,96,8,2]{1,3,0,2:T(2,128)}), f32[2,96,8,2]{1,3,0,2:T(2,128)S(1)}, u32[]{:S(2)}, u32[]{:S(2)}) async-start(f32[2,96,8,2]{1,3,0,2:T(2,128)} %copy.61), calls=%async_computation.1 | async-start | bytes 32768 | tf_op jit(solution)/shard_map/all_to_all | solution.py:186
  97.0 6.3 %all-to-all-done.1 = f32[2,96,8,2]{1,3,0,2:T(2,128)S(1)} async-done(((f32[2,96,8,2]{1,3,0,2:T(2,128)}), f32[2,96,8,2]{1,3,0,2:T(2,128)S(1)}, u32[]{:S(2)}, u32[]{:S(2)}) %all-to-all-start.1) | async-done | bytes 12320 | tf_op jit(solution)/shard_map/all_to_all | solution.py:186
  104.9 0.6 copy.64
  105.5 20.2 %all_to_all.21 = f32[96,8,2]{1,2,0:T(2,128)S(1)} all-to-all(f32[96,8,2]{1,2,0:T(2,128)S(1)} %copy.64), channel_id=1, replica_groups=mesh['gx'=96,'gy'=8] {'gx'}, dimensions={0} | all-to-all | bytes 12288 | tf_op jit(solution)/shard_map/all_to_all | solution.py:201
  125.9 8.9 %all_to_all.22 = f32[96,8,2]{0,2,1:T(2,128)S(1)} all-to-all(f32[96,8,2]{0,2,1:T(2,128)S(1)} %copy.65), channel_id=1, replica_groups=mesh['gx'=96,'gy'=8] {'gy'}, dimensions={1} | all-to-all | bytes 12288 | tf_op jit(solution)/shard_map/all_to_all | solution.py:200
  135.3 1.1 select_reduce_fusion
  (67 shorter events, 4.1 us)
Async XLA Ops:
  3.0 22.9 %collective-permute-start.4 = (f32[20,3,1,1]{3,2,1,0:T(1,128)S(1)}, f32[20,3,1,1]{3,2,1,0:T(1,128)S(1)}, u32[]{:S(2)}, u32[]{:S(2)}) collective-permute-start(f32[20,3,1,1]{3,2,1,0:T(1,128)S(1)} %pad_maximum_fusion.6), channel_id=1, source_target_pairs={{0,9},{1,10},{2,11},{3,12},{4,13},{5,14},{6,15},{8,17},{9,18},{10,... | collective-permute-start | bytes 728 | tf_op jit(solution)/shard_map/ppermute | solution.py:153
  10.6 14.8 %copy-start = (s32[3,32,128]{2,1,0:T(8,128)S(1)}, s32[3,32,128]{2,1,0:T(8,128)}, u32[]{:S(2)}) copy-start(s32[3,32,128]{2,1,0:T(8,128)} %param.10) | copy-start | bytes 147460
  11.0 14.5 %copy-start.9 = (s32[512]{0:T(512)S(1)}, s32[512]{0:T(512)}, u32[]{:S(2)}) copy-start(s32[512]{0:T(512)} %param.11) | copy-start | bytes 6148
  11.1 26.7 %collective-permute-start.2 = (f32[20,3,32,1]{2,3,1,0:T(1,128)S(1)}, f32[20,3,32,1]{2,3,1,0:T(1,128)S(1)}, u32[]{:S(2)}, u32[]{:S(2)}) collective-permute-start(f32[20,3,32,1]{2,3,1,0:T(1,128)S(1)} %pad_maximum_fusion.4), channel_id=1, source_target_pairs={{0,1},{1,2},{2,3},{3,4},{4,5},{5,6},{6,7},{8,9},{9,10},{10,11},{11... | collective-permute-start | bytes 23048 | tf_op jit(solution)/shard_map/ppermute | solution.py:151
  14.7 24.3 %collective-permute-start.3 = (f32[20,3,32,1]{2,3,1,0:T(1,128)S(1)}, f32[20,3,32,1]{2,3,1,0:T(1,128)S(1)}, u32[]{:S(2)}, u32[]{:S(2)}) collective-permute-start(f32[20,3,32,1]{2,3,1,0:T(1,128)S(1)} %pad_maximum_fusion.5), channel_id=1, source_target_pairs={{1,0},{2,1},{3,2},{4,3},{5,4},{6,5},{7,6},{9,8},{10,9},{11,10},{12... | collective-permute-start | bytes 23048 | tf_op jit(solution)/shard_map/ppermute | solution.py:152
  17.2 28.1 %collective-permute-start = (f32[20,3,1,128]{3,2,1,0:T(1,128)S(1)}, f32[20,3,1,128]{3,2,1,0:T(1,128)S(1)}, u32[]{:S(2)}, u32[]{:S(2)}) collective-permute-start(f32[20,3,1,128]{3,2,1,0:T(1,128)S(1)} %pad_maximum_fusion.2), channel_id=1, source_target_pairs={{0,8},{8,16},{16,24},{24,32},{32,40},{40,48},{48,56},{56,64},{64,7... | collective-permute-start | bytes 92168 | tf_op jit(solution)/shard_map/ppermute | solution.py:149
  19.4 25.8 %collective-permute-start.1 = (f32[20,3,1,128]{3,2,1,0:T(1,128)S(1)}, f32[20,3,1,128]{3,2,1,0:T(1,128)S(1)}, u32[]{:S(2)}, u32[]{:S(2)}) collective-permute-start(f32[20,3,1,128]{3,2,1,0:T(1,128)S(1)} %pad_maximum_fusion.3), channel_id=1, source_target_pairs={{8,0},{16,8},{24,16},{32,24},{40,32},{48,40},{56,48},{64,56},{72,6... | collective-permute-start | bytes 92168 | tf_op jit(solution)/shard_map/ppermute | solution.py:150
  26.0 17.2 %copy-start.1 = (f32[20,3,1,1]{3,2,1,0:T(1,128)}, f32[20,3,1,1]{3,2,1,0:T(1,128)S(1)}, u32[]{:S(2)}) copy-start(f32[20,3,1,1]{3,2,1,0:T(1,128)S(1)} %collective-permute-done.4.cll_ref) | copy-start | bytes 724
  26.0 17.2 %collective-permute-start.5 = (f32[20,3,1,1]{3,2,1,0:T(1,128)S(1)}, f32[20,3,1,1]{3,2,1,0:T(1,128)S(1)}, u32[]{:S(2)}, u32[]{:S(2)}) collective-permute-start(f32[20,3,1,1]{3,2,1,0:T(1,128)S(1)} %pad_maximum_fusion.7), channel_id=1, source_target_pairs={{0,761},{1,762},{2,763},{3,764},{4,765},{5,766},{6,767},{8,1},{9,2... | collective-permute-start | bytes 728 | tf_op jit(solution)/shard_map/ppermute | solution.py:154
  37.7 7.5 %collective-permute-start.6 = (f32[20,3,1,1]{3,2,1,0:T(1,128)S(1)}, f32[20,3,1,1]{3,2,1,0:T(1,128)S(1)}, u32[]{:S(2)}, u32[]{:S(2)}) collective-permute-start(f32[20,3,1,1]{3,2,1,0:T(1,128)S(1)} %pad_maximum_fusion.8), channel_id=1, source_target_pairs={{1,8},{2,9},{3,10},{4,11},{5,12},{6,13},{7,14},{9,16},{10,17},{11,... | collective-permute-start | bytes 728 | tf_op jit(solution)/shard_map/ppermute | solution.py:155
  39.0 6.2 %collective-permute-start.7 = (f32[20,3,1,1]{3,2,1,0:T(1,128)S(1)}, f32[20,3,1,1]{3,2,1,0:T(1,128)S(1)}, u32[]{:S(2)}, u32[]{:S(2)}) collective-permute-start(f32[20,3,1,1]{3,2,1,0:T(1,128)S(1)} %pad_maximum_fusion.9), channel_id=1, source_target_pairs={{1,760},{2,761},{3,762},{4,763},{5,764},{6,765},{7,766},{9,0},{10,... | collective-permute-start | bytes 728 | tf_op jit(solution)/shard_map/ppermute | solution.py:156
  43.2 2.1 %copy-start.4 = (f32[20,3,1,1]{3,2,1,0:T(1,128)}, f32[20,3,1,1]{3,2,1,0:T(1,128)S(1)}, u32[]{:S(2)}) copy-start(f32[20,3,1,1]{3,2,1,0:T(1,128)S(1)} %collective-permute-done.5.chl_ref) | copy-start | bytes 724
  45.2 0.6 copy-start.5
  45.2 0.6 copy-start.6
  45.2 0.6 copy-start.2
  45.9 0.6 copy-start.3
  55.0 41.6 %copy-start.7 = (s32[6,128]{1,0:T(8,128)S(1)}, s32[6,128]{1,0:T(8,128)}, u32[]{:S(2)}) copy-start(s32[6,128]{1,0:T(8,128)} %param.15) | copy-start | bytes 9220
  55.0 41.6 %copy-start.11 = (f32[128]{0:T(128)S(1)}, f32[128]{0:T(128)}, u32[]{:S(2)}) copy-start(f32[128]{0:T(128)} %param.12) | copy-start | bytes 1540
  83.8 20.6 %copy-start.8 = (f32[6,128]{1,0:T(8,128)S(1)}, f32[6,128]{1,0:T(8,128)}, u32[]{:S(2)}) copy-start(f32[6,128]{1,0:T(8,128)} %param.14) | copy-start | bytes 9220
  83.8 20.6 %copy-start.12 = (f32[128]{0:T(128)S(1)}, f32[128]{0:T(128)}, u32[]{:S(2)}) copy-start(f32[128]{0:T(128)} %param.13) | copy-start | bytes 1540
  84.5 18.8 %all-to-all-start.1 = ((f32[2,96,8,2]{1,3,0,2:T(2,128)}), f32[2,96,8,2]{1,3,0,2:T(2,128)S(1)}, u32[]{:S(2)}, u32[]{:S(2)}) async-start(f32[2,96,8,2]{1,3,0,2:T(2,128)} %copy.61), calls=%async_computation.1 | async-start | bytes 32768 | tf_op jit(solution)/shard_map/all_to_all | solution.py:186
  104.4 30.9 %copy-start.10 = (f32[128]{0:T(128)}, f32[128]{0:T(128)S(1)}, u32[]{:S(2)}) copy-start(f32[128]{0:T(128)S(1)} %fusion.22) | copy-start | bytes 1540

commit v7 on v6

--- a/solution.py
+++ b/solution.py
@@ -117,44 +117,37 @@
 def exchange_halos(populations, fluid):
     count_x = lax.axis_size("gx")
     count_y = lax.axis_size("gy")
-    stacked_x = [
+    faces_x = [
         jnp.concatenate([populations[:, :, at, None, :], fluid[None, :, at, None, :]], axis=0)
         for at in (0, -1)
     ]
-    stacked_y = [
-        jnp.concatenate([populations[:, :, :, at, None], fluid[None, :, :, at, None]], axis=0)
+    x_low = lax.ppermute(faces_x[1], "gx", [(i, (i + 1) % count_x) for i in range(count_x)])
+    x_high = lax.ppermute(faces_x[0], "gx", [((i + 1) % count_x, i) for i in range(count_x)])
+    faces_y = [
+        jnp.concatenate(
+            [
+                x_low[:, :, :, at, None],
+                jnp.concatenate(
+                    [populations[:, :, :, at, None], fluid[None, :, :, at, None]], axis=0
+                ),
+                x_high[:, :, :, at, None],
+            ],
+            axis=2,
+        )
         for at in (0, -1)
     ]
-    corner = {
-        (cx, cy): jnp.concatenate(
-            [populations[:, :, cx, None, cy, None], fluid[None, :, cx, None, cy, None]], axis=0
-        )
-        for cx in (0, -1)
-        for cy in (0, -1)
-    }
-    ring_up = [(i, (i + 1) % count_x) for i in range(count_x)]
-    ring_down = [((i + 1) % count_x, i) for i in range(count_x)]
-    line_up = [(j, j + 1) for j in range(count_y - 1)]
-    line_down = [(j + 1, j) for j in range(count_y - 1)]
-
-    def diagonal(step_x, step_y):
-        pairs = []
-        for i in range(count_x):
-            for j in range(count_y):
-                if 0 <= j + step_y < count_y:
-                    pairs.append((i * count_y + j, ((i + step_x) % count_x) * count_y + j + step_y))
-        return pairs
-
-    both = ("gx", "gy")
-    x_low = lax.ppermute(stacked_x[1], "gx", ring_up)
-    x_high = lax.ppermute(stacked_x[0], "gx", ring_down)
-    y_low = lax.ppermute(stacked_y[1], "gy", line_up)
-    y_high = lax.ppermute(stacked_y[0], "gy", line_down)
-    c_ll = lax.ppermute(corner[(-1, -1)], both, diagonal(1, 1))
-    c_hl = lax.ppermute(corner[(0, -1)], both, diagonal(-1, 1))
-    c_lh = lax.ppermute(corner[(-1, 0)], both, diagonal(1, -1))
-    c_hh = lax.ppermute(corner[(0, 0)], both, diagonal(-1, -1))
-    return (x_low, x_high, y_low, y_high, c_ll, c_hl, c_lh, c_hh)
+    y_low = lax.ppermute(faces_y[1], "gy", [(j, j + 1) for j in range(count_y - 1)])
+    y_high = lax.ppermute(faces_y[0], "gy", [(j + 1, j) for j in range(count_y - 1)])
+    return (
+        x_low,
+        x_high,
+        y_low[:, :, 1:-1],
+        y_high[:, :, 1:-1],
+        y_low[:, :, :1],
+        y_low[:, :, -1:],
+        y_high[:, :, :1],
+        y_high[:, :, -1:],
+    )
 
 
 def on_device(

time: 137 us -> 119 us (0.87)
  starting transfers between devices: 44.7 us -> 27.4 us
  blocking collectives: 56.7 us -> 58.8 us
  waiting for transfers between devices: 8.39 us -> 6.32 us
    ppermute x8 -> x4, starting transfers between devices: 32.5 us -> 19.6 us  [the longest x1 9.81 us: exchange_halos(): lax.ppermute(faces_x[0], 'gx', [((i + 1) % count_x, i) for i in range(cou...]
    all_to_all x1, starting transfers between devices: 12.2 us -> 7.86 us  [on_device(): lax.all_to_all(lax.all_to_all(outgoing, 'gx', split_axis=1, concat_axis=1...]
    unnamed x28 -> x24, local copies, waits for them, and re-layouts: 2.03 us -> 5.18 us
    ppermute x2 -> x0, local copies, waits for them, and re-layouts: 2.82 us -> none  [the longest x1 1.44 us: exchange_halos(): y_high = lax.ppermute(stacked_y[0], 'gy', line_down)]
    all_to_all x1, blocking collectives: 27.5 us -> 29.6 us  [on_device(): lax.all_to_all(outgoing, 'gx', split_axis=1, concat_axis=1, tiled=True)]
    ppermute x8 -> x4, waiting for transfers between devices: 2.09 us -> 0.01 us  [the longest x1 0.01 us: exchange_halos(): lax.ppermute(faces_x[0], 'gx', [((i + 1) % count_x, i) for i in range(cou...]
  transfers between devices with their start and end apart: 9 -> 5, of which waited for: 2 -> 1; matrix products, arithmetic and copies ran while one was open for 6% -> 5% of each run, Pallas kernels for 0% -> 0%
where the time goes in v7:
time: 119 us
  blocking collectives  58.8 us (49%)
  starting transfers between devices  27.4 us (23%)
  local copies, waits for them, and re-layouts  13.8 us (12%)
  waiting for transfers between devices  6.32 us (5%)
  other arithmetic  4.99 us (4%)
  Pallas kernels  4.22 us (4%)
  matrix products  1.97 us (2%)
    all_to_all x1, blocking collectives, on_device(): lax.all_to_all(outgoing, 'gx', split_axis=1, concat_axis=1, tiled=True)  29.6 us
    all_to_all x1, blocking collectives, on_device(): lax.all_to_all(answered, 'gx', split_axis=0, concat_axis=0, tiled=True)  20.2 us
    ppermute x1, starting transfers between devices, exchange_halos(): lax.ppermute(faces_x[0], 'gx', [((i + 1) % count_x, i) for i in range(cou...  9.81 us
    all_to_all x1, blocking collectives, on_device(): lax.all_to_all(lax.all_to_all(answered, 'gx', split_axis=0, concat_axis=0...  8.94 us
    all_to_all x1, starting transfers between devices, on_device(): lax.all_to_all(lax.all_to_all(outgoing, 'gx', split_axis=1, concat_axis=1...  7.86 us
    all_to_all x1, waiting for transfers between devices, on_device(): lax.all_to_all(lax.all_to_all(outgoing, 'gx', split_axis=1, concat_axis=1...  6.31 us
    unnamed x24, local copies, waits for them, and re-layouts  5.18 us
    ppermute x1, starting transfers between devices, exchange_halos(): lax.ppermute(faces_x[1], 'gx', [(i, (i + 1) % count_x) for i in range(cou...  4.5 us
  transfers between devices with their start and end apart: 5, of which 1 were waited for; matrix products, arithmetic and copies ran while one was open for 5% of the time, Pallas kernels for 0%

profile of v7, /device:TPU:1, one launch (start us, length us, event | category | flops | bytes accessed | tf_op | source)
XLA Modules:
  0.0 118.5 jit_solution(2415109062324638202)
XLA Ops:
  0.6 0.8 subtract_convert_fusion
  1.4 1.1 fusion.29
  2.6 4.5 %collective-permute-start = (f32[20,3,1,128]{3,2,1,0:T(1,128)S(1)}, f32[20,3,1,128]{3,2,1,0:T(1,128)S(1)}, u32[]{:S(2)}, u32[]{:S(2)}) collective-permute-start(f32[20,3,1,128]{3,2,1,0:T(1,128)S(1)} %pad_maximum_fusion.2), channel_id=1, source_target_pairs={{0,8},{8,16},{16,24},{24,32},{32,40},{40,48},{48,56},{56,64},{64,7... | collective-permute-start | bytes 92168 | tf_op jit(solution)/shard_map/ppermute | solution.py:124
  7.1 9.8 %collective-permute-start.1 = (f32[20,3,1,128]{3,2,1,0:T(1,128)S(1)}, f32[20,3,1,128]{3,2,1,0:T(1,128)S(1)}, u32[]{:S(2)}, u32[]{:S(2)}) collective-permute-start(f32[20,3,1,128]{3,2,1,0:T(1,128)S(1)} %pad_maximum_fusion.3), channel_id=1, source_target_pairs={{8,0},{16,8},{24,16},{32,24},{40,32},{48,40},{56,48},{64,56},{72,6... | collective-permute-start | bytes 92168 | tf_op jit(solution)/shard_map/ppermute | solution.py:125
  17.1 1.9 %fusion.28 = (f32[19,3,32,1]{3,2,1,0:T(8,128)S(1)}, f32[19,3,32,1]{3,2,1,0:T(8,128)S(1)}) fusion(f32[19,3,32,128]{3,2,1,0:T(8,128)} %pop_ref.1), kind=kLoop, calls=%fused_computation.90 | loop fusion | bytes 29184 | tf_op jit(solution)/shard_map/slice | solution.py:131
  19.1 0.2 convert_reduce_fusion
  19.4 0.4 copy.62
  19.8 0.4 copy.60
  20.7 1.3 %collective-permute-start.3 = (f32[20,3,34,1]{2,3,1,0:T(1,128)S(1)}, f32[20,3,34,1]{2,3,1,0:T(1,128)S(1)}, u32[]{:S(2)}, u32[]{:S(2)}) collective-permute-start(f32[20,3,34,1]{2,3,1,0:T(1,128)S(1)} %pad_maximum_fusion.5), channel_id=1, source_target_pairs={{1,0},{2,1},{3,2},{4,3},{5,4},{6,5},{7,6},{9,8},{10,9},{11,10},{12... | collective-permute-start | bytes 24488 | tf_op jit(solution)/shard_map/ppermute | solution.py:140
  22.2 4.0 %collective-permute-start.2 = (f32[20,3,34,1]{2,3,1,0:T(1,128)S(1)}, f32[20,3,34,1]{2,3,1,0:T(1,128)S(1)}, u32[]{:S(2)}, u32[]{:S(2)}) collective-permute-start(f32[20,3,34,1]{2,3,1,0:T(1,128)S(1)} %pad_maximum_fusion.4), channel_id=1, source_target_pairs={{0,1},{1,2},{2,3},{3,4},{4,5},{5,6},{6,7},{8,9},{9,10},{10,11},{11... | collective-permute-start | bytes 24488 | tf_op jit(solution)/shard_map/ppermute | solution.py:139
  26.4 1.4 %copy.63.yhi_ref = f32[20,3,32,1]{3,2,1,0:T(8,128)} copy(f32[20,3,32,1]{2,3,1,0:T(1,128)S(1)} %slice.157) | data formatting | bytes 15360
  27.9 1.4 %copy.61.ylo_ref = f32[20,3,32,1]{3,2,1,0:T(8,128)} copy(f32[20,3,32,1]{2,3,1,0:T(1,128)S(1)} %slice.153) | data formatting | bytes 15360
  29.4 0.7 slice_bitcast_fusion
  30.1 0.7 slice_bitcast_fusion.2
  30.8 4.2 %shard_map.103 = (f32[19,3,32,128]{3,2,1,0:T(8,128)}, f32[3,32,128]{2,1,0:T(8,128)}) custom-call(f32[19,3,32,128]{3,2,1,0:T(8,128)} %pop_ref.1, s32[3,32,128]{2,1,0:T(8,128)} %solid_ref.1, f32[20,3,1,128]{3,2,1,0:T(1,128)} %copy-done, f32[20,3,1,128]{3,2,1,0:T(1,128)} %copy-done.1, f32[20,3,32,1]{3,2,1,0:T(8,128)} %copy.61.ylo_ref, ...), custom_call_target="tpu_custom_call" | custom-call | tf_op jit(solution)/shard_map/pallas_call | solution.py:366
  35.1 0.8 bitcast_reduce-precision_fusion
  35.9 2.0 %fusion.4 = f32[3,4,128]{2,1,0:T(4,128)S(1)} fusion(s32[96,128]{1,0:T(8,128)S(1)} %get-tuple-element.18, bf16[3,96,128]{2,1,0:T(8,128)(2,1)S(1)} %pad_maximum_fusion.1, pred[4,96,128]{2,0,1:T(4,128)(4,1)S(1)} %iota_compare_fusion.5), kind=kOutput, calls=%fused_computation.8 | convolution fusion | flops 39469056 | bytes 178176 | tf_op jit(solution)/shard_map/khry,ryl->khl/dot_general | solution.py:226
  37.9 0.8 select_reduce_fusion.2
  38.6 0.3 stack.16
  39.0 0.3 stack.17
  39.4 1.2 %copy.52 = f32[2,96,8,2]{2,3,0,1:T(2,128)S(1)} copy(f32[2,96,8,2]{3,2,1,0:T(8,128)S(1)} %pad_maximum_fusion) | data formatting | bytes 24576 | tf_op jit(solution)/shard_map/stack | solution.py:178
  40.6 29.6 %all_to_all.20 = f32[2,96,8,2]{2,3,0,1:T(2,128)S(1)} all-to-all(f32[2,96,8,2]{2,3,0,1:T(2,128)S(1)} %copy.52), channel_id=1, replica_groups=mesh['gx'=96,'gy'=8] {'gx'}, dimensions={1} | all-to-all | bytes 24576 | tf_op jit(solution)/shard_map/all_to_all | solution.py:180
  70.3 0.7 copy.53
  71.0 7.9 %all-to-all-start.1 = ((f32[2,96,8,2]{1,3,0,2:T(2,128)}), f32[2,96,8,2]{1,3,0,2:T(2,128)S(1)}, u32[]{:S(2)}, u32[]{:S(2)}) async-start(f32[2,96,8,2]{1,3,0,2:T(2,128)} %copy.53), calls=%async_computation.1 | async-start | bytes 32768 | tf_op jit(solution)/shard_map/all_to_all | solution.py:179
  78.8 0.3 select_reduce_fusion.5
  79.1 6.3 %all-to-all-done.1 = f32[2,96,8,2]{1,3,0,2:T(2,128)S(1)} async-done(((f32[2,96,8,2]{1,3,0,2:T(2,128)}), f32[2,96,8,2]{1,3,0,2:T(2,128)S(1)}, u32[]{:S(2)}, u32[]{:S(2)}) %all-to-all-start.1) | async-done | bytes 12320 | tf_op jit(solution)/shard_map/all_to_all | solution.py:179
  86.1 0.2 eq.97
  86.7 0.3 reshape.163
  87.1 0.6 copy.56
  87.7 20.2 %all_to_all.21 = f32[96,8,2]{1,2,0:T(2,128)S(1)} all-to-all(f32[96,8,2]{1,2,0:T(2,128)S(1)} %copy.56), channel_id=1, replica_groups=mesh['gx'=96,'gy'=8] {'gx'}, dimensions={0} | all-to-all | bytes 12288 | tf_op jit(solution)/shard_map/all_to_all | solution.py:194
  108.0 8.9 %all_to_all.22 = f32[96,8,2]{0,2,1:T(2,128)S(1)} all-to-all(f32[96,8,2]{0,2,1:T(2,128)S(1)} %copy.57), channel_id=1, replica_groups=mesh['gx'=96,'gy'=8] {'gy'}, dimensions={1} | all-to-all | bytes 12288 | tf_op jit(solution)/shard_map/all_to_all | solution.py:193
  117.4 1.1 select_reduce_fusion
  (51 shorter events, 2.9 us)
Async XLA Ops:
  2.6 17.6 %collective-permute-start = (f32[20,3,1,128]{3,2,1,0:T(1,128)S(1)}, f32[20,3,1,128]{3,2,1,0:T(1,128)S(1)}, u32[]{:S(2)}, u32[]{:S(2)}) collective-permute-start(f32[20,3,1,128]{3,2,1,0:T(1,128)S(1)} %pad_maximum_fusion.2), channel_id=1, source_target_pairs={{0,8},{8,16},{16,24},{24,32},{32,40},{40,48},{48,56},{56,64},{64,7... | collective-permute-start | bytes 92168 | tf_op jit(solution)/shard_map/ppermute | solution.py:124
  7.1 13.2 %collective-permute-start.1 = (f32[20,3,1,128]{3,2,1,0:T(1,128)S(1)}, f32[20,3,1,128]{3,2,1,0:T(1,128)S(1)}, u32[]{:S(2)}, u32[]{:S(2)}) collective-permute-start(f32[20,3,1,128]{3,2,1,0:T(1,128)S(1)} %pad_maximum_fusion.3), channel_id=1, source_target_pairs={{8,0},{16,8},{24,16},{32,24},{40,32},{48,40},{56,48},{64,56},{72,6... | collective-permute-start | bytes 92168 | tf_op jit(solution)/shard_map/ppermute | solution.py:125
  17.1 1.9 %copy-start.2 = (s32[3,32,128]{2,1,0:T(8,128)S(1)}, s32[3,32,128]{2,1,0:T(8,128)}, u32[]{:S(2)}) copy-start(s32[3,32,128]{2,1,0:T(8,128)} %param.10) | copy-start | bytes 147460
  17.1 2.0 %copy-start.5 = (s32[512]{0:T(512)S(1)}, s32[512]{0:T(512)}, u32[]{:S(2)}) copy-start(s32[512]{0:T(512)} %param.11) | copy-start | bytes 6148
  20.2 9.1 %copy-start = (f32[20,3,1,128]{3,2,1,0:T(1,128)}, f32[20,3,1,128]{3,2,1,0:T(1,128)S(1)}, u32[]{:S(2)}) copy-start(f32[20,3,1,128]{3,2,1,0:T(1,128)S(1)} %collective-permute-done.xlo_ref) | copy-start | bytes 92164
  20.4 9.0 %copy-start.1 = (f32[20,3,1,128]{3,2,1,0:T(1,128)}, f32[20,3,1,128]{3,2,1,0:T(1,128)S(1)}, u32[]{:S(2)}) copy-start(f32[20,3,1,128]{3,2,1,0:T(1,128)S(1)} %collective-permute-done.1.xhi_ref) | copy-start | bytes 92164
  20.7 5.5 %collective-permute-start.3 = (f32[20,3,34,1]{2,3,1,0:T(1,128)S(1)}, f32[20,3,34,1]{2,3,1,0:T(1,128)S(1)}, u32[]{:S(2)}, u32[]{:S(2)}) collective-permute-start(f32[20,3,34,1]{2,3,1,0:T(1,128)S(1)} %pad_maximum_fusion.5), channel_id=1, source_target_pairs={{1,0},{2,1},{3,2},{4,3},{5,4},{6,5},{7,6},{9,8},{10,9},{11,10},{12... | collective-permute-start | bytes 24488 | tf_op jit(solution)/shard_map/ppermute | solution.py:140
  22.2 5.6 %collective-permute-start.2 = (f32[20,3,34,1]{2,3,1,0:T(1,128)S(1)}, f32[20,3,34,1]{2,3,1,0:T(1,128)S(1)}, u32[]{:S(2)}, u32[]{:S(2)}) collective-permute-start(f32[20,3,34,1]{2,3,1,0:T(1,128)S(1)} %pad_maximum_fusion.4), channel_id=1, source_target_pairs={{0,1},{1,2},{2,3},{3,4},{4,5},{5,6},{6,7},{8,9},{9,10},{10,11},{11... | collective-permute-start | bytes 24488 | tf_op jit(solution)/shard_map/ppermute | solution.py:139
  39.4 39.4 %copy-start.3 = (s32[6,128]{1,0:T(8,128)S(1)}, s32[6,128]{1,0:T(8,128)}, u32[]{:S(2)}) copy-start(s32[6,128]{1,0:T(8,128)} %param.15) | copy-start | bytes 9220
  39.4 39.4 %copy-start.7 = (f32[128]{0:T(128)S(1)}, f32[128]{0:T(128)}, u32[]{:S(2)}) copy-start(f32[128]{0:T(128)} %param.12) | copy-start | bytes 1540
  70.3 16.3 %copy-start.4 = (f32[6,128]{1,0:T(8,128)S(1)}, f32[6,128]{1,0:T(8,128)}, u32[]{:S(2)}) copy-start(f32[6,128]{1,0:T(8,128)} %param.14) | copy-start | bytes 9220
  70.3 16.3 %copy-start.8 = (f32[128]{0:T(128)S(1)}, f32[128]{0:T(128)}, u32[]{:S(2)}) copy-start(f32[128]{0:T(128)} %param.13) | copy-start | bytes 1540
  71.0 14.5 %all-to-all-start.1 = ((f32[2,96,8,2]{1,3,0,2:T(2,128)}), f32[2,96,8,2]{1,3,0,2:T(2,128)S(1)}, u32[]{:S(2)}, u32[]{:S(2)}) async-start(f32[2,96,8,2]{1,3,0,2:T(2,128)} %copy.53), calls=%async_computation.1 | async-start | bytes 32768 | tf_op jit(solution)/shard_map/all_to_all | solution.py:179
  86.6 30.9 %copy-start.6 = (f32[128]{0:T(128)}, f32[128]{0:T(128)S(1)}, u32[]{:S(2)}) copy-start(f32[128]{0:T(128)S(1)} %fusion.22) | copy-start | bytes 1540

commit v8 on v7

--- a/solution.py
+++ b/solution.py
@@ -175,30 +175,36 @@
     send_zone = jnp.sum(jnp.where(placed, local_zone.astype(jnp.float32)[:, None], 0.0), axis=0)
     count_x = lax.axis_size("gx")
     count_y = lax.axis_size("gy")
-    outgoing = jnp.stack([send_flux, send_zone]).reshape(2, count_x, count_y, capacity)
-    arrived = lax.all_to_all(
-        lax.all_to_all(outgoing, "gx", split_axis=1, concat_axis=1, tiled=True),
-        "gy",
-        split_axis=2,
-        concat_axis=2,
-        tiled=True,
-    ).reshape(2, devices * capacity)
-    matched = arrived[1][None, :] == jnp.arange(zone_dev, dtype=jnp.float32)[:, None]
-    inflow = jnp.sum(jnp.where(matched, arrived[0][None, :], 0.0), axis=1)
+    outgoing = jnp.stack([send_flux, send_zone]).reshape(2, count_x, count_y * capacity)
+    arrived = lax.all_to_all(outgoing, "gx", split_axis=1, concat_axis=1, tiled=True)
+    arrived = arrived.reshape(2, count_x, count_y, capacity)
+    zones = jnp.arange(zone_dev, dtype=jnp.float32)
+    matched = arrived[1][..., None] == zones
+    gathered = jnp.sum(jnp.where(matched, arrived[0][..., None], 0.0), axis=(0, 2))
     coupled, total = couple(old_pressure, leakage, conductance, neighbour)
-    zone_pressure = (inflow + coupled) / total
-    answered = jnp.sum(jnp.where(matched, zone_pressure[:, None], 0.0), axis=0).reshape(
-        count_x, count_y, capacity
-    )
+    column = lax.axis_index("gy")
+    is_own = (jnp.arange(count_y, dtype=jnp.int32) == column)[:, None]
+    numer = gathered + jnp.where(is_own, coupled[None, :], 0.0)
+    denom = jnp.where(is_own, total[None, :], 0.0)
+    summed = row_sum(jnp.stack([numer, denom]), "gy", count_y)
+    row_pressure = summed[0] / summed[1]
+    zone_pressure = lax.dynamic_index_in_dim(row_pressure, column, axis=0, keepdims=False)
+    answered = jnp.sum(jnp.where(matched, row_pressure[None, :, None, :], 0.0), axis=3)
     returned = lax.all_to_all(
-        lax.all_to_all(answered, "gx", split_axis=0, concat_axis=0, tiled=True),
-        "gy",
-        split_axis=1,
-        concat_axis=1,
-        tiled=True,
+        answered.reshape(count_x, count_y * capacity), "gx", split_axis=0, concat_axis=0, tiled=True
     ).reshape(-1)
     opening_pressure = jnp.sum(jnp.where(placed, returned[None, :], 0.0), axis=1)
     return (new_populations, zone_pressure, opening_pressure)
+
+
+def row_sum(values, axis, count):
+    if count & (count - 1):
+        return lax.psum(values, axis)
+    step = 1
+    while step < count:
+        values = values + lax.ppermute(values, axis, [(j, j ^ step) for j in range(count)])
+        step *= 2
+    return values
 
 
 def patch_sums(momentum_x, cell_patch, openings):

time: 119 us -> 112 us (0.941)
  blocking collectives: 58.8 us -> 0 us
  starting transfers between devices: 27.4 us -> 57.2 us
  waiting for transfers between devices: 6.32 us -> 28.6 us
  local copies, waits for them, and re-layouts: 13.8 us -> 12 us
  other arithmetic: 4.99 us -> 6.55 us
    all_to_all x3 -> x0, blocking collectives: 58.8 us -> none  [the longest x1 29.6 us: on_device(): lax.all_to_all(outgoing, 'gx', split_axis=1, concat_axis=1, tiled=True)]
    all_to_all x1 -> x2, waiting for transfers between devices: 6.31 us -> 25.4 us  [the longest x1 13.5 us: on_device(): lax.all_to_all(outgoing, 'gx', split_axis=1, concat_axis=1, tiled=True)]
    ppermute x0 -> x3, starting transfers between devices: none -> 15.9 us  [row_sum(): lax.ppermute(values, axis, [(j, j ^ step) for j in range(count)])]
    all_to_all x1 -> x2, starting transfers between devices: 7.86 us -> 21.7 us  [the longest x1 13.1 us: on_device(): lax.all_to_all(outgoing, 'gx', split_axis=1, concat_axis=1, tiled=True)]
    ppermute x0 -> x3, waiting for transfers between devices: none -> 3.23 us  [row_sum(): lax.ppermute(values, axis, [(j, j ^ step) for j in range(count)])]
  transfers between devices with their start and end apart: 5 -> 9, of which waited for: 1 -> 5; matrix products, arithmetic and copies ran while one was open for 5% -> 5% of each run, Pallas kernels for 0% -> 0%
where the time goes in v8:
time: 112 us
  starting transfers between devices  57.2 us (51%)
  waiting for transfers between devices  28.6 us (26%)
  local copies, waits for them, and re-layouts  12 us (11%)
  other arithmetic  6.55 us (6%)
  Pallas kernels  4.22 us (4%)
  matrix products  1.97 us (2%)
    ppermute x3, starting transfers between devices, row_sum(): lax.ppermute(values, axis, [(j, j ^ step) for j in range(count)])  15.9 us
    all_to_all x1, waiting for transfers between devices, on_device(): lax.all_to_all(outgoing, 'gx', split_axis=1, concat_axis=1, tiled=True)  13.5 us
    all_to_all x1, starting transfers between devices, on_device(): lax.all_to_all(outgoing, 'gx', split_axis=1, concat_axis=1, tiled=True)  13.1 us
    all_to_all x1, waiting for transfers between devices, on_device(): lax.all_to_all(answered.reshape(count_x, count_y * capacity), 'gx', split...  11.9 us
    ppermute x1, starting transfers between devices, exchange_halos(): lax.ppermute(faces_x[0], 'gx', [((i + 1) % count_x, i) for i in range(cou...  9.81 us
    all_to_all x1, starting transfers between devices, on_device(): lax.all_to_all(answered.reshape(count_x, count_y * capacity), 'gx', split...  8.6 us
    unnamed x24, local copies, waits for them, and re-layouts  5.28 us
    ppermute x1, starting transfers between devices, exchange_halos(): lax.ppermute(faces_x[1], 'gx', [(i, (i + 1) % count_x) for i in range(cou...  4.5 us
  transfers between devices with their start and end apart: 9, of which 5 were waited for; matrix products, arithmetic and copies ran while one was open for 5% of the time, Pallas kernels for 0%

profile of v8, /device:TPU:1, one launch (start us, length us, event | category | flops | bytes accessed | tf_op | source)
XLA Modules:
  0.0 111.7 jit_solution(1792555120168449571)
XLA Ops:
  0.6 0.8 subtract_convert_fusion
  1.4 1.1 fusion.23
  2.6 4.5 %collective-permute-start = (f32[20,3,1,128]{3,2,1,0:T(1,128)S(1)}, f32[20,3,1,128]{3,2,1,0:T(1,128)S(1)}, u32[]{:S(2)}, u32[]{:S(2)}) collective-permute-start(f32[20,3,1,128]{3,2,1,0:T(1,128)S(1)} %pad_maximum_fusion.2), channel_id=1, source_target_pairs={{0,8},{8,16},{16,24},{24,32},{32,40},{40,48},{48,56},{56,64},{64,7... | collective-permute-start | bytes 92168 | tf_op jit(solution)/shard_map/ppermute | solution.py:124
  7.1 9.8 %collective-permute-start.1 = (f32[20,3,1,128]{3,2,1,0:T(1,128)S(1)}, f32[20,3,1,128]{3,2,1,0:T(1,128)S(1)}, u32[]{:S(2)}, u32[]{:S(2)}) collective-permute-start(f32[20,3,1,128]{3,2,1,0:T(1,128)S(1)} %pad_maximum_fusion.3), channel_id=1, source_target_pairs={{8,0},{16,8},{24,16},{32,24},{40,32},{48,40},{56,48},{64,56},{72,6... | collective-permute-start | bytes 92168 | tf_op jit(solution)/shard_map/ppermute | solution.py:125
  17.2 1.8 %fusion.22 = (f32[19,3,32,1]{3,2,1,0:T(8,128)S(1)}, f32[19,3,32,1]{3,2,1,0:T(8,128)S(1)}) fusion(f32[19,3,32,128]{3,2,1,0:T(8,128)} %pop_ref.1), kind=kLoop, calls=%fused_computation.85 | loop fusion | bytes 29184 | tf_op jit(solution)/shard_map/slice | solution.py:131
  21.1 1.3 %collective-permute-start.3 = (f32[20,3,34,1]{2,3,1,0:T(1,128)S(1)}, f32[20,3,34,1]{2,3,1,0:T(1,128)S(1)}, u32[]{:S(2)}, u32[]{:S(2)}) collective-permute-start(f32[20,3,34,1]{2,3,1,0:T(1,128)S(1)} %pad_maximum_fusion.5), channel_id=1, source_target_pairs={{1,0},{2,1},{3,2},{4,3},{5,4},{6,5},{7,6},{9,8},{10,9},{11,10},{12... | collective-permute-start | bytes 24488 | tf_op jit(solution)/shard_map/ppermute | solution.py:140
  22.6 4.0 %collective-permute-start.2 = (f32[20,3,34,1]{2,3,1,0:T(1,128)S(1)}, f32[20,3,34,1]{2,3,1,0:T(1,128)S(1)}, u32[]{:S(2)}, u32[]{:S(2)}) collective-permute-start(f32[20,3,34,1]{2,3,1,0:T(1,128)S(1)} %pad_maximum_fusion.4), channel_id=1, source_target_pairs={{0,1},{1,2},{2,3},{3,4},{4,5},{5,6},{6,7},{8,9},{9,10},{10,11},{11... | collective-permute-start | bytes 24488 | tf_op jit(solution)/shard_map/ppermute | solution.py:139
  26.8 1.4 %copy.67.yhi_ref = f32[20,3,32,1]{3,2,1,0:T(8,128)} copy(f32[20,3,32,1]{2,3,1,0:T(1,128)S(1)} %slice.165) | data formatting | bytes 15360
  28.3 1.4 %copy.65.ylo_ref = f32[20,3,32,1]{3,2,1,0:T(8,128)} copy(f32[20,3,32,1]{2,3,1,0:T(1,128)S(1)} %slice.161) | data formatting | bytes 15360
  29.8 0.7 slice_bitcast_fusion
  30.5 0.7 slice_bitcast_fusion.2
  31.2 4.2 %shard_map.103 = (f32[19,3,32,128]{3,2,1,0:T(8,128)}, f32[3,32,128]{2,1,0:T(8,128)}) custom-call(f32[19,3,32,128]{3,2,1,0:T(8,128)} %pop_ref.1, s32[3,32,128]{2,1,0:T(8,128)} %solid_ref.1, f32[20,3,1,128]{3,2,1,0:T(1,128)} %copy-done, f32[20,3,1,128]{3,2,1,0:T(1,128)} %copy-done.1, f32[20,3,32,1]{3,2,1,0:T(8,128)} %copy.65.ylo_ref, ...), custom_call_target="tpu_custom_call" | custom-call | tf_op jit(solution)/shard_map/pallas_call | solution.py:372
  35.5 0.8 bitcast_reduce-precision_fusion
  36.3 2.0 %fusion.4 = f32[3,4,128]{2,1,0:T(4,128)S(1)} fusion(s32[96,128]{1,0:T(8,128)S(1)} %get-tuple-element.20, bf16[3,96,128]{2,1,0:T(8,128)(2,1)S(1)} %pad_maximum_fusion, pred[4,96,128]{2,0,1:T(4,128)(4,1)S(1)} %iota_compare_fusion.5), kind=kOutput, calls=%fused_computation.8 | convolution fusion | flops 39469056 | bytes 178176 | tf_op jit(solution)/shard_map/khry,ryl->khl/dot_general | solution.py:232
  38.3 0.8 select_reduce_fusion.2
  39.2 0.7 copy.56
  39.9 13.1 %all-to-all-start = ((f32[2,96,16]{2,0,1:T(2,128)}), f32[2,96,16]{2,0,1:T(2,128)S(1)}, u32[]{:S(2)}, u32[]{:S(2)}) async-start(f32[2,96,16]{2,0,1:T(2,128)} %copy.56), calls=%async_computation | async-start | bytes 196608 | tf_op jit(solution)/shard_map/all_to_all | solution.py:179
  53.1 13.5 %all-to-all-done = f32[2,96,16]{2,0,1:T(2,128)S(1)} async-done(((f32[2,96,16]{2,0,1:T(2,128)}), f32[2,96,16]{2,0,1:T(2,128)S(1)}, u32[]{:S(2)}, u32[]{:S(2)}) %all-to-all-start) | async-done | bytes 12320 | tf_op jit(solution)/shard_map/all_to_all | solution.py:179
  67.7 3.2 %collective-permute-start.4 = (f32[2,8,128]{2,1,0:T(8,128)S(1)}, f32[2,8,128]{2,1,0:T(8,128)S(1)}, u32[]{:S(2)}, u32[]{:S(2)}) collective-permute-start(f32[2,8,128]{2,1,0:T(8,128)S(1)} %pad_maximum_fusion.6), channel_id=1, source_target_pairs={{0,1},{1,0},{2,3},{3,2},{4,5},{5,4},{6,7},{7,6},{8,9},{9,8},{10,11... | collective-permute-start | bytes 24584 | tf_op jit(solution)/shard_map/ppermute | solution.py:205
  70.9 1.2 %collective-permute-done.4 = f32[2,8,128]{2,1,0:T(8,128)S(1)} collective-permute-done((f32[2,8,128]{2,1,0:T(8,128)S(1)}, f32[2,8,128]{2,1,0:T(8,128)S(1)}, u32[]{:S(2)}, u32[]{:S(2)}) %collective-permute-start.4) | collective-permute-done | bytes 8224 | tf_op jit(solution)/shard_map/ppermute | solution.py:205
  72.1 5.3 %collective-permute-start.5 = (f32[2,8,128]{2,1,0:T(8,128)S(1)}, f32[2,8,128]{2,1,0:T(8,128)S(1)}, u32[]{:S(2)}, u32[]{:S(2)}) collective-permute-start(f32[2,8,128]{2,1,0:T(8,128)S(1)} %fusion.21), channel_id=1, source_target_pairs={{0,2},{1,3},{2,0},{3,1},{4,6},{5,7},{6,4},{7,5},{8,10},{9,11},{10,... | collective-permute-start | bytes 24584 | tf_op jit(solution)/shard_map/ppermute | solution.py:205
  77.4 1.0 collective-permute-done.5
  78.4 7.5 %collective-permute-start.6 = (f32[2,8,128]{2,1,0:T(8,128)S(1)}, f32[2,8,128]{2,1,0:T(8,128)S(1)}, u32[]{:S(2)}, u32[]{:S(2)}) collective-permute-start(f32[2,8,128]{2,1,0:T(8,128)S(1)} %fusion.26), channel_id=1, source_target_pairs={{0,4},{1,5},{2,6},{3,7},{4,0},{5,1},{6,2},{7,3},{8,12},{9,13},{10,... | collective-permute-start | bytes 24584 | tf_op jit(solution)/shard_map/ppermute | solution.py:205
  85.9 1.0 collective-permute-done.6
  86.9 0.6 select_reduce_fusion.3
  87.6 0.7 copy.62
  88.3 8.6 %all-to-all-start.1 = ((f32[96,1,16]{2,1,0:T(1,128)}), f32[96,1,16]{2,1,0:T(1,128)S(1)}, u32[]{:S(2)}, u32[]{:S(2)}) async-start(f32[96,1,16]{2,1,0:T(1,128)} %copy.62), calls=%async_computation.1 | async-start | bytes 98304 | tf_op jit(solution)/shard_map/all_to_all | solution.py:193
  96.9 0.5 dynamic-slice_bitcast_fusion
  97.4 11.9 %all-to-all-done.1 = f32[96,1,16]{2,1,0:T(1,128)S(1)} async-done(((f32[96,1,16]{2,1,0:T(1,128)}), f32[96,1,16]{2,1,0:T(1,128)S(1)}, u32[]{:S(2)}, u32[]{:S(2)}) %all-to-all-start.1) | async-done | bytes 6176 | tf_op jit(solution)/shard_map/all_to_all | solution.py:193
  109.3 0.5 broadcast.201
  109.8 0.8 reduce.7
  110.6 1.1 select_reduce_fusion
  (63 shorter events, 4.1 us)
Async XLA Ops:
  2.6 18.0 %collective-permute-start = (f32[20,3,1,128]{3,2,1,0:T(1,128)S(1)}, f32[20,3,1,128]{3,2,1,0:T(1,128)S(1)}, u32[]{:S(2)}, u32[]{:S(2)}) collective-permute-start(f32[20,3,1,128]{3,2,1,0:T(1,128)S(1)} %pad_maximum_fusion.2), channel_id=1, source_target_pairs={{0,8},{8,16},{16,24},{24,32},{32,40},{40,48},{48,56},{56,64},{64,7... | collective-permute-start | bytes 92168 | tf_op jit(solution)/shard_map/ppermute | solution.py:124
  7.1 13.6 %collective-permute-start.1 = (f32[20,3,1,128]{3,2,1,0:T(1,128)S(1)}, f32[20,3,1,128]{3,2,1,0:T(1,128)S(1)}, u32[]{:S(2)}, u32[]{:S(2)}) collective-permute-start(f32[20,3,1,128]{3,2,1,0:T(1,128)S(1)} %pad_maximum_fusion.3), channel_id=1, source_target_pairs={{8,0},{16,8},{24,16},{32,24},{40,32},{48,40},{56,48},{64,56},{72,6... | collective-permute-start | bytes 92168 | tf_op jit(solution)/shard_map/ppermute | solution.py:125
  17.1 1.9 %copy-start.2 = (s32[3,32,128]{2,1,0:T(8,128)S(1)}, s32[3,32,128]{2,1,0:T(8,128)}, u32[]{:S(2)}) copy-start(s32[3,32,128]{2,1,0:T(8,128)} %param.10) | copy-start | bytes 147460
  17.1 2.0 %copy-start.5 = (s32[512]{0:T(512)S(1)}, s32[512]{0:T(512)}, u32[]{:S(2)}) copy-start(s32[512]{0:T(512)} %param.11) | copy-start | bytes 6148
  17.1 2.3 %copy-start.4 = (s32[6,128]{1,0:T(8,128)S(1)}, s32[6,128]{1,0:T(8,128)}, u32[]{:S(2)}) copy-start(s32[6,128]{1,0:T(8,128)} %param.15) | copy-start | bytes 9220
  17.1 2.3 %copy-start.6 = (f32[128]{0:T(128)S(1)}, f32[128]{0:T(128)}, u32[]{:S(2)}) copy-start(f32[128]{0:T(128)} %param.12) | copy-start | bytes 1540
  17.2 2.6 %copy-start.3 = (f32[6,128]{1,0:T(8,128)S(1)}, f32[6,128]{1,0:T(8,128)}, u32[]{:S(2)}) copy-start(f32[6,128]{1,0:T(8,128)} %param.14) | copy-start | bytes 9220
  19.8 6.8 %copy-start.7 = (f32[128]{0:T(128)S(1)}, f32[128]{0:T(128)}, u32[]{:S(2)}) copy-start(f32[128]{0:T(128)} %param.13) | copy-start | bytes 1540
  20.6 9.1 %copy-start = (f32[20,3,1,128]{3,2,1,0:T(1,128)}, f32[20,3,1,128]{3,2,1,0:T(1,128)S(1)}, u32[]{:S(2)}) copy-start(f32[20,3,1,128]{3,2,1,0:T(1,128)S(1)} %collective-permute-done.xlo_ref) | copy-start | bytes 92164
  20.8 9.0 %copy-start.1 = (f32[20,3,1,128]{3,2,1,0:T(1,128)}, f32[20,3,1,128]{3,2,1,0:T(1,128)S(1)}, u32[]{:S(2)}) copy-start(f32[20,3,1,128]{3,2,1,0:T(1,128)S(1)} %collective-permute-done.1.xhi_ref) | copy-start | bytes 92164
  21.1 5.5 %collective-permute-start.3 = (f32[20,3,34,1]{2,3,1,0:T(1,128)S(1)}, f32[20,3,34,1]{2,3,1,0:T(1,128)S(1)}, u32[]{:S(2)}, u32[]{:S(2)}) collective-permute-start(f32[20,3,34,1]{2,3,1,0:T(1,128)S(1)} %pad_maximum_fusion.5), channel_id=1, source_target_pairs={{1,0},{2,1},{3,2},{4,3},{5,4},{6,5},{7,6},{9,8},{10,9},{11,10},{12... | collective-permute-start | bytes 24488 | tf_op jit(solution)/shard_map/ppermute | solution.py:140
  22.6 5.6 %collective-permute-start.2 = (f32[20,3,34,1]{2,3,1,0:T(1,128)S(1)}, f32[20,3,34,1]{2,3,1,0:T(1,128)S(1)}, u32[]{:S(2)}, u32[]{:S(2)}) collective-permute-start(f32[20,3,34,1]{2,3,1,0:T(1,128)S(1)} %pad_maximum_fusion.4), channel_id=1, source_target_pairs={{0,1},{1,2},{2,3},{3,4},{4,5},{5,6},{6,7},{8,9},{9,10},{10,11},{11... | collective-permute-start | bytes 24488 | tf_op jit(solution)/shard_map/ppermute | solution.py:139
  39.9 26.7 %all-to-all-start = ((f32[2,96,16]{2,0,1:T(2,128)}), f32[2,96,16]{2,0,1:T(2,128)S(1)}, u32[]{:S(2)}, u32[]{:S(2)}) async-start(f32[2,96,16]{2,0,1:T(2,128)} %copy.56), calls=%async_computation | async-start | bytes 196608 | tf_op jit(solution)/shard_map/all_to_all | solution.py:179
  67.7 4.4 %collective-permute-start.4 = (f32[2,8,128]{2,1,0:T(8,128)S(1)}, f32[2,8,128]{2,1,0:T(8,128)S(1)}, u32[]{:S(2)}, u32[]{:S(2)}) collective-permute-start(f32[2,8,128]{2,1,0:T(8,128)S(1)} %pad_maximum_fusion.6), channel_id=1, source_target_pairs={{0,1},{1,0},{2,3},{3,2},{4,5},{5,4},{6,7},{7,6},{8,9},{9,8},{10,11... | collective-permute-start | bytes 24584 | tf_op jit(solution)/shard_map/ppermute | solution.py:205
  72.1 6.3 %collective-permute-start.5 = (f32[2,8,128]{2,1,0:T(8,128)S(1)}, f32[2,8,128]{2,1,0:T(8,128)S(1)}, u32[]{:S(2)}, u32[]{:S(2)}) collective-permute-start(f32[2,8,128]{2,1,0:T(8,128)S(1)} %fusion.21), channel_id=1, source_target_pairs={{0,2},{1,3},{2,0},{3,1},{4,6},{5,7},{6,4},{7,5},{8,10},{9,11},{10,... | collective-permute-start | bytes 24584 | tf_op jit(solution)/shard_map/ppermute | solution.py:205
  78.4 8.5 %collective-permute-start.6 = (f32[2,8,128]{2,1,0:T(8,128)S(1)}, f32[2,8,128]{2,1,0:T(8,128)S(1)}, u32[]{:S(2)}, u32[]{:S(2)}) collective-permute-start(f32[2,8,128]{2,1,0:T(8,128)S(1)} %fusion.26), channel_id=1, source_target_pairs={{0,4},{1,5},{2,6},{3,7},{4,0},{5,1},{6,2},{7,3},{8,12},{9,13},{10,... | collective-permute-start | bytes 24584 | tf_op jit(solution)/shard_map/ppermute | solution.py:205
  88.3 21.0 %all-to-all-start.1 = ((f32[96,1,16]{2,1,0:T(1,128)}), f32[96,1,16]{2,1,0:T(1,128)S(1)}, u32[]{:S(2)}, u32[]{:S(2)}) async-start(f32[96,1,16]{2,1,0:T(1,128)} %copy.62), calls=%async_computation.1 | async-start | bytes 98304 | tf_op jit(solution)/shard_map/all_to_all | solution.py:193

commit v9 on v8

--- a/solution.py
+++ b/solution.py
@@ -114,11 +114,15 @@
     return (inflow + coupled) / total
 
 
-def exchange_halos(populations, fluid):
+def exchange_halos(populations, solid_flag):
     count_x = lax.axis_size("gx")
     count_y = lax.axis_size("gy")
+
+    def fluid(*at):
+        return (1 - solid_flag[at]).astype(jnp.float32)
+
     faces_x = [
-        jnp.concatenate([populations[:, :, at, None, :], fluid[None, :, at, None, :]], axis=0)
+        jnp.concatenate([populations[:, :, at, None, :], fluid(None, slice(None), at, None, slice(None))], axis=0)
         for at in (0, -1)
     ]
     x_low = lax.ppermute(faces_x[1], "gx", [(i, (i + 1) % count_x) for i in range(count_x)])
@@ -128,7 +132,7 @@
             [
                 x_low[:, :, :, at, None],
                 jnp.concatenate(
-                    [populations[:, :, :, at, None], fluid[None, :, :, at, None]], axis=0
+                    [populations[:, :, :, at, None], fluid(None, slice(None), slice(None), at, None)], axis=0
                 ),
                 x_high[:, :, :, at, None],
             ],
@@ -153,10 +157,9 @@
 def on_device(
     populations, solid_flag, cell_patch, patch_zone, old_pressure, leakage, conductance, neighbour
 ):
-    fluid = (1 - solid_flag).astype(jnp.float32)
-    halos = exchange_halos(populations, fluid)
-    new_populations, momentum_x = lbm_step(populations, solid_flag, halos)
-    patch_flux = patch_sums(momentum_x, cell_patch, patch_zone.shape[0])
+    halos = exchange_halos(populations, solid_flag)
+    new_populations, momentum_parts = lbm_step(populations, solid_flag, halos)
+    patch_flux = patch_sums(momentum_parts, cell_patch, patch_zone.shape[0])
     zone_dev = old_pressure.shape[0]
     openings = patch_zone.shape[0]
     devices = lax.axis_size("gx") * lax.axis_size("gy")
@@ -207,25 +210,20 @@
     return values
 
 
-def patch_sums(momentum_x, cell_patch, openings):
+def patch_sums(momentum_parts, cell_patch, openings):
     depth, width_x, width_y = cell_patch.shape
     rows = depth * width_x
-    momentum = momentum_x.reshape(rows, width_y)
+    parts = momentum_parts.reshape(3, rows, width_y)
     patch = cell_patch.reshape(rows, width_y)
     lanes = 128
     high = patch // lanes
     low = patch - high * lanes
     groups = openings // lanes
-    upper = lax.reduce_precision(momentum, exponent_bits=8, mantissa_bits=7)
-    rest = momentum - upper
-    middle = lax.reduce_precision(rest, exponent_bits=8, mantissa_bits=7)
-    lower = rest - middle
-    parts = jnp.stack([upper, middle, lower])
     picked = jnp.where(
         high[None, None] == jnp.arange(groups, dtype=jnp.int32)[None, :, None, None],
         parts[:, None],
-        0.0,
-    ).astype(jnp.bfloat16)
+        jnp.zeros((), jnp.bfloat16),
+    )
     onehot = (low[:, :, None] == jnp.arange(lanes, dtype=jnp.int32)[None, None, :]).astype(
         jnp.bfloat16
     )
@@ -364,7 +362,13 @@
             new_ref[d, level] = value
             if step_x != 0:
                 momentum = momentum + float(step_x) * value
-        mom_ref[level] = momentum
+        upper = momentum.astype(jnp.bfloat16)
+        rest = momentum - upper.astype(jnp.float32)
+        middle = rest.astype(jnp.bfloat16)
+        lower = (rest - middle.astype(jnp.float32)).astype(jnp.bfloat16)
+        mom_ref[0, level] = upper
+        mom_ref[1, level] = middle
+        mom_ref[2, level] = lower
 
 
 def lbm_step(populations, solid_flag, halos, interpret=False):
@@ -373,7 +377,7 @@
         lbm_kernel,
         out_shape=(
             jax.ShapeDtypeStruct(populations.shape, jnp.float32),
-            jax.ShapeDtypeStruct(solid_flag.shape, jnp.float32),
+            jax.ShapeDtypeStruct((3,) + solid_flag.shape, jnp.bfloat16),
         ),
         scratch_shapes=[pltpu.VMEM(populations.shape, jnp.float32)],
         interpret=interpret,

time: 112 us -> 113 us (level)
    unnamed x24 -> x26, local copies, waits for them, and re-layouts: 5.28 us -> 5.28 us
where the time goes in v9:
time: 113 us; the launch traced here: 112 us
  starting transfers between devices  57.4 us (51%)
  waiting for transfers between devices  28.6 us (25%)
  local copies, waits for them, and re-layouts  11.9 us (11%)
  other arithmetic  5.81 us (5%)
  Pallas kernels  4.25 us (4%)
  matrix products  2.85 us (3%)
    ppermute x3, starting transfers between devices, row_sum(): lax.ppermute(values, axis, [(j, j ^ step) for j in range(count)])  15.9 us
    all_to_all x1, waiting for transfers between devices, on_device(): lax.all_to_all(outgoing, 'gx', split_axis=1, concat_axis=1, tiled=True)  13.5 us
    all_to_all x1, starting transfers between devices, on_device(): lax.all_to_all(outgoing, 'gx', split_axis=1, concat_axis=1, tiled=True)  13.2 us
    all_to_all x1, waiting for transfers between devices, on_device(): lax.all_to_all(answered.reshape(count_x, count_y * capacity), 'gx', split...  11.9 us
    ppermute x1, starting transfers between devices, exchange_halos(): lax.ppermute(faces_x[0], 'gx', [((i + 1) % count_x, i) for i in range(cou...  9.94 us
    all_to_all x1, starting transfers between devices, on_device(): lax.all_to_all(answered.reshape(count_x, count_y * capacity), 'gx', split...  8.6 us
    unnamed x26, local copies, waits for them, and re-layouts  5.28 us
    ppermute x1, starting transfers between devices, exchange_halos(): lax.ppermute(faces_x[1], 'gx', [(i, (i + 1) % count_x) for i in range(cou...  4.5 us
  transfers between devices with their start and end apart: 9, of which 5 were waited for; matrix products, arithmetic and copies ran while one was open for 5% of the time, Pallas kernels for 0%

profile of v9, /device:TPU:1, one launch (start us, length us, event | category | flops | bytes accessed | tf_op | source)
XLA Modules:
  0.0 111.9 jit_solution(16751296795151498611)
XLA Ops:
  0.6 1.1 fusion.22
  1.7 0.7 convert_bitcast_fusion
  2.5 4.5 %collective-permute-start = (f32[20,3,1,128]{3,2,1,0:T(1,128)S(1)}, f32[20,3,1,128]{3,2,1,0:T(1,128)S(1)}, u32[]{:S(2)}, u32[]{:S(2)}) collective-permute-start(f32[20,3,1,128]{3,2,1,0:T(1,128)S(1)} %pad_maximum_fusion.1), channel_id=1, source_target_pairs={{0,8},{8,16},{16,24},{24,32},{32,40},{40,48},{48,56},{56,64},{64,7... | collective-permute-start | bytes 92168 | tf_op jit(solution)/shard_map/ppermute | solution.py:128
  7.1 9.9 %collective-permute-start.1 = (f32[20,3,1,128]{3,2,1,0:T(1,128)S(1)}, f32[20,3,1,128]{3,2,1,0:T(1,128)S(1)}, u32[]{:S(2)}, u32[]{:S(2)}) collective-permute-start(f32[20,3,1,128]{3,2,1,0:T(1,128)S(1)} %pad_maximum_fusion.2), channel_id=1, source_target_pairs={{8,0},{16,8},{24,16},{32,24},{40,32},{48,40},{56,48},{64,56},{72,6... | collective-permute-start | bytes 92168 | tf_op jit(solution)/shard_map/ppermute | solution.py:129
  17.1 1.8 %fusion.21 = (f32[19,3,32,1]{3,2,1,0:T(8,128)S(1)}, f32[19,3,32,1]{3,2,1,0:T(8,128)S(1)}) fusion(f32[19,3,32,128]{3,2,1,0:T(8,128)} %pop_ref.1), kind=kLoop, calls=%fused_computation.79 | loop fusion | bytes 29184 | tf_op jit(solution)/shard_map/slice | solution.py:135
  21.2 1.3 %collective-permute-start.3 = (f32[20,3,34,1]{2,3,1,0:T(1,128)S(1)}, f32[20,3,34,1]{2,3,1,0:T(1,128)S(1)}, u32[]{:S(2)}, u32[]{:S(2)}) collective-permute-start(f32[20,3,34,1]{2,3,1,0:T(1,128)S(1)} %pad_maximum_fusion.4), channel_id=1, source_target_pairs={{1,0},{2,1},{3,2},{4,3},{5,4},{6,5},{7,6},{9,8},{10,9},{11,10},{12... | collective-permute-start | bytes 24488 | tf_op jit(solution)/shard_map/ppermute | solution.py:144
  22.7 4.0 %collective-permute-start.2 = (f32[20,3,34,1]{2,3,1,0:T(1,128)S(1)}, f32[20,3,34,1]{2,3,1,0:T(1,128)S(1)}, u32[]{:S(2)}, u32[]{:S(2)}) collective-permute-start(f32[20,3,34,1]{2,3,1,0:T(1,128)S(1)} %pad_maximum_fusion.3), channel_id=1, source_target_pairs={{0,1},{1,2},{2,3},{3,4},{4,5},{5,6},{6,7},{8,9},{9,10},{10,11},{11... | collective-permute-start | bytes 24488 | tf_op jit(solution)/shard_map/ppermute | solution.py:143
  26.9 1.4 %copy.67.yhi_ref = f32[20,3,32,1]{3,2,1,0:T(8,128)} copy(f32[20,3,32,1]{2,3,1,0:T(1,128)S(1)} %slice.161) | data formatting | bytes 15360
  28.4 1.4 %copy.65.ylo_ref = f32[20,3,32,1]{3,2,1,0:T(8,128)} copy(f32[20,3,32,1]{2,3,1,0:T(1,128)S(1)} %slice.158) | data formatting | bytes 15360
  29.8 0.7 slice_bitcast_fusion
  30.6 0.7 slice_bitcast_fusion.2
  31.3 4.2 %shard_map.103 = (f32[19,3,32,128]{3,2,1,0:T(8,128)}, bf16[3,3,32,128]{3,2,1,0:T(8,128)(2,1)}) custom-call(f32[19,3,32,128]{3,2,1,0:T(8,128)} %pop_ref.1, s32[3,32,128]{2,1,0:T(8,128)} %solid_ref.1, f32[20,3,1,128]{3,2,1,0:T(1,128)} %copy-done.1, f32[20,3,1,128]{3,2,1,0:T(1,128)} %copy-done.2, f32[20,3,32,1]{3,2,1,0:T(8,128)} %copy.65.ylo_ref, ...), custom_call_target="tpu_custom_call" | custom-call | tf_op jit(solution)/shard_map/pallas_call | solution.py:376
  35.6 2.9 %fusion.4 = f32[3,4,128]{2,1,0:T(4,128)S(1)} fusion(s32[96,128]{1,0:T(8,128)S(1)} %get-tuple-element.20, pred[4,96,128]{2,0,1:T(4,128)(4,1)S(1)} %iota_compare_fusion.5, bf16[3,96,128]{2,1,0:T(8,128)(2,1)} %bitcast.90), kind=kOutput, calls=%fused_computation.8 | convolution fusion | flops 39469056 | bytes 178176 | tf_op jit(solution)/shard_map/khry,ryl->khl/dot_general | solution.py:230
  38.4 0.8 select_reduce_fusion.2
  39.4 0.7 copy.56
  40.1 13.2 %all-to-all-start = ((f32[2,96,16]{2,0,1:T(2,128)}), f32[2,96,16]{2,0,1:T(2,128)S(1)}, u32[]{:S(2)}, u32[]{:S(2)}) async-start(f32[2,96,16]{2,0,1:T(2,128)} %copy.56), calls=%async_computation | async-start | bytes 196608 | tf_op jit(solution)/shard_map/all_to_all | solution.py:182
  53.3 13.5 %all-to-all-done = f32[2,96,16]{2,0,1:T(2,128)S(1)} async-done(((f32[2,96,16]{2,0,1:T(2,128)}), f32[2,96,16]{2,0,1:T(2,128)S(1)}, u32[]{:S(2)}, u32[]{:S(2)}) %all-to-all-start) | async-done | bytes 12320 | tf_op jit(solution)/shard_map/all_to_all | solution.py:182
  67.3 0.5 select_reduce_fusion.4
  67.9 3.2 %collective-permute-start.4 = (f32[2,8,128]{2,1,0:T(8,128)S(1)}, f32[2,8,128]{2,1,0:T(8,128)S(1)}, u32[]{:S(2)}, u32[]{:S(2)}) collective-permute-start(f32[2,8,128]{2,1,0:T(8,128)S(1)} %pad_maximum_fusion.5), channel_id=1, source_target_pairs={{0,1},{1,0},{2,3},{3,2},{4,5},{5,4},{6,7},{7,6},{8,9},{9,8},{10,11... | collective-permute-start | bytes 24584 | tf_op jit(solution)/shard_map/ppermute | solution.py:208
  71.1 1.2 %collective-permute-done.4 = f32[2,8,128]{2,1,0:T(8,128)S(1)} collective-permute-done((f32[2,8,128]{2,1,0:T(8,128)S(1)}, f32[2,8,128]{2,1,0:T(8,128)S(1)}, u32[]{:S(2)}, u32[]{:S(2)}) %collective-permute-start.4) | collective-permute-done | bytes 8224 | tf_op jit(solution)/shard_map/ppermute | solution.py:208
  72.3 5.3 %collective-permute-start.5 = (f32[2,8,128]{2,1,0:T(8,128)S(1)}, f32[2,8,128]{2,1,0:T(8,128)S(1)}, u32[]{:S(2)}, u32[]{:S(2)}) collective-permute-start(f32[2,8,128]{2,1,0:T(8,128)S(1)} %fusion.20), channel_id=1, source_target_pairs={{0,2},{1,3},{2,0},{3,1},{4,6},{5,7},{6,4},{7,5},{8,10},{9,11},{10,... | collective-permute-start | bytes 24584 | tf_op jit(solution)/shard_map/ppermute | solution.py:208
  77.5 1.0 collective-permute-done.5
  78.6 7.5 %collective-permute-start.6 = (f32[2,8,128]{2,1,0:T(8,128)S(1)}, f32[2,8,128]{2,1,0:T(8,128)S(1)}, u32[]{:S(2)}, u32[]{:S(2)}) collective-permute-start(f32[2,8,128]{2,1,0:T(8,128)S(1)} %fusion.25), channel_id=1, source_target_pairs={{0,4},{1,5},{2,6},{3,7},{4,0},{5,1},{6,2},{7,3},{8,12},{9,13},{10,... | collective-permute-start | bytes 24584 | tf_op jit(solution)/shard_map/ppermute | solution.py:208
  86.0 1.0 collective-permute-done.6
  87.1 0.6 select_reduce_fusion.3
  87.7 0.7 copy.62
  88.5 8.6 %all-to-all-start.1 = ((f32[96,1,16]{2,1,0:T(1,128)}), f32[96,1,16]{2,1,0:T(1,128)S(1)}, u32[]{:S(2)}, u32[]{:S(2)}) async-start(f32[96,1,16]{2,1,0:T(1,128)} %copy.62), calls=%async_computation.1 | async-start | bytes 98304 | tf_op jit(solution)/shard_map/all_to_all | solution.py:196
  97.1 0.5 dynamic-slice_bitcast_fusion
  97.6 11.9 %all-to-all-done.1 = f32[96,1,16]{2,1,0:T(1,128)S(1)} async-done(((f32[96,1,16]{2,1,0:T(1,128)}), f32[96,1,16]{2,1,0:T(1,128)S(1)}, u32[]{:S(2)}, u32[]{:S(2)}) %all-to-all-start.1) | async-done | bytes 6176 | tf_op jit(solution)/shard_map/all_to_all | solution.py:196
  109.5 0.5 broadcast.250
  110.0 0.8 reduce.7
  110.8 1.1 select_reduce_fusion
  (62 shorter events, 3.6 us)
Async XLA Ops:
  2.5 18.2 %collective-permute-start = (f32[20,3,1,128]{3,2,1,0:T(1,128)S(1)}, f32[20,3,1,128]{3,2,1,0:T(1,128)S(1)}, u32[]{:S(2)}, u32[]{:S(2)}) collective-permute-start(f32[20,3,1,128]{3,2,1,0:T(1,128)S(1)} %pad_maximum_fusion.1), channel_id=1, source_target_pairs={{0,8},{8,16},{16,24},{24,32},{32,40},{40,48},{48,56},{56,64},{64,7... | collective-permute-start | bytes 92168 | tf_op jit(solution)/shard_map/ppermute | solution.py:128
  7.0 11.9 %copy-start = (s32[3,32,128]{2,1,0:T(8,128)S(1)}, s32[3,32,128]{2,1,0:T(8,128)}, u32[]{:S(2)}) copy-start(s32[3,32,128]{2,1,0:T(8,128)} %solid_ref.1) | copy-start | bytes 147460
  7.1 12.1 %copy-start.3 = (s32[3,32,128]{2,1,0:T(8,128)S(1)}, s32[3,32,128]{2,1,0:T(8,128)}, u32[]{:S(2)}) copy-start(s32[3,32,128]{2,1,0:T(8,128)} %param.10) | copy-start | bytes 147460
  7.1 12.2 %copy-start.6 = (s32[512]{0:T(512)S(1)}, s32[512]{0:T(512)}, u32[]{:S(2)}) copy-start(s32[512]{0:T(512)} %param.11) | copy-start | bytes 6148
  7.1 12.4 %copy-start.5 = (s32[6,128]{1,0:T(8,128)S(1)}, s32[6,128]{1,0:T(8,128)}, u32[]{:S(2)}) copy-start(s32[6,128]{1,0:T(8,128)} %param.15) | copy-start | bytes 9220
  7.1 12.4 %copy-start.7 = (f32[128]{0:T(128)S(1)}, f32[128]{0:T(128)}, u32[]{:S(2)}) copy-start(f32[128]{0:T(128)} %param.12) | copy-start | bytes 1540
  7.1 12.7 %copy-start.4 = (f32[6,128]{1,0:T(8,128)S(1)}, f32[6,128]{1,0:T(8,128)}, u32[]{:S(2)}) copy-start(f32[6,128]{1,0:T(8,128)} %param.14) | copy-start | bytes 9220
  7.1 13.7 %collective-permute-start.1 = (f32[20,3,1,128]{3,2,1,0:T(1,128)S(1)}, f32[20,3,1,128]{3,2,1,0:T(1,128)S(1)}, u32[]{:S(2)}, u32[]{:S(2)}) collective-permute-start(f32[20,3,1,128]{3,2,1,0:T(1,128)S(1)} %pad_maximum_fusion.2), channel_id=1, source_target_pairs={{8,0},{16,8},{24,16},{32,24},{40,32},{48,40},{56,48},{64,56},{72,6... | collective-permute-start | bytes 92168 | tf_op jit(solution)/shard_map/ppermute | solution.py:129
  19.9 6.8 %copy-start.8 = (f32[128]{0:T(128)S(1)}, f32[128]{0:T(128)}, u32[]{:S(2)}) copy-start(f32[128]{0:T(128)} %param.13) | copy-start | bytes 1540
  20.7 9.1 %copy-start.1 = (f32[20,3,1,128]{3,2,1,0:T(1,128)}, f32[20,3,1,128]{3,2,1,0:T(1,128)S(1)}, u32[]{:S(2)}) copy-start(f32[20,3,1,128]{3,2,1,0:T(1,128)S(1)} %collective-permute-done.xlo_ref) | copy-start | bytes 92164
  20.8 9.0 %copy-start.2 = (f32[20,3,1,128]{3,2,1,0:T(1,128)}, f32[20,3,1,128]{3,2,1,0:T(1,128)S(1)}, u32[]{:S(2)}) copy-start(f32[20,3,1,128]{3,2,1,0:T(1,128)S(1)} %collective-permute-done.1.xhi_ref) | copy-start | bytes 92164
  21.2 5.5 %collective-permute-start.3 = (f32[20,3,34,1]{2,3,1,0:T(1,128)S(1)}, f32[20,3,34,1]{2,3,1,0:T(1,128)S(1)}, u32[]{:S(2)}, u32[]{:S(2)}) collective-permute-start(f32[20,3,34,1]{2,3,1,0:T(1,128)S(1)} %pad_maximum_fusion.4), channel_id=1, source_target_pairs={{1,0},{2,1},{3,2},{4,3},{5,4},{6,5},{7,6},{9,8},{10,9},{11,10},{12... | collective-permute-start | bytes 24488 | tf_op jit(solution)/shard_map/ppermute | solution.py:144
  22.7 5.6 %collective-permute-start.2 = (f32[20,3,34,1]{2,3,1,0:T(1,128)S(1)}, f32[20,3,34,1]{2,3,1,0:T(1,128)S(1)}, u32[]{:S(2)}, u32[]{:S(2)}) collective-permute-start(f32[20,3,34,1]{2,3,1,0:T(1,128)S(1)} %pad_maximum_fusion.3), channel_id=1, source_target_pairs={{0,1},{1,2},{2,3},{3,4},{4,5},{5,6},{6,7},{8,9},{9,10},{10,11},{11... | collective-permute-start | bytes 24488 | tf_op jit(solution)/shard_map/ppermute | solution.py:143
  40.1 26.7 %all-to-all-start = ((f32[2,96,16]{2,0,1:T(2,128)}), f32[2,96,16]{2,0,1:T(2,128)S(1)}, u32[]{:S(2)}, u32[]{:S(2)}) async-start(f32[2,96,16]{2,0,1:T(2,128)} %copy.56), calls=%async_computation | async-start | bytes 196608 | tf_op jit(solution)/shard_map/all_to_all | solution.py:182
  67.9 4.4 %collective-permute-start.4 = (f32[2,8,128]{2,1,0:T(8,128)S(1)}, f32[2,8,128]{2,1,0:T(8,128)S(1)}, u32[]{:S(2)}, u32[]{:S(2)}) collective-permute-start(f32[2,8,128]{2,1,0:T(8,128)S(1)} %pad_maximum_fusion.5), channel_id=1, source_target_pairs={{0,1},{1,0},{2,3},{3,2},{4,5},{5,4},{6,7},{7,6},{8,9},{9,8},{10,11... | collective-permute-start | bytes 24584 | tf_op jit(solution)/shard_map/ppermute | solution.py:208
  72.3 6.3 %collective-permute-start.5 = (f32[2,8,128]{2,1,0:T(8,128)S(1)}, f32[2,8,128]{2,1,0:T(8,128)S(1)}, u32[]{:S(2)}, u32[]{:S(2)}) collective-permute-start(f32[2,8,128]{2,1,0:T(8,128)S(1)} %fusion.20), channel_id=1, source_target_pairs={{0,2},{1,3},{2,0},{3,1},{4,6},{5,7},{6,4},{7,5},{8,10},{9,11},{10,... | collective-permute-start | bytes 24584 | tf_op jit(solution)/shard_map/ppermute | solution.py:208
  78.6 8.5 %collective-permute-start.6 = (f32[2,8,128]{2,1,0:T(8,128)S(1)}, f32[2,8,128]{2,1,0:T(8,128)S(1)}, u32[]{:S(2)}, u32[]{:S(2)}) collective-permute-start(f32[2,8,128]{2,1,0:T(8,128)S(1)} %fusion.25), channel_id=1, source_target_pairs={{0,4},{1,5},{2,6},{3,7},{4,0},{5,1},{6,2},{7,3},{8,12},{9,13},{10,... | collective-permute-start | bytes 24584 | tf_op jit(solution)/shard_map/ppermute | solution.py:208
  88.5 21.0 %all-to-all-start.1 = ((f32[96,1,16]{2,1,0:T(1,128)}), f32[96,1,16]{2,1,0:T(1,128)S(1)}, u32[]{:S(2)}, u32[]{:S(2)}) async-start(f32[96,1,16]{2,1,0:T(1,128)} %copy.62), calls=%async_computation.1 | async-start | bytes 98304 | tf_op jit(solution)/shard_map/all_to_all | solution.py:196

commit v10 on v8

--- a/solution.py
+++ b/solution.py
@@ -200,10 +200,10 @@
 def row_sum(values, axis, count):
     if count & (count - 1):
         return lax.psum(values, axis)
-    step = 1
-    while step < count:
+    step = count // 2
+    while step:
         values = values + lax.ppermute(values, axis, [(j, j ^ step) for j in range(count)])
-        step *= 2
+        step //= 2
     return values
 
 

time: 112 us -> 112 us (level)
  waiting for transfers between devices: 28.6 us -> 30 us
  starting transfers between devices: 57.2 us -> 55.9 us
    ppermute x3, starting transfers between devices: 15.9 us -> 14.6 us  [row_sum(): lax.ppermute(values, axis, [(j, j ^ step) for j in range(count)])]
    ppermute x3, waiting for transfers between devices: 3.23 us -> 4.54 us  [row_sum(): lax.ppermute(values, axis, [(j, j ^ step) for j in range(count)])]
where the time goes in v10:
time: 112 us
  starting transfers between devices  55.9 us (50%)
  waiting for transfers between devices  30 us (27%)
  local copies, waits for them, and re-layouts  12 us (11%)
  other arithmetic  6.55 us (6%)
  Pallas kernels  4.22 us (4%)
  matrix products  1.97 us (2%)
    ppermute x3, starting transfers between devices, row_sum(): lax.ppermute(values, axis, [(j, j ^ step) for j in range(count)])  14.6 us
    all_to_all x1, waiting for transfers between devices, on_device(): lax.all_to_all(outgoing, 'gx', split_axis=1, concat_axis=1, tiled=True)  13.5 us
    all_to_all x1, starting transfers between devices, on_device(): lax.all_to_all(outgoing, 'gx', split_axis=1, concat_axis=1, tiled=True)  13.1 us
    all_to_all x1, waiting for transfers between devices, on_device(): lax.all_to_all(answered.reshape(count_x, count_y * capacity), 'gx', split...  11.9 us
    ppermute x1, starting transfers between devices, exchange_halos(): lax.ppermute(faces_x[0], 'gx', [((i + 1) % count_x, i) for i in range(cou...  9.81 us
    all_to_all x1, starting transfers between devices, on_device(): lax.all_to_all(answered.reshape(count_x, count_y * capacity), 'gx', split...  8.6 us
    unnamed x24, local copies, waits for them, and re-layouts  5.28 us
    ppermute x3, waiting for transfers between devices, row_sum(): lax.ppermute(values, axis, [(j, j ^ step) for j in range(count)])  4.54 us
  transfers between devices with their start and end apart: 9, of which 5 were waited for; matrix products, arithmetic and copies ran while one was open for 5% of the time, Pallas kernels for 0%

profile of v10, /device:TPU:1, one launch (start us, length us, event | category | flops | bytes accessed | tf_op | source)
XLA Modules:
  0.0 111.7 jit_solution(9179081792424075872)
XLA Ops:
  0.6 0.8 subtract_convert_fusion
  1.4 1.1 fusion.23
  2.6 4.5 %collective-permute-start = (f32[20,3,1,128]{3,2,1,0:T(1,128)S(1)}, f32[20,3,1,128]{3,2,1,0:T(1,128)S(1)}, u32[]{:S(2)}, u32[]{:S(2)}) collective-permute-start(f32[20,3,1,128]{3,2,1,0:T(1,128)S(1)} %pad_maximum_fusion.2), channel_id=1, source_target_pairs={{0,8},{8,16},{16,24},{24,32},{32,40},{40,48},{48,56},{56,64},{64,7... | collective-permute-start | bytes 92168 | tf_op jit(solution)/shard_map/ppermute | solution.py:124
  7.1 9.8 %collective-permute-start.1 = (f32[20,3,1,128]{3,2,1,0:T(1,128)S(1)}, f32[20,3,1,128]{3,2,1,0:T(1,128)S(1)}, u32[]{:S(2)}, u32[]{:S(2)}) collective-permute-start(f32[20,3,1,128]{3,2,1,0:T(1,128)S(1)} %pad_maximum_fusion.3), channel_id=1, source_target_pairs={{8,0},{16,8},{24,16},{32,24},{40,32},{48,40},{56,48},{64,56},{72,6... | collective-permute-start | bytes 92168 | tf_op jit(solution)/shard_map/ppermute | solution.py:125
  17.2 1.8 %fusion.22 = (f32[19,3,32,1]{3,2,1,0:T(8,128)S(1)}, f32[19,3,32,1]{3,2,1,0:T(8,128)S(1)}) fusion(f32[19,3,32,128]{3,2,1,0:T(8,128)} %pop_ref.1), kind=kLoop, calls=%fused_computation.85 | loop fusion | bytes 29184 | tf_op jit(solution)/shard_map/slice | solution.py:131
  21.1 1.3 %collective-permute-start.3 = (f32[20,3,34,1]{2,3,1,0:T(1,128)S(1)}, f32[20,3,34,1]{2,3,1,0:T(1,128)S(1)}, u32[]{:S(2)}, u32[]{:S(2)}) collective-permute-start(f32[20,3,34,1]{2,3,1,0:T(1,128)S(1)} %pad_maximum_fusion.5), channel_id=1, source_target_pairs={{1,0},{2,1},{3,2},{4,3},{5,4},{6,5},{7,6},{9,8},{10,9},{11,10},{12... | collective-permute-start | bytes 24488 | tf_op jit(solution)/shard_map/ppermute | solution.py:140
  22.6 4.0 %collective-permute-start.2 = (f32[20,3,34,1]{2,3,1,0:T(1,128)S(1)}, f32[20,3,34,1]{2,3,1,0:T(1,128)S(1)}, u32[]{:S(2)}, u32[]{:S(2)}) collective-permute-start(f32[20,3,34,1]{2,3,1,0:T(1,128)S(1)} %pad_maximum_fusion.4), channel_id=1, source_target_pairs={{0,1},{1,2},{2,3},{3,4},{4,5},{5,6},{6,7},{8,9},{9,10},{10,11},{11... | collective-permute-start | bytes 24488 | tf_op jit(solution)/shard_map/ppermute | solution.py:139
  26.8 1.4 %copy.67.yhi_ref = f32[20,3,32,1]{3,2,1,0:T(8,128)} copy(f32[20,3,32,1]{2,3,1,0:T(1,128)S(1)} %slice.165) | data formatting | bytes 15360
  28.3 1.4 %copy.65.ylo_ref = f32[20,3,32,1]{3,2,1,0:T(8,128)} copy(f32[20,3,32,1]{2,3,1,0:T(1,128)S(1)} %slice.161) | data formatting | bytes 15360
  29.8 0.7 slice_bitcast_fusion
  30.5 0.7 slice_bitcast_fusion.2
  31.2 4.2 %shard_map.103 = (f32[19,3,32,128]{3,2,1,0:T(8,128)}, f32[3,32,128]{2,1,0:T(8,128)}) custom-call(f32[19,3,32,128]{3,2,1,0:T(8,128)} %pop_ref.1, s32[3,32,128]{2,1,0:T(8,128)} %solid_ref.1, f32[20,3,1,128]{3,2,1,0:T(1,128)} %copy-done, f32[20,3,1,128]{3,2,1,0:T(1,128)} %copy-done.1, f32[20,3,32,1]{3,2,1,0:T(8,128)} %copy.65.ylo_ref, ...), custom_call_target="tpu_custom_call" | custom-call | tf_op jit(solution)/shard_map/pallas_call | solution.py:372
  35.5 0.8 bitcast_reduce-precision_fusion
  36.3 2.0 %fusion.4 = f32[3,4,128]{2,1,0:T(4,128)S(1)} fusion(s32[96,128]{1,0:T(8,128)S(1)} %get-tuple-element.20, bf16[3,96,128]{2,1,0:T(8,128)(2,1)S(1)} %pad_maximum_fusion, pred[4,96,128]{2,0,1:T(4,128)(4,1)S(1)} %iota_compare_fusion.5), kind=kOutput, calls=%fused_computation.8 | convolution fusion | flops 39469056 | bytes 178176 | tf_op jit(solution)/shard_map/khry,ryl->khl/dot_general | solution.py:232
  38.3 0.8 select_reduce_fusion.2
  39.2 0.7 copy.56
  39.9 13.1 %all-to-all-start = ((f32[2,96,16]{2,0,1:T(2,128)}), f32[2,96,16]{2,0,1:T(2,128)S(1)}, u32[]{:S(2)}, u32[]{:S(2)}) async-start(f32[2,96,16]{2,0,1:T(2,128)} %copy.56), calls=%async_computation | async-start | bytes 196608 | tf_op jit(solution)/shard_map/all_to_all | solution.py:179
  53.1 13.5 %all-to-all-done = f32[2,96,16]{2,0,1:T(2,128)S(1)} async-done(((f32[2,96,16]{2,0,1:T(2,128)}), f32[2,96,16]{2,0,1:T(2,128)S(1)}, u32[]{:S(2)}, u32[]{:S(2)}) %all-to-all-start) | async-done | bytes 12320 | tf_op jit(solution)/shard_map/all_to_all | solution.py:179
  67.7 8.5 %collective-permute-start.4 = (f32[2,8,128]{2,1,0:T(8,128)S(1)}, f32[2,8,128]{2,1,0:T(8,128)S(1)}, u32[]{:S(2)}, u32[]{:S(2)}) collective-permute-start(f32[2,8,128]{2,1,0:T(8,128)S(1)} %pad_maximum_fusion.6), channel_id=1, source_target_pairs={{0,4},{1,5},{2,6},{3,7},{4,0},{5,1},{6,2},{7,3},{8,12},{9,13},{10,... | collective-permute-start | bytes 24584 | tf_op jit(solution)/shard_map/ppermute | solution.py:205
  76.2 1.0 collective-permute-done.4
  77.2 3.0 %collective-permute-start.5 = (f32[2,8,128]{2,1,0:T(8,128)S(1)}, f32[2,8,128]{2,1,0:T(8,128)S(1)}, u32[]{:S(2)}, u32[]{:S(2)}) collective-permute-start(f32[2,8,128]{2,1,0:T(8,128)S(1)} %fusion.21), channel_id=1, source_target_pairs={{0,2},{1,3},{2,0},{3,1},{4,6},{5,7},{6,4},{7,5},{8,10},{9,11},{10,... | collective-permute-start | bytes 24584 | tf_op jit(solution)/shard_map/ppermute | solution.py:205
  80.2 2.3 %collective-permute-done.5 = f32[2,8,128]{2,1,0:T(8,128)S(1)} collective-permute-done((f32[2,8,128]{2,1,0:T(8,128)S(1)}, f32[2,8,128]{2,1,0:T(8,128)S(1)}, u32[]{:S(2)}, u32[]{:S(2)}) %collective-permute-start.5) | collective-permute-done | bytes 8224 | tf_op jit(solution)/shard_map/ppermute | solution.py:205
  82.5 3.1 %collective-permute-start.6 = (f32[2,8,128]{2,1,0:T(8,128)S(1)}, f32[2,8,128]{2,1,0:T(8,128)S(1)}, u32[]{:S(2)}, u32[]{:S(2)}) collective-permute-start(f32[2,8,128]{2,1,0:T(8,128)S(1)} %fusion.26), channel_id=1, source_target_pairs={{0,1},{1,0},{2,3},{3,2},{4,5},{5,4},{6,7},{7,6},{8,9},{9,8},{10,11... | collective-permute-start | bytes 24584 | tf_op jit(solution)/shard_map/ppermute | solution.py:205
  85.6 1.2 %collective-permute-done.6 = f32[2,8,128]{2,1,0:T(8,128)S(1)} collective-permute-done((f32[2,8,128]{2,1,0:T(8,128)S(1)}, f32[2,8,128]{2,1,0:T(8,128)S(1)}, u32[]{:S(2)}, u32[]{:S(2)}) %collective-permute-start.6) | collective-permute-done | bytes 8224 | tf_op jit(solution)/shard_map/ppermute | solution.py:205
  86.9 0.6 select_reduce_fusion.3
  87.6 0.7 copy.62
  88.3 8.6 %all-to-all-start.1 = ((f32[96,1,16]{2,1,0:T(1,128)}), f32[96,1,16]{2,1,0:T(1,128)S(1)}, u32[]{:S(2)}, u32[]{:S(2)}) async-start(f32[96,1,16]{2,1,0:T(1,128)} %copy.62), calls=%async_computation.1 | async-start | bytes 98304 | tf_op jit(solution)/shard_map/all_to_all | solution.py:193
  96.9 0.5 dynamic-slice_bitcast_fusion
  97.4 11.9 %all-to-all-done.1 = f32[96,1,16]{2,1,0:T(1,128)S(1)} async-done(((f32[96,1,16]{2,1,0:T(1,128)}), f32[96,1,16]{2,1,0:T(1,128)S(1)}, u32[]{:S(2)}, u32[]{:S(2)}) %all-to-all-start.1) | async-done | bytes 6176 | tf_op jit(solution)/shard_map/all_to_all | solution.py:193
  109.3 0.5 broadcast.201
  109.8 0.8 reduce.7
  110.6 1.1 select_reduce_fusion
  (63 shorter events, 4.1 us)
Async XLA Ops:
  2.6 18.0 %collective-permute-start = (f32[20,3,1,128]{3,2,1,0:T(1,128)S(1)}, f32[20,3,1,128]{3,2,1,0:T(1,128)S(1)}, u32[]{:S(2)}, u32[]{:S(2)}) collective-permute-start(f32[20,3,1,128]{3,2,1,0:T(1,128)S(1)} %pad_maximum_fusion.2), channel_id=1, source_target_pairs={{0,8},{8,16},{16,24},{24,32},{32,40},{40,48},{48,56},{56,64},{64,7... | collective-permute-start | bytes 92168 | tf_op jit(solution)/shard_map/ppermute | solution.py:124
  7.1 13.6 %collective-permute-start.1 = (f32[20,3,1,128]{3,2,1,0:T(1,128)S(1)}, f32[20,3,1,128]{3,2,1,0:T(1,128)S(1)}, u32[]{:S(2)}, u32[]{:S(2)}) collective-permute-start(f32[20,3,1,128]{3,2,1,0:T(1,128)S(1)} %pad_maximum_fusion.3), channel_id=1, source_target_pairs={{8,0},{16,8},{24,16},{32,24},{40,32},{48,40},{56,48},{64,56},{72,6... | collective-permute-start | bytes 92168 | tf_op jit(solution)/shard_map/ppermute | solution.py:125
  17.1 1.9 %copy-start.2 = (s32[3,32,128]{2,1,0:T(8,128)S(1)}, s32[3,32,128]{2,1,0:T(8,128)}, u32[]{:S(2)}) copy-start(s32[3,32,128]{2,1,0:T(8,128)} %param.10) | copy-start | bytes 147460
  17.1 2.0 %copy-start.5 = (s32[512]{0:T(512)S(1)}, s32[512]{0:T(512)}, u32[]{:S(2)}) copy-start(s32[512]{0:T(512)} %param.11) | copy-start | bytes 6148
  17.1 2.3 %copy-start.4 = (s32[6,128]{1,0:T(8,128)S(1)}, s32[6,128]{1,0:T(8,128)}, u32[]{:S(2)}) copy-start(s32[6,128]{1,0:T(8,128)} %param.15) | copy-start | bytes 9220
  17.1 2.3 %copy-start.6 = (f32[128]{0:T(128)S(1)}, f32[128]{0:T(128)}, u32[]{:S(2)}) copy-start(f32[128]{0:T(128)} %param.12) | copy-start | bytes 1540
  17.2 2.6 %copy-start.3 = (f32[6,128]{1,0:T(8,128)S(1)}, f32[6,128]{1,0:T(8,128)}, u32[]{:S(2)}) copy-start(f32[6,128]{1,0:T(8,128)} %param.14) | copy-start | bytes 9220
  19.8 6.8 %copy-start.7 = (f32[128]{0:T(128)S(1)}, f32[128]{0:T(128)}, u32[]{:S(2)}) copy-start(f32[128]{0:T(128)} %param.13) | copy-start | bytes 1540
  20.6 9.1 %copy-start = (f32[20,3,1,128]{3,2,1,0:T(1,128)}, f32[20,3,1,128]{3,2,1,0:T(1,128)S(1)}, u32[]{:S(2)}) copy-start(f32[20,3,1,128]{3,2,1,0:T(1,128)S(1)} %collective-permute-done.xlo_ref) | copy-start | bytes 92164
  20.8 9.0 %copy-start.1 = (f32[20,3,1,128]{3,2,1,0:T(1,128)}, f32[20,3,1,128]{3,2,1,0:T(1,128)S(1)}, u32[]{:S(2)}) copy-start(f32[20,3,1,128]{3,2,1,0:T(1,128)S(1)} %collective-permute-done.1.xhi_ref) | copy-start | bytes 92164
  21.1 5.5 %collective-permute-start.3 = (f32[20,3,34,1]{2,3,1,0:T(1,128)S(1)}, f32[20,3,34,1]{2,3,1,0:T(1,128)S(1)}, u32[]{:S(2)}, u32[]{:S(2)}) collective-permute-start(f32[20,3,34,1]{2,3,1,0:T(1,128)S(1)} %pad_maximum_fusion.5), channel_id=1, source_target_pairs={{1,0},{2,1},{3,2},{4,3},{5,4},{6,5},{7,6},{9,8},{10,9},{11,10},{12... | collective-permute-start | bytes 24488 | tf_op jit(solution)/shard_map/ppermute | solution.py:140
  22.6 5.6 %collective-permute-start.2 = (f32[20,3,34,1]{2,3,1,0:T(1,128)S(1)}, f32[20,3,34,1]{2,3,1,0:T(1,128)S(1)}, u32[]{:S(2)}, u32[]{:S(2)}) collective-permute-start(f32[20,3,34,1]{2,3,1,0:T(1,128)S(1)} %pad_maximum_fusion.4), channel_id=1, source_target_pairs={{0,1},{1,2},{2,3},{3,4},{4,5},{5,6},{6,7},{8,9},{9,10},{10,11},{11... | collective-permute-start | bytes 24488 | tf_op jit(solution)/shard_map/ppermute | solution.py:139
  39.9 26.7 %all-to-all-start = ((f32[2,96,16]{2,0,1:T(2,128)}), f32[2,96,16]{2,0,1:T(2,128)S(1)}, u32[]{:S(2)}, u32[]{:S(2)}) async-start(f32[2,96,16]{2,0,1:T(2,128)} %copy.56), calls=%async_computation | async-start | bytes 196608 | tf_op jit(solution)/shard_map/all_to_all | solution.py:179
  67.7 9.5 %collective-permute-start.4 = (f32[2,8,128]{2,1,0:T(8,128)S(1)}, f32[2,8,128]{2,1,0:T(8,128)S(1)}, u32[]{:S(2)}, u32[]{:S(2)}) collective-permute-start(f32[2,8,128]{2,1,0:T(8,128)S(1)} %pad_maximum_fusion.6), channel_id=1, source_target_pairs={{0,4},{1,5},{2,6},{3,7},{4,0},{5,1},{6,2},{7,3},{8,12},{9,13},{10,... | collective-permute-start | bytes 24584 | tf_op jit(solution)/shard_map/ppermute | solution.py:205
  77.2 5.3 %collective-permute-start.5 = (f32[2,8,128]{2,1,0:T(8,128)S(1)}, f32[2,8,128]{2,1,0:T(8,128)S(1)}, u32[]{:S(2)}, u32[]{:S(2)}) collective-permute-start(f32[2,8,128]{2,1,0:T(8,128)S(1)} %fusion.21), channel_id=1, source_target_pairs={{0,2},{1,3},{2,0},{3,1},{4,6},{5,7},{6,4},{7,5},{8,10},{9,11},{10,... | collective-permute-start | bytes 24584 | tf_op jit(solution)/shard_map/ppermute | solution.py:205
  82.5 4.4 %collective-permute-start.6 = (f32[2,8,128]{2,1,0:T(8,128)S(1)}, f32[2,8,128]{2,1,0:T(8,128)S(1)}, u32[]{:S(2)}, u32[]{:S(2)}) collective-permute-start(f32[2,8,128]{2,1,0:T(8,128)S(1)} %fusion.26), channel_id=1, source_target_pairs={{0,1},{1,0},{2,3},{3,2},{4,5},{5,4},{6,7},{7,6},{8,9},{9,8},{10,11... | collective-permute-start | bytes 24584 | tf_op jit(solution)/shard_map/ppermute | solution.py:205
  88.3 21.0 %all-to-all-start.1 = ((f32[96,1,16]{2,1,0:T(1,128)}), f32[96,1,16]{2,1,0:T(1,128)S(1)}, u32[]{:S(2)}, u32[]{:S(2)}) async-start(f32[96,1,16]{2,1,0:T(1,128)} %copy.62), calls=%async_computation.1 | async-start | bytes 98304 | tf_op jit(solution)/shard_map/all_to_all | solution.py:193

commit v11 on v10

--- a/solution.py
+++ b/solution.py
@@ -138,16 +138,7 @@
     ]
     y_low = lax.ppermute(faces_y[1], "gy", [(j, j + 1) for j in range(count_y - 1)])
     y_high = lax.ppermute(faces_y[0], "gy", [(j + 1, j) for j in range(count_y - 1)])
-    return (
-        x_low,
-        x_high,
-        y_low[:, :, 1:-1],
-        y_high[:, :, 1:-1],
-        y_low[:, :, :1],
-        y_low[:, :, -1:],
-        y_high[:, :, :1],
-        y_high[:, :, -1:],
-    )
+    return (x_low, x_high, y_low, y_high)
 
 
 def on_device(
@@ -294,7 +285,6 @@
 
 def lbm_kernel(
     pop_ref, solid_ref, xlo_ref, xhi_ref, ylo_ref, yhi_ref,
-    cll_ref, chl_ref, clh_ref, chh_ref,
     new_ref, mom_ref, rel_ref,
 ):
     _, depth, width_x, width_y = pop_ref.shape
@@ -314,24 +304,16 @@
     xhi, xhi_f = halo(xhi_ref)
     ylo, ylo_f = halo(ylo_ref)
     yhi, yhi_f = halo(yhi_ref)
-    cll, cll_f = halo(cll_ref)
-    chl, chl_f = halo(chl_ref)
-    clh, clh_f = halo(clh_ref)
-    chh, chh_f = halo(chh_ref)
 
     def pieces(step_x, step_y, level, direction):
         if direction is None:
             x_lo, x_hi, y_lo, y_hi = xlo_f, xhi_f, ylo_f, yhi_f
-            c_ll, c_hl, c_lh, c_hh = cll_f, chl_f, clh_f, chh_f
         else:
             x_lo, x_hi, y_lo, y_hi = xlo[direction], xhi[direction], ylo[direction], yhi[direction]
-            c_ll, c_hl, c_lh, c_hh = cll[direction], chl[direction], clh[direction], chh[direction]
         row = x_lo[level] if step_x == 1 else x_hi[level]
-        column = y_lo[level] if step_y == 1 else y_hi[level]
-        if step_y == 1:
-            corner = c_ll[level] if step_x == 1 else c_hl[level]
-        else:
-            corner = c_lh[level] if step_x == 1 else c_hh[level]
+        widened = y_lo[level] if step_y == 1 else y_hi[level]
+        column = widened[1 : width_x + 1]
+        corner = widened[:1] if step_x == 1 else widened[width_x + 1 :]
         row = jnp.broadcast_to(row, shape)
         column = jnp.broadcast_to(column, shape)
         corner = jnp.broadcast_to(corner, shape)

time: 112 us -> 111 us (level)
  local copies, waits for them, and re-layouts: 12 us -> 10.6 us
    unnamed x24 -> x20, local copies, waits for them, and re-layouts: 5.28 us -> 0.96 us
    ppermute x0 -> x2, local copies, waits for them, and re-layouts: none -> 3.18 us  [the longest x1 1.61 us: exchange_halos(): lax.ppermute(faces_y[0], 'gy', [(j + 1, j) for j in range(count_y - 1)])]
where the time goes in v11:
time: 111 us
  starting transfers between devices  56 us (50%)
  waiting for transfers between devices  29.8 us (27%)
  local copies, waits for them, and re-layouts  10.6 us (10%)
  other arithmetic  6.55 us (6%)
  Pallas kernels  4.47 us (4%)
  matrix products  1.97 us (2%)
    ppermute x3, starting transfers between devices, row_sum(): lax.ppermute(values, axis, [(j, j ^ step) for j in range(count)])  14.7 us
    all_to_all x1, waiting for transfers between devices, on_device(): lax.all_to_all(outgoing, 'gx', split_axis=1, concat_axis=1, tiled=True)  13.5 us
    all_to_all x1, starting transfers between devices, on_device(): lax.all_to_all(outgoing, 'gx', split_axis=1, concat_axis=1, tiled=True)  13.1 us
    all_to_all x1, waiting for transfers between devices, on_device(): lax.all_to_all(answered.reshape(count_x, count_y * capacity), 'gx', split...  11.9 us
    ppermute x1, starting transfers between devices, exchange_halos(): lax.ppermute(faces_x[0], 'gx', [((i + 1) % count_x, i) for i in range(cou...  9.81 us
    all_to_all x1, starting transfers between devices, on_device(): lax.all_to_all(answered.reshape(count_x, count_y * capacity), 'gx', split...  8.66 us
    ppermute x1, starting transfers between devices, exchange_halos(): lax.ppermute(faces_x[1], 'gx', [(i, (i + 1) % count_x) for i in range(cou...  4.5 us
    pallas_call x1, Pallas kernels, lbm_step(): pl.pallas_call(lbm_kernel, out_shape=(jax.ShapeDtypeStruct(populations.sh...  4.47 us
  transfers between devices with their start and end apart: 9, of which 5 were waited for; matrix products, arithmetic and copies ran while one was open for 5% of the time, Pallas kernels for 0%

profile of v11, /device:TPU:1, one launch (start us, length us, event | category | flops | bytes accessed | tf_op | source)
XLA Modules:
  0.0 110.5 jit_solution(12482512905280953344)
XLA Ops:
  0.6 0.8 subtract_convert_fusion
  1.4 1.1 fusion.23
  2.6 4.5 %collective-permute-start = (f32[20,3,1,128]{3,2,1,0:T(1,128)S(1)}, f32[20,3,1,128]{3,2,1,0:T(1,128)S(1)}, u32[]{:S(2)}, u32[]{:S(2)}) collective-permute-start(f32[20,3,1,128]{3,2,1,0:T(1,128)S(1)} %pad_maximum_fusion.2), channel_id=1, source_target_pairs={{0,8},{8,16},{16,24},{24,32},{32,40},{40,48},{48,56},{56,64},{64,7... | collective-permute-start | bytes 92168 | tf_op jit(solution)/shard_map/ppermute | solution.py:124
  7.1 9.8 %collective-permute-start.1 = (f32[20,3,1,128]{3,2,1,0:T(1,128)S(1)}, f32[20,3,1,128]{3,2,1,0:T(1,128)S(1)}, u32[]{:S(2)}, u32[]{:S(2)}) collective-permute-start(f32[20,3,1,128]{3,2,1,0:T(1,128)S(1)} %pad_maximum_fusion.3), channel_id=1, source_target_pairs={{8,0},{16,8},{24,16},{32,24},{40,32},{48,40},{56,48},{64,56},{72,6... | collective-permute-start | bytes 92168 | tf_op jit(solution)/shard_map/ppermute | solution.py:125
  17.2 1.8 %fusion.22 = (f32[19,3,32,1]{3,2,1,0:T(8,128)S(1)}, f32[19,3,32,1]{3,2,1,0:T(8,128)S(1)}) fusion(f32[19,3,32,128]{3,2,1,0:T(8,128)} %pop_ref.1), kind=kLoop, calls=%fused_computation.81 | loop fusion | bytes 29184 | tf_op jit(solution)/shard_map/slice | solution.py:131
  20.2 0.4 copy.56
  21.1 1.3 %collective-permute-start.3 = (f32[20,3,34,1]{2,3,1,0:T(1,128)S(1)}, f32[20,3,34,1]{2,3,1,0:T(1,128)S(1)}, u32[]{:S(2)}, u32[]{:S(2)}) collective-permute-start(f32[20,3,34,1]{2,3,1,0:T(1,128)S(1)} %pad_maximum_fusion.5), channel_id=1, source_target_pairs={{1,0},{2,1},{3,2},{4,3},{5,4},{6,5},{7,6},{9,8},{10,9},{11,10},{12... | collective-permute-start | bytes 24488 | tf_op jit(solution)/shard_map/ppermute | solution.py:140
  22.6 4.0 %collective-permute-start.2 = (f32[20,3,34,1]{2,3,1,0:T(1,128)S(1)}, f32[20,3,34,1]{2,3,1,0:T(1,128)S(1)}, u32[]{:S(2)}, u32[]{:S(2)}) collective-permute-start(f32[20,3,34,1]{2,3,1,0:T(1,128)S(1)} %pad_maximum_fusion.4), channel_id=1, source_target_pairs={{0,1},{1,2},{2,3},{3,4},{4,5},{5,6},{6,7},{8,9},{9,10},{10,11},{11... | collective-permute-start | bytes 24488 | tf_op jit(solution)/shard_map/ppermute | solution.py:139
  26.7 1.6 %copy.47.yhi_ref = f32[20,3,34,1]{3,2,1,0:T(8,128)} copy(f32[20,3,34,1]{2,3,1,0:T(1,128)S(1)} %collective-permute-done.3) | data formatting | bytes 16320 | tf_op jit(solution)/shard_map/ppermute | solution.py:140
  28.3 1.6 %copy.46.ylo_ref = f32[20,3,34,1]{3,2,1,0:T(8,128)} copy(f32[20,3,34,1]{2,3,1,0:T(1,128)S(1)} %collective-permute-done.2) | data formatting | bytes 16320 | tf_op jit(solution)/shard_map/ppermute | solution.py:139
  29.8 4.5 %shard_map.103 = (f32[19,3,32,128]{3,2,1,0:T(8,128)}, f32[3,32,128]{2,1,0:T(8,128)}) custom-call(f32[19,3,32,128]{3,2,1,0:T(8,128)} %pop_ref.1, s32[3,32,128]{2,1,0:T(8,128)} %solid_ref.1, f32[20,3,1,128]{3,2,1,0:T(1,128)} %copy-done, f32[20,3,1,128]{3,2,1,0:T(1,128)} %copy-done.1, f32[20,3,34,1]{3,2,1,0:T(8,128)} %copy.46.ylo_ref, ...), custom_call_target="tpu_custom_call" | custom-call | tf_op jit(solution)/shard_map/pallas_call | solution.py:354
  34.3 0.8 bitcast_reduce-precision_fusion
  35.2 2.0 %fusion.4 = f32[3,4,128]{2,1,0:T(4,128)S(1)} fusion(s32[96,128]{1,0:T(8,128)S(1)} %get-tuple-element.20, bf16[3,96,128]{2,1,0:T(8,128)(2,1)S(1)} %pad_maximum_fusion, pred[4,96,128]{2,0,1:T(4,128)(4,1)S(1)} %iota_compare_fusion.5), kind=kOutput, calls=%fused_computation.8 | convolution fusion | flops 39469056 | bytes 178176 | tf_op jit(solution)/shard_map/khry,ryl->khl/dot_general | solution.py:223
  37.1 0.8 select_reduce_fusion.2
  38.1 0.7 copy.48
  38.8 13.1 %all-to-all-start = ((f32[2,96,16]{2,0,1:T(2,128)}), f32[2,96,16]{2,0,1:T(2,128)S(1)}, u32[]{:S(2)}, u32[]{:S(2)}) async-start(f32[2,96,16]{2,0,1:T(2,128)} %copy.48), calls=%async_computation | async-start | bytes 196608 | tf_op jit(solution)/shard_map/all_to_all | solution.py:170
  52.0 13.5 %all-to-all-done = f32[2,96,16]{2,0,1:T(2,128)S(1)} async-done(((f32[2,96,16]{2,0,1:T(2,128)}), f32[2,96,16]{2,0,1:T(2,128)S(1)}, u32[]{:S(2)}, u32[]{:S(2)}) %all-to-all-start) | async-done | bytes 12320 | tf_op jit(solution)/shard_map/all_to_all | solution.py:170
  66.0 0.5 select_reduce_fusion.4
  66.5 8.4 %collective-permute-start.4 = (f32[2,8,128]{2,1,0:T(8,128)S(1)}, f32[2,8,128]{2,1,0:T(8,128)S(1)}, u32[]{:S(2)}, u32[]{:S(2)}) collective-permute-start(f32[2,8,128]{2,1,0:T(8,128)S(1)} %pad_maximum_fusion.6), channel_id=1, source_target_pairs={{0,4},{1,5},{2,6},{3,7},{4,0},{5,1},{6,2},{7,3},{8,12},{9,13},{10,... | collective-permute-start | bytes 24584 | tf_op jit(solution)/shard_map/ppermute | solution.py:196
  75.0 1.0 collective-permute-done.4
  76.0 3.0 %collective-permute-start.5 = (f32[2,8,128]{2,1,0:T(8,128)S(1)}, f32[2,8,128]{2,1,0:T(8,128)S(1)}, u32[]{:S(2)}, u32[]{:S(2)}) collective-permute-start(f32[2,8,128]{2,1,0:T(8,128)S(1)} %fusion.21), channel_id=1, source_target_pairs={{0,2},{1,3},{2,0},{3,1},{4,6},{5,7},{6,4},{7,5},{8,10},{9,11},{10,... | collective-permute-start | bytes 24584 | tf_op jit(solution)/shard_map/ppermute | solution.py:196
  79.1 2.2 %collective-permute-done.5 = f32[2,8,128]{2,1,0:T(8,128)S(1)} collective-permute-done((f32[2,8,128]{2,1,0:T(8,128)S(1)}, f32[2,8,128]{2,1,0:T(8,128)S(1)}, u32[]{:S(2)}, u32[]{:S(2)}) %collective-permute-start.5) | collective-permute-done | bytes 8224 | tf_op jit(solution)/shard_map/ppermute | solution.py:196
  81.3 3.2 %collective-permute-start.6 = (f32[2,8,128]{2,1,0:T(8,128)S(1)}, f32[2,8,128]{2,1,0:T(8,128)S(1)}, u32[]{:S(2)}, u32[]{:S(2)}) collective-permute-start(f32[2,8,128]{2,1,0:T(8,128)S(1)} %fusion.26), channel_id=1, source_target_pairs={{0,1},{1,0},{2,3},{3,2},{4,5},{5,4},{6,7},{7,6},{8,9},{9,8},{10,11... | collective-permute-start | bytes 24584 | tf_op jit(solution)/shard_map/ppermute | solution.py:196
  84.5 1.2 %collective-permute-done.6 = f32[2,8,128]{2,1,0:T(8,128)S(1)} collective-permute-done((f32[2,8,128]{2,1,0:T(8,128)S(1)}, f32[2,8,128]{2,1,0:T(8,128)S(1)}, u32[]{:S(2)}, u32[]{:S(2)}) %collective-permute-start.6) | collective-permute-done | bytes 8224 | tf_op jit(solution)/shard_map/ppermute | solution.py:196
  85.7 0.6 select_reduce_fusion.3
  86.4 0.7 copy.54
  87.1 8.7 %all-to-all-start.1 = ((f32[96,1,16]{2,1,0:T(1,128)}), f32[96,1,16]{2,1,0:T(1,128)S(1)}, u32[]{:S(2)}, u32[]{:S(2)}) async-start(f32[96,1,16]{2,1,0:T(1,128)} %copy.54), calls=%async_computation.1 | async-start | bytes 98304 | tf_op jit(solution)/shard_map/all_to_all | solution.py:184
  95.7 0.5 dynamic-slice_bitcast_fusion
  96.3 11.9 %all-to-all-done.1 = f32[96,1,16]{2,1,0:T(1,128)S(1)} async-done(((f32[96,1,16]{2,1,0:T(1,128)}), f32[96,1,16]{2,1,0:T(1,128)S(1)}, u32[]{:S(2)}, u32[]{:S(2)}) %all-to-all-start.1) | async-done | bytes 6176 | tf_op jit(solution)/shard_map/all_to_all | solution.py:184
  108.1 0.5 broadcast.201
  108.6 0.8 reduce.7
  109.5 1.1 select_reduce_fusion
  (59 shorter events, 2.9 us)
Async XLA Ops:
  2.6 18.0 %collective-permute-start = (f32[20,3,1,128]{3,2,1,0:T(1,128)S(1)}, f32[20,3,1,128]{3,2,1,0:T(1,128)S(1)}, u32[]{:S(2)}, u32[]{:S(2)}) collective-permute-start(f32[20,3,1,128]{3,2,1,0:T(1,128)S(1)} %pad_maximum_fusion.2), channel_id=1, source_target_pairs={{0,8},{8,16},{16,24},{24,32},{32,40},{40,48},{48,56},{56,64},{64,7... | collective-permute-start | bytes 92168 | tf_op jit(solution)/shard_map/ppermute | solution.py:124
  7.1 13.6 %collective-permute-start.1 = (f32[20,3,1,128]{3,2,1,0:T(1,128)S(1)}, f32[20,3,1,128]{3,2,1,0:T(1,128)S(1)}, u32[]{:S(2)}, u32[]{:S(2)}) collective-permute-start(f32[20,3,1,128]{3,2,1,0:T(1,128)S(1)} %pad_maximum_fusion.3), channel_id=1, source_target_pairs={{8,0},{16,8},{24,16},{32,24},{40,32},{48,40},{56,48},{64,56},{72,6... | collective-permute-start | bytes 92168 | tf_op jit(solution)/shard_map/ppermute | solution.py:125
  17.1 1.9 %copy-start.2 = (s32[3,32,128]{2,1,0:T(8,128)S(1)}, s32[3,32,128]{2,1,0:T(8,128)}, u32[]{:S(2)}) copy-start(s32[3,32,128]{2,1,0:T(8,128)} %param.10) | copy-start | bytes 147460
  17.1 2.0 %copy-start.5 = (s32[512]{0:T(512)S(1)}, s32[512]{0:T(512)}, u32[]{:S(2)}) copy-start(s32[512]{0:T(512)} %param.11) | copy-start | bytes 6148
  17.1 2.3 %copy-start.4 = (s32[6,128]{1,0:T(8,128)S(1)}, s32[6,128]{1,0:T(8,128)}, u32[]{:S(2)}) copy-start(s32[6,128]{1,0:T(8,128)} %param.15) | copy-start | bytes 9220
  17.1 2.3 %copy-start.6 = (f32[128]{0:T(128)S(1)}, f32[128]{0:T(128)}, u32[]{:S(2)}) copy-start(f32[128]{0:T(128)} %param.12) | copy-start | bytes 1540
  17.2 2.6 %copy-start.3 = (f32[6,128]{1,0:T(8,128)S(1)}, f32[6,128]{1,0:T(8,128)}, u32[]{:S(2)}) copy-start(f32[6,128]{1,0:T(8,128)} %param.14) | copy-start | bytes 9220
  19.4 7.2 %copy-start.7 = (f32[128]{0:T(128)S(1)}, f32[128]{0:T(128)}, u32[]{:S(2)}) copy-start(f32[128]{0:T(128)} %param.13) | copy-start | bytes 1540
  20.6 9.2 %copy-start = (f32[20,3,1,128]{3,2,1,0:T(1,128)}, f32[20,3,1,128]{3,2,1,0:T(1,128)S(1)}, u32[]{:S(2)}) copy-start(f32[20,3,1,128]{3,2,1,0:T(1,128)S(1)} %collective-permute-done.xlo_ref) | copy-start | bytes 92164
  20.8 9.1 %copy-start.1 = (f32[20,3,1,128]{3,2,1,0:T(1,128)}, f32[20,3,1,128]{3,2,1,0:T(1,128)S(1)}, u32[]{:S(2)}) copy-start(f32[20,3,1,128]{3,2,1,0:T(1,128)S(1)} %collective-permute-done.1.xhi_ref) | copy-start | bytes 92164
  21.1 5.5 %collective-permute-start.3 = (f32[20,3,34,1]{2,3,1,0:T(1,128)S(1)}, f32[20,3,34,1]{2,3,1,0:T(1,128)S(1)}, u32[]{:S(2)}, u32[]{:S(2)}) collective-permute-start(f32[20,3,34,1]{2,3,1,0:T(1,128)S(1)} %pad_maximum_fusion.5), channel_id=1, source_target_pairs={{1,0},{2,1},{3,2},{4,3},{5,4},{6,5},{7,6},{9,8},{10,9},{11,10},{12... | collective-permute-start | bytes 24488 | tf_op jit(solution)/shard_map/ppermute | solution.py:140
  22.6 5.6 %collective-permute-start.2 = (f32[20,3,34,1]{2,3,1,0:T(1,128)S(1)}, f32[20,3,34,1]{2,3,1,0:T(1,128)S(1)}, u32[]{:S(2)}, u32[]{:S(2)}) collective-permute-start(f32[20,3,34,1]{2,3,1,0:T(1,128)S(1)} %pad_maximum_fusion.4), channel_id=1, source_target_pairs={{0,1},{1,2},{2,3},{3,4},{4,5},{5,6},{6,7},{8,9},{9,10},{10,11},{11... | collective-permute-start | bytes 24488 | tf_op jit(solution)/shard_map/ppermute | solution.py:139
  38.8 26.7 %all-to-all-start = ((f32[2,96,16]{2,0,1:T(2,128)}), f32[2,96,16]{2,0,1:T(2,128)S(1)}, u32[]{:S(2)}, u32[]{:S(2)}) async-start(f32[2,96,16]{2,0,1:T(2,128)} %copy.48), calls=%async_computation | async-start | bytes 196608 | tf_op jit(solution)/shard_map/all_to_all | solution.py:170
  66.5 9.5 %collective-permute-start.4 = (f32[2,8,128]{2,1,0:T(8,128)S(1)}, f32[2,8,128]{2,1,0:T(8,128)S(1)}, u32[]{:S(2)}, u32[]{:S(2)}) collective-permute-start(f32[2,8,128]{2,1,0:T(8,128)S(1)} %pad_maximum_fusion.6), channel_id=1, source_target_pairs={{0,4},{1,5},{2,6},{3,7},{4,0},{5,1},{6,2},{7,3},{8,12},{9,13},{10,... | collective-permute-start | bytes 24584 | tf_op jit(solution)/shard_map/ppermute | solution.py:196
  76.0 5.3 %collective-permute-start.5 = (f32[2,8,128]{2,1,0:T(8,128)S(1)}, f32[2,8,128]{2,1,0:T(8,128)S(1)}, u32[]{:S(2)}, u32[]{:S(2)}) collective-permute-start(f32[2,8,128]{2,1,0:T(8,128)S(1)} %fusion.21), channel_id=1, source_target_pairs={{0,2},{1,3},{2,0},{3,1},{4,6},{5,7},{6,4},{7,5},{8,10},{9,11},{10,... | collective-permute-start | bytes 24584 | tf_op jit(solution)/shard_map/ppermute | solution.py:196
  81.3 4.4 %collective-permute-start.6 = (f32[2,8,128]{2,1,0:T(8,128)S(1)}, f32[2,8,128]{2,1,0:T(8,128)S(1)}, u32[]{:S(2)}, u32[]{:S(2)}) collective-permute-start(f32[2,8,128]{2,1,0:T(8,128)S(1)} %fusion.26), channel_id=1, source_target_pairs={{0,1},{1,0},{2,3},{3,2},{4,5},{5,4},{6,7},{7,6},{8,9},{9,8},{10,11... | collective-permute-start | bytes 24584 | tf_op jit(solution)/shard_map/ppermute | solution.py:196
  87.1 21.0 %all-to-all-start.1 = ((f32[96,1,16]{2,1,0:T(1,128)}), f32[96,1,16]{2,1,0:T(1,128)S(1)}, u32[]{:S(2)}, u32[]{:S(2)}) async-start(f32[96,1,16]{2,1,0:T(1,128)} %copy.54), calls=%async_computation.1 | async-start | bytes 98304 | tf_op jit(solution)/shard_map/all_to_all | solution.py:184

commit v12 on v11

--- a/solution.py
+++ b/solution.py
@@ -114,11 +114,15 @@
     return (inflow + coupled) / total
 
 
+def relaxed_face(face):
+    return jnp.stack(collide_list([face[d] for d in range(19)]))
+
+
 def exchange_halos(populations, fluid):
     count_x = lax.axis_size("gx")
     count_y = lax.axis_size("gy")
     faces_x = [
-        jnp.concatenate([populations[:, :, at, None, :], fluid[None, :, at, None, :]], axis=0)
+        jnp.concatenate([relaxed_face(populations[:, :, at, None, :]), fluid[None, :, at, None, :]], axis=0)
         for at in (0, -1)
     ]
     x_low = lax.ppermute(faces_x[1], "gx", [(i, (i + 1) % count_x) for i in range(count_x)])
@@ -128,7 +132,7 @@
             [
                 x_low[:, :, :, at, None],
                 jnp.concatenate(
-                    [populations[:, :, :, at, None], fluid[None, :, :, at, None]], axis=0
+                    [relaxed_face(populations[:, :, :, at, None]), fluid[None, :, :, at, None]], axis=0
                 ),
                 x_high[:, :, :, at, None],
             ],
@@ -298,7 +302,7 @@
 
     def halo(ref):
         values = [ref[d] for d in range(20)]
-        return collide_list(values[:19]), values[19]
+        return values[:19], values[19]
 
     xlo, xlo_f = halo(xlo_ref)
     xhi, xhi_f = halo(xhi_ref)

time: 111 us -> 139 us (1.25); the launches traced: 111 us -> 137 us
  other arithmetic: 6.55 us -> 32.7 us
  starting transfers between devices: 56 us -> 54.5 us
    unnamed x0 -> x72, other arithmetic: none -> 26.2 us
    unnamed x20 -> x58, local copies, waits for them, and re-layouts: 0.96 us -> 3.62 us
    slice x2, local copies, waits for them, and re-layouts: 2.95 us -> 1.55 us  [relaxed_face(): return jnp.stack(collide_list([face[d] for d in range(19)]))]
  transfers between devices with their start and end apart: 9 -> 9, of which waited for: 5 -> 5; matrix products, arithmetic and copies ran while one was open for 5% -> 7% of each run, Pallas kernels for 0% -> 0%
where the time goes in v12:
time: 139 us; the launch traced here: 137 us
  starting transfers between devices  54.5 us (39%)
  other arithmetic  32.7 us (24%)
  waiting for transfers between devices  31 us (22%)
  local copies, waits for them, and re-layouts  11.9 us (9%)
  Pallas kernels  3.87 us (3%)
  matrix products  1.97 us (1%)
    unnamed x72, other arithmetic  26.2 us
    ppermute x3, starting transfers between devices, row_sum(): lax.ppermute(values, axis, [(j, j ^ step) for j in range(count)])  14.4 us
    all_to_all x1, waiting for transfers between devices, on_device(): lax.all_to_all(outgoing, 'gx', split_axis=1, concat_axis=1, tiled=True)  13.5 us
    all_to_all x1, waiting for transfers between devices, on_device(): lax.all_to_all(answered.reshape(count_x, count_y * capacity), 'gx', split...  11.9 us
    all_to_all x1, starting transfers between devices, on_device(): lax.all_to_all(outgoing, 'gx', split_axis=1, concat_axis=1, tiled=True)  11.8 us
    ppermute x1, starting transfers between devices, exchange_halos(): lax.ppermute(faces_x[0], 'gx', [((i + 1) % count_x, i) for i in range(cou...  9.81 us
    all_to_all x1, starting transfers between devices, on_device(): lax.all_to_all(answered.reshape(count_x, count_y * capacity), 'gx', split...  8.66 us
    ppermute x3, waiting for transfers between devices, row_sum(): lax.ppermute(values, axis, [(j, j ^ step) for j in range(count)])  5.57 us
  transfers between devices with their start and end apart: 9, of which 5 were waited for; matrix products, arithmetic and copies ran while one was open for 7% of the time, Pallas kernels for 0%

profile of v12, /device:TPU:1, one launch (start us, length us, event | category | flops | bytes accessed | tf_op | source)
XLA Modules:
  0.0 137.1 jit_solution(12134729253988355692)
XLA Ops:
  0.6 1.0 constant_dynamic-update-slice_fusion.39
  1.6 1.0 constant_dynamic-update-slice_fusion.19
  2.6 0.8 subtract_convert_fusion
  4.9 0.7 constant_dynamic-update-slice_fusion.36
  11.4 0.7 constant_dynamic-update-slice_fusion.27
  13.6 0.8 constant_dynamic-update-slice_fusion.24
  14.4 0.8 constant_dynamic-update-slice_fusion.23
  15.8 0.8 constant_dynamic-update-slice_fusion.22
  17.3 0.8 constant_dynamic-update-slice_fusion.21
  26.8 4.5 %collective-permute-start = (f32[20,3,1,128]{3,2,1,0:T(1,128)S(1)}, f32[20,3,1,128]{3,2,1,0:T(1,128)S(1)}, u32[]{:S(2)}, u32[]{:S(2)}) collective-permute-start(f32[20,3,1,128]{3,2,1,0:T(1,128)S(1)} %get-tuple-element.91), channel_id=1, source_target_pairs={{0,8},{8,16},{16,24},{24,32},{32,40},{40,48},{48,56},{56,64},{64,7... | collective-permute-start | bytes 92168 | tf_op jit(solution)/shard_map/ppermute | solution.py:128
  31.3 9.8 %collective-permute-start.1 = (f32[20,3,1,128]{3,2,1,0:T(1,128)S(1)}, f32[20,3,1,128]{3,2,1,0:T(1,128)S(1)}, u32[]{:S(2)}, u32[]{:S(2)}) collective-permute-start(f32[20,3,1,128]{3,2,1,0:T(1,128)S(1)} %get-tuple-element.90), channel_id=1, source_target_pairs={{8,0},{16,8},{24,16},{32,24},{40,32},{48,40},{56,48},{64,56},{72,6... | collective-permute-start | bytes 92168 | tf_op jit(solution)/shard_map/ppermute | solution.py:129
  41.1 1.3 fusion.142
  48.7 1.3 collective-permute-start.3
  50.2 4.0 %collective-permute-start.2 = (f32[20,3,34,1]{2,3,1,0:T(1,128)S(1)}, f32[20,3,34,1]{2,3,1,0:T(1,128)S(1)}, u32[]{:S(2)}, u32[]{:S(2)}) collective-permute-start(f32[20,3,34,1]{2,3,1,0:T(1,128)S(1)} %pad_maximum_fusion.2), channel_id=1, source_target_pairs={{0,1},{1,2},{2,3},{3,4},{4,5},{5,6},{6,7},{8,9},{9,10},{10,11},{11... | collective-permute-start | bytes 24488 | tf_op jit(solution)/shard_map/ppermute | solution.py:143
  54.2 1.6 %copy.119.yhi_ref = f32[20,3,34,1]{3,2,1,0:T(8,128)} copy(f32[20,3,34,1]{2,3,1,0:T(1,128)S(1)} %collective-permute-done.3) | data formatting | bytes 16320 | tf_op jit(solution)/shard_map/ppermute | solution.py:144
  55.8 1.6 %copy.118.ylo_ref = f32[20,3,34,1]{3,2,1,0:T(8,128)} copy(f32[20,3,34,1]{2,3,1,0:T(1,128)S(1)} %collective-permute-done.2) | data formatting | bytes 16320 | tf_op jit(solution)/shard_map/ppermute | solution.py:143
  57.4 3.9 %shard_map.103 = (f32[19,3,32,128]{3,2,1,0:T(8,128)}, f32[3,32,128]{2,1,0:T(8,128)}) custom-call(f32[19,3,32,128]{3,2,1,0:T(8,128)} %pop_ref.1, s32[3,32,128]{2,1,0:T(8,128)} %solid_ref.1, f32[20,3,1,128]{3,2,1,0:T(1,128)} %copy-done.1, f32[20,3,1,128]{3,2,1,0:T(1,128)} %copy-done.2, f32[20,3,34,1]{3,2,1,0:T(8,128)} %copy.118.ylo_ref, ...), custom_call_target="tpu_custom_call" | custom-call | tf_op jit(solution)/shard_map/pallas_call | solution.py:358
  61.3 0.8 bitcast_reduce-precision_fusion
  62.1 2.0 %fusion.4 = f32[3,4,128]{2,1,0:T(4,128)S(1)} fusion(s32[96,128]{1,0:T(8,128)S(1)} %get-tuple-element.86, bf16[3,96,128]{2,1,0:T(8,128)(2,1)S(1)} %pad_maximum_fusion, pred[4,96,128]{2,0,1:T(4,128)(4,1)S(1)} %iota_compare_fusion.5), kind=kOutput, calls=%fused_computation.8 | convolution fusion | flops 39469056 | bytes 178176 | tf_op jit(solution)/shard_map/khry,ryl->khl/dot_general | solution.py:227
  64.1 0.8 select_reduce_fusion.2
  65.7 11.8 %all-to-all-start = ((f32[2,96,16]{2,0,1:T(2,128)}), f32[2,96,16]{2,0,1:T(2,128)S(1)}, u32[]{:S(2)}, u32[]{:S(2)}) async-start(f32[2,96,16]{2,0,1:T(2,128)} %copy.120), calls=%async_computation | async-start | bytes 196608 | tf_op jit(solution)/shard_map/all_to_all | solution.py:174
  77.6 13.5 %all-to-all-done = f32[2,96,16]{2,0,1:T(2,128)S(1)} async-done(((f32[2,96,16]{2,0,1:T(2,128)}), f32[2,96,16]{2,0,1:T(2,128)S(1)}, u32[]{:S(2)}, u32[]{:S(2)}) %all-to-all-start) | async-done | bytes 12320 | tf_op jit(solution)/shard_map/all_to_all | solution.py:174
  92.2 9.3 %collective-permute-start.4 = (f32[2,8,128]{2,1,0:T(8,128)S(1)}, f32[2,8,128]{2,1,0:T(8,128)S(1)}, u32[]{:S(2)}, u32[]{:S(2)}) collective-permute-start(f32[2,8,128]{2,1,0:T(8,128)S(1)} %pad_maximum_fusion.4), channel_id=1, source_target_pairs={{0,4},{1,5},{2,6},{3,7},{4,0},{5,1},{6,2},{7,3},{8,12},{9,13},{10,... | collective-permute-start | bytes 24584 | tf_op jit(solution)/shard_map/ppermute | solution.py:200
  101.5 1.0 collective-permute-done.4
  102.5 2.8 %collective-permute-start.5 = (f32[2,8,128]{2,1,0:T(8,128)S(1)}, f32[2,8,128]{2,1,0:T(8,128)S(1)}, u32[]{:S(2)}, u32[]{:S(2)}) collective-permute-start(f32[2,8,128]{2,1,0:T(8,128)S(1)} %fusion.141), channel_id=1, source_target_pairs={{0,2},{1,3},{2,0},{3,1},{4,6},{5,7},{6,4},{7,5},{8,10},{9,11},{10,... | collective-permute-start | bytes 24584 | tf_op jit(solution)/shard_map/ppermute | solution.py:200
  105.4 2.5 %collective-permute-done.5 = f32[2,8,128]{2,1,0:T(8,128)S(1)} collective-permute-done((f32[2,8,128]{2,1,0:T(8,128)S(1)}, f32[2,8,128]{2,1,0:T(8,128)S(1)}, u32[]{:S(2)}, u32[]{:S(2)}) %collective-permute-start.5) | collective-permute-done | bytes 8224 | tf_op jit(solution)/shard_map/ppermute | solution.py:200
  107.8 2.3 %collective-permute-start.6 = (f32[2,8,128]{2,1,0:T(8,128)S(1)}, f32[2,8,128]{2,1,0:T(8,128)S(1)}, u32[]{:S(2)}, u32[]{:S(2)}) collective-permute-start(f32[2,8,128]{2,1,0:T(8,128)S(1)} %fusion.146), channel_id=1, source_target_pairs={{0,1},{1,0},{2,3},{3,2},{4,5},{5,4},{6,7},{7,6},{8,9},{9,8},{10,11... | collective-permute-start | bytes 24584 | tf_op jit(solution)/shard_map/ppermute | solution.py:200
  110.1 2.1 %collective-permute-done.6 = f32[2,8,128]{2,1,0:T(8,128)S(1)} collective-permute-done((f32[2,8,128]{2,1,0:T(8,128)S(1)}, f32[2,8,128]{2,1,0:T(8,128)S(1)}, u32[]{:S(2)}, u32[]{:S(2)}) %collective-permute-start.6) | collective-permute-done | bytes 8224 | tf_op jit(solution)/shard_map/ppermute | solution.py:200
  113.6 8.7 %all-to-all-start.1 = ((f32[96,1,16]{2,1,0:T(1,128)}), f32[96,1,16]{2,1,0:T(1,128)S(1)}, u32[]{:S(2)}, u32[]{:S(2)}) async-start(f32[96,1,16]{2,1,0:T(1,128)} %copy.126), calls=%async_computation.1 | async-start | bytes 98304 | tf_op jit(solution)/shard_map/all_to_all | solution.py:188
  122.8 11.9 %all-to-all-done.1 = f32[96,1,16]{2,1,0:T(1,128)S(1)} async-done(((f32[96,1,16]{2,1,0:T(1,128)}), f32[96,1,16]{2,1,0:T(1,128)S(1)}, u32[]{:S(2)}, u32[]{:S(2)}) %all-to-all-start.1) | async-done | bytes 6176 | tf_op jit(solution)/shard_map/all_to_all | solution.py:188
  135.2 0.8 reduce.7
  136.0 1.1 select_reduce_fusion
  (167 shorter events, 29.6 us)
Async XLA Ops:
  0.6 41.8 %copy-start = (f32[19,3,32,128]{3,2,1,0:T(8,128)S(1)}, f32[19,3,32,128]{3,2,1,0:T(8,128)}, u32[]{:S(2)}) copy-start(f32[19,3,32,128]{3,2,1,0:T(8,128)} %pop_ref.1) | copy-start | bytes 2801668
  26.8 21.3 %collective-permute-start = (f32[20,3,1,128]{3,2,1,0:T(1,128)S(1)}, f32[20,3,1,128]{3,2,1,0:T(1,128)S(1)}, u32[]{:S(2)}, u32[]{:S(2)}) collective-permute-start(f32[20,3,1,128]{3,2,1,0:T(1,128)S(1)} %get-tuple-element.91), channel_id=1, source_target_pairs={{0,8},{8,16},{16,24},{24,32},{32,40},{40,48},{48,56},{56,64},{64,7... | collective-permute-start | bytes 92168 | tf_op jit(solution)/shard_map/ppermute | solution.py:128
  31.3 17.0 %collective-permute-start.1 = (f32[20,3,1,128]{3,2,1,0:T(1,128)S(1)}, f32[20,3,1,128]{3,2,1,0:T(1,128)S(1)}, u32[]{:S(2)}, u32[]{:S(2)}) collective-permute-start(f32[20,3,1,128]{3,2,1,0:T(1,128)S(1)} %get-tuple-element.90), channel_id=1, source_target_pairs={{8,0},{16,8},{24,16},{32,24},{40,32},{48,40},{56,48},{64,56},{72,6... | collective-permute-start | bytes 92168 | tf_op jit(solution)/shard_map/ppermute | solution.py:129
  42.9 4.5 %copy-start.3 = (s32[3,32,128]{2,1,0:T(8,128)S(1)}, s32[3,32,128]{2,1,0:T(8,128)}, u32[]{:S(2)}) copy-start(s32[3,32,128]{2,1,0:T(8,128)} %param.10) | copy-start | bytes 147460
  43.3 4.2 %copy-start.6 = (s32[512]{0:T(512)S(1)}, s32[512]{0:T(512)}, u32[]{:S(2)}) copy-start(s32[512]{0:T(512)} %param.11) | copy-start | bytes 6148
  43.3 4.5 %copy-start.5 = (s32[6,128]{1,0:T(8,128)S(1)}, s32[6,128]{1,0:T(8,128)}, u32[]{:S(2)}) copy-start(s32[6,128]{1,0:T(8,128)} %param.15) | copy-start | bytes 9220
  43.3 4.6 %copy-start.7 = (f32[128]{0:T(128)S(1)}, f32[128]{0:T(128)}, u32[]{:S(2)}) copy-start(f32[128]{0:T(128)} %param.12) | copy-start | bytes 1540
  43.4 4.8 %copy-start.4 = (f32[6,128]{1,0:T(8,128)S(1)}, f32[6,128]{1,0:T(8,128)}, u32[]{:S(2)}) copy-start(f32[6,128]{1,0:T(8,128)} %param.14) | copy-start | bytes 9220
  44.2 10.0 %copy-start.8 = (f32[128]{0:T(128)S(1)}, f32[128]{0:T(128)}, u32[]{:S(2)}) copy-start(f32[128]{0:T(128)} %param.13) | copy-start | bytes 1540
  48.2 9.2 %copy-start.1 = (f32[20,3,1,128]{3,2,1,0:T(1,128)}, f32[20,3,1,128]{3,2,1,0:T(1,128)S(1)}, u32[]{:S(2)}) copy-start(f32[20,3,1,128]{3,2,1,0:T(1,128)S(1)} %collective-permute-done.xlo_ref) | copy-start | bytes 92164
  48.3 9.1 %copy-start.2 = (f32[20,3,1,128]{3,2,1,0:T(1,128)}, f32[20,3,1,128]{3,2,1,0:T(1,128)S(1)}, u32[]{:S(2)}) copy-start(f32[20,3,1,128]{3,2,1,0:T(1,128)S(1)} %collective-permute-done.1.xhi_ref) | copy-start | bytes 92164
  48.7 5.5 %collective-permute-start.3 = (f32[20,3,34,1]{2,3,1,0:T(1,128)S(1)}, f32[20,3,34,1]{2,3,1,0:T(1,128)S(1)}, u32[]{:S(2)}, u32[]{:S(2)}) collective-permute-start(f32[20,3,34,1]{2,3,1,0:T(1,128)S(1)} %pad_maximum_fusion.3), channel_id=1, source_target_pairs={{1,0},{2,1},{3,2},{4,3},{5,4},{6,5},{7,6},{9,8},{10,9},{11,10},{12... | collective-permute-start | bytes 24488 | tf_op jit(solution)/shard_map/ppermute | solution.py:144
  50.2 5.6 %collective-permute-start.2 = (f32[20,3,34,1]{2,3,1,0:T(1,128)S(1)}, f32[20,3,34,1]{2,3,1,0:T(1,128)S(1)}, u32[]{:S(2)}, u32[]{:S(2)}) collective-permute-start(f32[20,3,34,1]{2,3,1,0:T(1,128)S(1)} %pad_maximum_fusion.2), channel_id=1, source_target_pairs={{0,1},{1,2},{2,3},{3,4},{4,5},{5,6},{6,7},{8,9},{9,10},{10,11},{11... | collective-permute-start | bytes 24488 | tf_op jit(solution)/shard_map/ppermute | solution.py:143
  65.7 25.4 %all-to-all-start = ((f32[2,96,16]{2,0,1:T(2,128)}), f32[2,96,16]{2,0,1:T(2,128)S(1)}, u32[]{:S(2)}, u32[]{:S(2)}) async-start(f32[2,96,16]{2,0,1:T(2,128)} %copy.120), calls=%async_computation | async-start | bytes 196608 | tf_op jit(solution)/shard_map/all_to_all | solution.py:174
  92.2 10.4 %collective-permute-start.4 = (f32[2,8,128]{2,1,0:T(8,128)S(1)}, f32[2,8,128]{2,1,0:T(8,128)S(1)}, u32[]{:S(2)}, u32[]{:S(2)}) collective-permute-start(f32[2,8,128]{2,1,0:T(8,128)S(1)} %pad_maximum_fusion.4), channel_id=1, source_target_pairs={{0,4},{1,5},{2,6},{3,7},{4,0},{5,1},{6,2},{7,3},{8,12},{9,13},{10,... | collective-permute-start | bytes 24584 | tf_op jit(solution)/shard_map/ppermute | solution.py:200
  102.5 5.3 %collective-permute-start.5 = (f32[2,8,128]{2,1,0:T(8,128)S(1)}, f32[2,8,128]{2,1,0:T(8,128)S(1)}, u32[]{:S(2)}, u32[]{:S(2)}) collective-permute-start(f32[2,8,128]{2,1,0:T(8,128)S(1)} %fusion.141), channel_id=1, source_target_pairs={{0,2},{1,3},{2,0},{3,1},{4,6},{5,7},{6,4},{7,5},{8,10},{9,11},{10,... | collective-permute-start | bytes 24584 | tf_op jit(solution)/shard_map/ppermute | solution.py:200
  107.8 4.4 %collective-permute-start.6 = (f32[2,8,128]{2,1,0:T(8,128)S(1)}, f32[2,8,128]{2,1,0:T(8,128)S(1)}, u32[]{:S(2)}, u32[]{:S(2)}) collective-permute-start(f32[2,8,128]{2,1,0:T(8,128)S(1)} %fusion.146), channel_id=1, source_target_pairs={{0,1},{1,0},{2,3},{3,2},{4,5},{5,4},{6,7},{7,6},{8,9},{9,8},{10,11... | collective-permute-start | bytes 24584 | tf_op jit(solution)/shard_map/ppermute | solution.py:200
  113.6 21.1 %all-to-all-start.1 = ((f32[96,1,16]{2,1,0:T(1,128)}), f32[96,1,16]{2,1,0:T(1,128)S(1)}, u32[]{:S(2)}, u32[]{:S(2)}) async-start(f32[96,1,16]{2,1,0:T(1,128)} %copy.126), calls=%async_computation.1 | async-start | bytes 98304 | tf_op jit(solution)/shard_map/all_to_all | solution.py:188

commit v13 on v12

--- a/solution.py
+++ b/solution.py
@@ -115,7 +115,15 @@
 
 
 def relaxed_face(face):
-    return jnp.stack(collide_list([face[d] for d in range(19)]))
+    shape = (19,) + (1,) * (face.ndim - 1)
+    weights = jnp.asarray(np.array(LATTICE_WEIGHTS, np.float32).reshape(shape))
+    steps = [jnp.asarray(DIRECTIONS[:, k].astype(np.float32).reshape(shape)) for k in range(3)]
+    density = jnp.sum(face, axis=0, keepdims=True)
+    velocity = [jnp.sum(step * face, axis=0, keepdims=True) / density for step in steps]
+    speed_sq = velocity[0] * velocity[0] + velocity[1] * velocity[1] + velocity[2] * velocity[2]
+    along = steps[0] * velocity[0] + steps[1] * velocity[1] + steps[2] * velocity[2]
+    equilibrium = weights * density * (1.0 + 3.0 * along + 4.5 * along * along - 1.5 * speed_sq)
+    return face - OMEGA * (face - equilibrium)
 
 
 def exchange_halos(populations, fluid):

time: 139 us -> 114 us (0.82)
  other arithmetic: 32.7 us -> 12.1 us
  local copies, waits for them, and re-layouts: 11.9 us -> 7.71 us
    unnamed x72 -> x0, other arithmetic: 26.2 us -> none
    reduce_sum x0 -> x3, other arithmetic: none -> 3.59 us  [the longest x1 1.97 us: relaxed_face(): density = jnp.sum(face, axis=0, keepdims=True)]
    unnamed x58 -> x28, local copies, waits for them, and re-layouts: 3.62 us -> 0.99 us
    ppermute x1, starting transfers between devices: 9.81 us -> 12.4 us  [exchange_halos(): lax.ppermute(faces_x[0], 'gx', [((i + 1) % count_x, i) for i in range(cou...]
    ppermute x1, starting transfers between devices: 4.5 us -> 1.92 us  [exchange_halos(): lax.ppermute(faces_x[1], 'gx', [(i, (i + 1) % count_x) for i in range(cou...]
    sub x0 -> x2, other arithmetic: none -> 1.88 us  [relaxed_face(): return face - OMEGA * (face - equilibrium)]
    slice x2 -> x0, local copies, waits for them, and re-layouts: 1.55 us -> none  [relaxed_face(): return jnp.stack(collide_list([face[d] for d in range(19)]))]
  transfers between devices with their start and end apart: 9 -> 9, of which waited for: 5 -> 6; matrix products, arithmetic and copies ran while one was open for 7% -> 6% of each run, Pallas kernels for 0% -> 0%
where the time goes in v13:
time: 114 us; the launch traced here: 113 us
  starting transfers between devices  55 us (48%)
  waiting for transfers between devices  31.7 us (28%)
  other arithmetic  12.1 us (11%)
  local copies, waits for them, and re-layouts  7.71 us (7%)
  Pallas kernels  3.87 us (3%)
  matrix products  1.97 us (2%)
    ppermute x3, starting transfers between devices, row_sum(): lax.ppermute(values, axis, [(j, j ^ step) for j in range(count)])  14.4 us
    all_to_all x1, waiting for transfers between devices, on_device(): lax.all_to_all(outgoing, 'gx', split_axis=1, concat_axis=1, tiled=True)  13.5 us
    all_to_all x1, starting transfers between devices, on_device(): lax.all_to_all(outgoing, 'gx', split_axis=1, concat_axis=1, tiled=True)  12.5 us
    ppermute x1, starting transfers between devices, exchange_halos(): lax.ppermute(faces_x[0], 'gx', [((i + 1) % count_x, i) for i in range(cou...  12.4 us
    all_to_all x1, waiting for transfers between devices, on_device(): lax.all_to_all(answered.reshape(count_x, count_y * capacity), 'gx', split...  11.9 us
    all_to_all x1, starting transfers between devices, on_device(): lax.all_to_all(answered.reshape(count_x, count_y * capacity), 'gx', split...  8.53 us
    ppermute x3, waiting for transfers between devices, row_sum(): lax.ppermute(values, axis, [(j, j ^ step) for j in range(count)])  5.04 us
    ppermute x1, starting transfers between devices, exchange_halos(): lax.ppermute(faces_y[1], 'gy', [(j, j + 1) for j in range(count_y - 1)])  3.99 us
  transfers between devices with their start and end apart: 9, of which 6 were waited for; matrix products, arithmetic and copies ran while one was open for 6% of the time, Pallas kernels for 0%

profile of v13, /device:TPU:1, one launch (start us, length us, event | category | flops | bytes accessed | tf_op | source)
XLA Modules:
  0.0 113.4 jit_solution(8094601398273925822)
XLA Ops:
  0.6 0.8 subtract_convert_fusion
  1.4 1.3 %multiply_reduce_fusion.8 = (f32[3,128]{1,0:T(4,128)S(1)}, f32[3,128]{1,0:T(4,128)S(1)}, f32[3,128]{1,0:T(4,128)S(1)}, f32[3,128]{1,0:T(4,128)S(1)}, f32[3,128]{...) fusion(f32[19]{0:T(128)} %constant.82, f32[19,3,32,128]{3,2,1,0:T(8,128)} %pop_ref.1, ...), kind=kLoop, calls=%fused_computation.66 | loop fusion | flops 99072 | bytes 70884 | tf_op jit(solution)/shard_map/reduce_sum | solution.py:122
  2.8 1.5 %multiply_subtract_fusion.2 = (f32[19,3,1,128]{3,2,1,0:T(1,128)S(1)}, f32[19,3,1,128]{3,2,1,0:T(1,128)S(1)}) fusion(f32[3,128]{1,0:T(4,128)S(1)} %get-tuple-element.44, f32[3,128]{1,0:T(4,128)S(1)} %get-tuple-element.47, f32[3,128]{1,0:T(4,128)S(1)} %get-tuple-element.46, f32[3,128]{1,0:T(4,128)S(1)} %get-tuple-element.45, ...), kind=kLoop, calls=%fused_computation.63 | loop fusion | flops 233472 | bytes 132400 | tf_op jit(solution)/shard_map/sub | solution.py:126
  4.4 12.4 %collective-permute-start.1 = (f32[20,3,1,128]{3,2,1,0:T(1,128)S(1)}, f32[20,3,1,128]{3,2,1,0:T(1,128)S(1)}, u32[]{:S(2)}, u32[]{:S(2)}) collective-permute-start(f32[20,3,1,128]{3,2,1,0:T(1,128)S(1)} %pad_maximum_fusion.3), channel_id=1, source_target_pairs={{8,0},{16,8},{24,16},{32,24},{40,32},{48,40},{56,48},{64,56},{72,6... | collective-permute-start | bytes 92168 | tf_op jit(solution)/shard_map/ppermute | solution.py:137
  16.8 1.9 %collective-permute-start = (f32[20,3,1,128]{3,2,1,0:T(1,128)S(1)}, f32[20,3,1,128]{3,2,1,0:T(1,128)S(1)}, u32[]{:S(2)}, u32[]{:S(2)}) collective-permute-start(f32[20,3,1,128]{3,2,1,0:T(1,128)S(1)} %pad_maximum_fusion.2), channel_id=1, source_target_pairs={{0,8},{8,16},{16,24},{24,32},{32,40},{40,48},{48,56},{56,64},{64,7... | collective-permute-start | bytes 92168 | tf_op jit(solution)/shard_map/ppermute | solution.py:136
  18.7 2.0 %slice_reduce_fusion.4 = (f32[3,32]{1,0:T(4,128)S(1)}, f32[3,32]{1,0:T(4,128)S(1)}, f32[19,3,32,1]{3,2,1,0:T(8,128)S(1)}, f32[19,3,32,1]{3,2,1,0:T(8,128)S(1)}) fusion(f32[19,3,32,128]{3,2,1,0:T(8,128)} %pop_ref.1), kind=kLoop, calls=%fused_computation.111 | loop fusion | flops 3456 | bytes 29952 | tf_op jit(solution)/shard_map/reduce_sum | solution.py:121
  23.4 1.3 %collective-permute-done.xlo_ref = f32[20,3,1,128]{3,2,1,0:T(1,128)S(1)} collective-permute-done((f32[20,3,1,128]{3,2,1,0:T(1,128)S(1)}, f32[20,3,1,128]{3,2,1,0:T(1,128)S(1)}, u32[]{:S(2)}, u32[]{:S(2)}) %collective-permute-start) | collective-permute-done | bytes 30752 | tf_op jit(solution)/shard_map/ppermute | solution.py:136
  25.1 1.3 %collective-permute-start.3 = (f32[20,3,34,1]{2,3,1,0:T(1,128)S(1)}, f32[20,3,34,1]{2,3,1,0:T(1,128)S(1)}, u32[]{:S(2)}, u32[]{:S(2)}) collective-permute-start(f32[20,3,34,1]{2,3,1,0:T(1,128)S(1)} %pad_maximum_fusion.5), channel_id=1, source_target_pairs={{1,0},{2,1},{3,2},{4,3},{5,4},{6,5},{7,6},{9,8},{10,9},{11,10},{12... | collective-permute-start | bytes 24488 | tf_op jit(solution)/shard_map/ppermute | solution.py:152
  26.6 4.0 %collective-permute-start.2 = (f32[20,3,34,1]{2,3,1,0:T(1,128)S(1)}, f32[20,3,34,1]{2,3,1,0:T(1,128)S(1)}, u32[]{:S(2)}, u32[]{:S(2)}) collective-permute-start(f32[20,3,34,1]{2,3,1,0:T(1,128)S(1)} %pad_maximum_fusion.4), channel_id=1, source_target_pairs={{0,1},{1,2},{2,3},{3,4},{4,5},{5,6},{6,7},{8,9},{9,10},{10,11},{11... | collective-permute-start | bytes 24488 | tf_op jit(solution)/shard_map/ppermute | solution.py:151
  30.6 1.6 %copy.63.yhi_ref = f32[20,3,34,1]{3,2,1,0:T(8,128)} copy(f32[20,3,34,1]{2,3,1,0:T(1,128)S(1)} %collective-permute-done.3) | data formatting | bytes 16320 | tf_op jit(solution)/shard_map/ppermute | solution.py:152
  32.2 1.6 %copy.62.ylo_ref = f32[20,3,34,1]{3,2,1,0:T(8,128)} copy(f32[20,3,34,1]{2,3,1,0:T(1,128)S(1)} %collective-permute-done.2) | data formatting | bytes 16320 | tf_op jit(solution)/shard_map/ppermute | solution.py:151
  33.8 3.9 %shard_map.247 = (f32[19,3,32,128]{3,2,1,0:T(8,128)}, f32[3,32,128]{2,1,0:T(8,128)}) custom-call(f32[19,3,32,128]{3,2,1,0:T(8,128)} %pop_ref.1, s32[3,32,128]{2,1,0:T(8,128)} %solid_ref.1, f32[20,3,1,128]{3,2,1,0:T(1,128)} %copy-done.1, f32[20,3,1,128]{3,2,1,0:T(1,128)} %copy-done, f32[20,3,34,1]{3,2,1,0:T(8,128)} %copy.62.ylo_ref, ...), custom_call_target="tpu_custom_call" | custom-call | tf_op jit(solution)/shard_map/pallas_call | solution.py:366
  37.7 0.8 bitcast_reduce-precision_fusion
  38.5 2.0 %fusion.4 = f32[3,4,128]{2,1,0:T(4,128)S(1)} fusion(s32[96,128]{1,0:T(8,128)S(1)} %get-tuple-element.59, bf16[3,96,128]{2,1,0:T(8,128)(2,1)S(1)} %pad_maximum_fusion, pred[4,96,128]{2,0,1:T(4,128)(4,1)S(1)} %iota_compare_fusion.5), kind=kOutput, calls=%fused_computation.8 | convolution fusion | flops 39469056 | bytes 178176 | tf_op jit(solution)/shard_map/khry,ryl->khl/dot_general | solution.py:235
  40.5 0.8 select_reduce_fusion.2
  41.4 0.7 copy.64
  42.1 12.5 %all-to-all-start = ((f32[2,96,16]{2,0,1:T(2,128)}), f32[2,96,16]{2,0,1:T(2,128)S(1)}, u32[]{:S(2)}, u32[]{:S(2)}) async-start(f32[2,96,16]{2,0,1:T(2,128)} %copy.64), calls=%async_computation | async-start | bytes 196608 | tf_op jit(solution)/shard_map/all_to_all | solution.py:182
  54.6 13.5 %all-to-all-done = f32[2,96,16]{2,0,1:T(2,128)S(1)} async-done(((f32[2,96,16]{2,0,1:T(2,128)}), f32[2,96,16]{2,0,1:T(2,128)S(1)}, u32[]{:S(2)}, u32[]{:S(2)}) %all-to-all-start) | async-done | bytes 12320 | tf_op jit(solution)/shard_map/all_to_all | solution.py:182
  69.2 8.7 %collective-permute-start.4 = (f32[2,8,128]{2,1,0:T(8,128)S(1)}, f32[2,8,128]{2,1,0:T(8,128)S(1)}, u32[]{:S(2)}, u32[]{:S(2)}) collective-permute-start(f32[2,8,128]{2,1,0:T(8,128)S(1)} %pad_maximum_fusion.6), channel_id=1, source_target_pairs={{0,4},{1,5},{2,6},{3,7},{4,0},{5,1},{6,2},{7,3},{8,12},{9,13},{10,... | collective-permute-start | bytes 24584 | tf_op jit(solution)/shard_map/ppermute | solution.py:208
  77.9 1.0 collective-permute-done.4
  79.0 2.7 %collective-permute-start.5 = (f32[2,8,128]{2,1,0:T(8,128)S(1)}, f32[2,8,128]{2,1,0:T(8,128)S(1)}, u32[]{:S(2)}, u32[]{:S(2)}) collective-permute-start(f32[2,8,128]{2,1,0:T(8,128)S(1)} %fusion.25), channel_id=1, source_target_pairs={{0,2},{1,3},{2,0},{3,1},{4,6},{5,7},{6,4},{7,5},{8,10},{9,11},{10,... | collective-permute-start | bytes 24584 | tf_op jit(solution)/shard_map/ppermute | solution.py:208
  81.7 2.5 %collective-permute-done.5 = f32[2,8,128]{2,1,0:T(8,128)S(1)} collective-permute-done((f32[2,8,128]{2,1,0:T(8,128)S(1)}, f32[2,8,128]{2,1,0:T(8,128)S(1)}, u32[]{:S(2)}, u32[]{:S(2)}) %collective-permute-start.5) | collective-permute-done | bytes 8224 | tf_op jit(solution)/shard_map/ppermute | solution.py:208
  84.3 2.9 %collective-permute-start.6 = (f32[2,8,128]{2,1,0:T(8,128)S(1)}, f32[2,8,128]{2,1,0:T(8,128)S(1)}, u32[]{:S(2)}, u32[]{:S(2)}) collective-permute-start(f32[2,8,128]{2,1,0:T(8,128)S(1)} %fusion.28), channel_id=1, source_target_pairs={{0,1},{1,0},{2,3},{3,2},{4,5},{5,4},{6,7},{7,6},{8,9},{9,8},{10,11... | collective-permute-start | bytes 24584 | tf_op jit(solution)/shard_map/ppermute | solution.py:208
  87.2 1.5 %collective-permute-done.6 = f32[2,8,128]{2,1,0:T(8,128)S(1)} collective-permute-done((f32[2,8,128]{2,1,0:T(8,128)S(1)}, f32[2,8,128]{2,1,0:T(8,128)S(1)}, u32[]{:S(2)}, u32[]{:S(2)}) %collective-permute-start.6) | collective-permute-done | bytes 8224 | tf_op jit(solution)/shard_map/ppermute | solution.py:208
  88.7 0.6 select_reduce_fusion.3
  89.3 0.7 copy.70
  90.1 8.5 %all-to-all-start.1 = ((f32[96,1,16]{2,1,0:T(1,128)}), f32[96,1,16]{2,1,0:T(1,128)S(1)}, u32[]{:S(2)}, u32[]{:S(2)}) async-start(f32[96,1,16]{2,1,0:T(1,128)} %copy.70), calls=%async_computation.1 | async-start | bytes 98304 | tf_op jit(solution)/shard_map/all_to_all | solution.py:196
  98.6 0.5 dynamic-slice_bitcast_fusion
  99.1 11.9 %all-to-all-done.1 = f32[96,1,16]{2,1,0:T(1,128)S(1)} async-done(((f32[96,1,16]{2,1,0:T(1,128)}), f32[96,1,16]{2,1,0:T(1,128)S(1)}, u32[]{:S(2)}, u32[]{:S(2)}) %all-to-all-start.1) | async-done | bytes 6176 | tf_op jit(solution)/shard_map/all_to_all | solution.py:196
  111.0 0.5 broadcast.705
  111.5 0.8 reduce.23
  112.4 1.1 select_reduce_fusion
  (72 shorter events, 4.5 us)
Async XLA Ops:
  4.4 18.9 %collective-permute-start.1 = (f32[20,3,1,128]{3,2,1,0:T(1,128)S(1)}, f32[20,3,1,128]{3,2,1,0:T(1,128)S(1)}, u32[]{:S(2)}, u32[]{:S(2)}) collective-permute-start(f32[20,3,1,128]{3,2,1,0:T(1,128)S(1)} %pad_maximum_fusion.3), channel_id=1, source_target_pairs={{8,0},{16,8},{24,16},{32,24},{40,32},{48,40},{56,48},{64,56},{72,6... | collective-permute-start | bytes 92168 | tf_op jit(solution)/shard_map/ppermute | solution.py:137
  16.8 7.9 %collective-permute-start = (f32[20,3,1,128]{3,2,1,0:T(1,128)S(1)}, f32[20,3,1,128]{3,2,1,0:T(1,128)S(1)}, u32[]{:S(2)}, u32[]{:S(2)}) collective-permute-start(f32[20,3,1,128]{3,2,1,0:T(1,128)S(1)} %pad_maximum_fusion.2), channel_id=1, source_target_pairs={{0,8},{8,16},{16,24},{24,32},{32,40},{40,48},{48,56},{56,64},{64,7... | collective-permute-start | bytes 92168 | tf_op jit(solution)/shard_map/ppermute | solution.py:136
  20.7 1.1 copy-start.2
  20.7 1.2 %copy-start.9 = (s32[512]{0:T(512)S(1)}, s32[512]{0:T(512)}, u32[]{:S(2)}) copy-start(s32[512]{0:T(512)} %param.27) | copy-start | bytes 6148
  20.7 1.5 %copy-start.4 = (f32[19]{0:T(128)S(1)}, f32[19]{0:T(128)}, u32[]{:S(2)}) copy-start(f32[19]{0:T(128)} %constant.82) | copy-start | bytes 232
  20.7 1.5 %copy-start.5 = (f32[19]{0:T(128)S(1)}, f32[19]{0:T(128)}, u32[]{:S(2)}) copy-start(f32[19]{0:T(128)} %constant.83) | copy-start | bytes 232
  20.7 1.5 %copy-start.6 = (f32[19]{0:T(128)S(1)}, f32[19]{0:T(128)}, u32[]{:S(2)}) copy-start(f32[19]{0:T(128)} %constant.84) | copy-start | bytes 232
  20.8 1.7 %copy-start.7 = (s32[6,128]{1,0:T(8,128)S(1)}, s32[6,128]{1,0:T(8,128)}, u32[]{:S(2)}) copy-start(s32[6,128]{1,0:T(8,128)} %param.31) | copy-start | bytes 9220
  20.8 1.7 %copy-start.10 = (f32[128]{0:T(128)S(1)}, f32[128]{0:T(128)}, u32[]{:S(2)}) copy-start(f32[128]{0:T(128)} %param.28) | copy-start | bytes 1540
  20.8 2.0 %copy-start.3 = (f32[6,128]{1,0:T(8,128)S(1)}, f32[6,128]{1,0:T(8,128)}, u32[]{:S(2)}) copy-start(f32[6,128]{1,0:T(8,128)} %param.30) | copy-start | bytes 9220
  20.8 2.1 %copy-start.8 = (f32[19]{0:T(128)S(1)}, f32[19]{0:T(128)}, u32[]{:S(2)}) copy-start(f32[19]{0:T(128)} %constant.81) | copy-start | bytes 232
  21.4 9.2 %copy-start.11 = (f32[128]{0:T(128)S(1)}, f32[128]{0:T(128)}, u32[]{:S(2)}) copy-start(f32[128]{0:T(128)} %param.29) | copy-start | bytes 1540
  23.3 10.5 %copy-start = (f32[20,3,1,128]{3,2,1,0:T(1,128)}, f32[20,3,1,128]{3,2,1,0:T(1,128)S(1)}, u32[]{:S(2)}) copy-start(f32[20,3,1,128]{3,2,1,0:T(1,128)S(1)} %collective-permute-done.1.xhi_ref) | copy-start | bytes 92164
  24.7 9.1 %copy-start.1 = (f32[20,3,1,128]{3,2,1,0:T(1,128)}, f32[20,3,1,128]{3,2,1,0:T(1,128)S(1)}, u32[]{:S(2)}) copy-start(f32[20,3,1,128]{3,2,1,0:T(1,128)S(1)} %collective-permute-done.xlo_ref) | copy-start | bytes 92164
  25.1 5.5 %collective-permute-start.3 = (f32[20,3,34,1]{2,3,1,0:T(1,128)S(1)}, f32[20,3,34,1]{2,3,1,0:T(1,128)S(1)}, u32[]{:S(2)}, u32[]{:S(2)}) collective-permute-start(f32[20,3,34,1]{2,3,1,0:T(1,128)S(1)} %pad_maximum_fusion.5), channel_id=1, source_target_pairs={{1,0},{2,1},{3,2},{4,3},{5,4},{6,5},{7,6},{9,8},{10,9},{11,10},{12... | collective-permute-start | bytes 24488 | tf_op jit(solution)/shard_map/ppermute | solution.py:152
  26.6 5.6 %collective-permute-start.2 = (f32[20,3,34,1]{2,3,1,0:T(1,128)S(1)}, f32[20,3,34,1]{2,3,1,0:T(1,128)S(1)}, u32[]{:S(2)}, u32[]{:S(2)}) collective-permute-start(f32[20,3,34,1]{2,3,1,0:T(1,128)S(1)} %pad_maximum_fusion.4), channel_id=1, source_target_pairs={{0,1},{1,2},{2,3},{3,4},{4,5},{5,6},{6,7},{8,9},{9,10},{10,11},{11... | collective-permute-start | bytes 24488 | tf_op jit(solution)/shard_map/ppermute | solution.py:151
  42.1 26.0 %all-to-all-start = ((f32[2,96,16]{2,0,1:T(2,128)}), f32[2,96,16]{2,0,1:T(2,128)S(1)}, u32[]{:S(2)}, u32[]{:S(2)}) async-start(f32[2,96,16]{2,0,1:T(2,128)} %copy.64), calls=%async_computation | async-start | bytes 196608 | tf_op jit(solution)/shard_map/all_to_all | solution.py:182
  69.2 9.8 %collective-permute-start.4 = (f32[2,8,128]{2,1,0:T(8,128)S(1)}, f32[2,8,128]{2,1,0:T(8,128)S(1)}, u32[]{:S(2)}, u32[]{:S(2)}) collective-permute-start(f32[2,8,128]{2,1,0:T(8,128)S(1)} %pad_maximum_fusion.6), channel_id=1, source_target_pairs={{0,4},{1,5},{2,6},{3,7},{4,0},{5,1},{6,2},{7,3},{8,12},{9,13},{10,... | collective-permute-start | bytes 24584 | tf_op jit(solution)/shard_map/ppermute | solution.py:208
  79.0 5.3 %collective-permute-start.5 = (f32[2,8,128]{2,1,0:T(8,128)S(1)}, f32[2,8,128]{2,1,0:T(8,128)S(1)}, u32[]{:S(2)}, u32[]{:S(2)}) collective-permute-start(f32[2,8,128]{2,1,0:T(8,128)S(1)} %fusion.25), channel_id=1, source_target_pairs={{0,2},{1,3},{2,0},{3,1},{4,6},{5,7},{6,4},{7,5},{8,10},{9,11},{10,... | collective-permute-start | bytes 24584 | tf_op jit(solution)/shard_map/ppermute | solution.py:208
  84.3 4.4 %collective-permute-start.6 = (f32[2,8,128]{2,1,0:T(8,128)S(1)}, f32[2,8,128]{2,1,0:T(8,128)S(1)}, u32[]{:S(2)}, u32[]{:S(2)}) collective-permute-start(f32[2,8,128]{2,1,0:T(8,128)S(1)} %fusion.28), channel_id=1, source_target_pairs={{0,1},{1,0},{2,3},{3,2},{4,5},{5,4},{6,7},{7,6},{8,9},{9,8},{10,11... | collective-permute-start | bytes 24584 | tf_op jit(solution)/shard_map/ppermute | solution.py:208
  90.1 20.9 %all-to-all-start.1 = ((f32[96,1,16]{2,1,0:T(1,128)}), f32[96,1,16]{2,1,0:T(1,128)S(1)}, u32[]{:S(2)}, u32[]{:S(2)}) async-start(f32[96,1,16]{2,1,0:T(1,128)} %copy.70), calls=%async_computation.1 | async-start | bytes 98304 | tf_op jit(solution)/shard_map/all_to_all | solution.py:196

commit v14 on v11

--- a/solution.py
+++ b/solution.py
@@ -114,22 +114,22 @@
     return (inflow + coupled) / total
 
 
-def exchange_halos(populations, fluid):
+def marked(face, solid):
+    first = jnp.where(solid == 1, -face[0], face[0])
+    return jnp.concatenate([first[None], face[1:]], axis=0)
+
+
+def exchange_halos(populations, solid_flag):
     count_x = lax.axis_size("gx")
     count_y = lax.axis_size("gy")
-    faces_x = [
-        jnp.concatenate([populations[:, :, at, None, :], fluid[None, :, at, None, :]], axis=0)
-        for at in (0, -1)
-    ]
+    faces_x = [marked(populations[:, :, at, None, :], solid_flag[:, at, None, :]) for at in (0, -1)]
     x_low = lax.ppermute(faces_x[1], "gx", [(i, (i + 1) % count_x) for i in range(count_x)])
     x_high = lax.ppermute(faces_x[0], "gx", [((i + 1) % count_x, i) for i in range(count_x)])
     faces_y = [
         jnp.concatenate(
             [
                 x_low[:, :, :, at, None],
-                jnp.concatenate(
-                    [populations[:, :, :, at, None], fluid[None, :, :, at, None]], axis=0
-                ),
+                marked(populations[:, :, :, at, None], solid_flag[:, :, at, None]),
                 x_high[:, :, :, at, None],
             ],
             axis=2,
@@ -144,8 +144,7 @@
 def on_device(
     populations, solid_flag, cell_patch, patch_zone, old_pressure, leakage, conductance, neighbour
 ):
-    fluid = (1 - solid_flag).astype(jnp.float32)
-    halos = exchange_halos(populations, fluid)
+    halos = exchange_halos(populations, solid_flag)
     new_populations, momentum_x = lbm_step(populations, solid_flag, halos)
     patch_flux = patch_sums(momentum_x, cell_patch, patch_zone.shape[0])
     zone_dev = old_pressure.shape[0]
@@ -297,8 +296,10 @@
             rel_ref[d, level] = relaxed[d]
 
     def halo(ref):
-        values = [ref[d] for d in range(20)]
-        return collide_list(values[:19]), values[19]
+        values = [ref[d] for d in range(19)]
+        fluid = (values[0] > 0.0).astype(jnp.float32)
+        values[0] = jnp.abs(values[0])
+        return collide_list(values), fluid
 
     xlo, xlo_f = halo(xlo_ref)
     xhi, xhi_f = halo(xhi_ref)

time: 111 us -> 113 us (1.018)
  local copies, waits for them, and re-layouts: 10.6 us -> 12.5 us
  starting transfers between devices: 56 us -> 54.5 us
  waiting for transfers between devices: 29.8 us -> 31 us
    slice x3 -> x4, local copies, waits for them, and re-layouts: 3.11 us -> 4.88 us  [the longest x2 2.89 us: marked(): return jnp.concatenate([first[None], face[1:]], axis=0)]
    all_to_all x1, starting transfers between devices: 13.1 us -> 11.8 us  [on_device(): lax.all_to_all(outgoing, 'gx', split_axis=1, concat_axis=1, tiled=True)]
  transfers between devices with their start and end apart: 9 -> 9, of which waited for: 5 -> 5; matrix products, arithmetic and copies ran while one was open for 5% -> 7% of each run, Pallas kernels for 0% -> 0%
where the time goes in v14:
time: 113 us; the launch traced here: 112 us
  starting transfers between devices  54.5 us (48%)
  waiting for transfers between devices  31 us (27%)
  local copies, waits for them, and re-layouts  12.5 us (11%)
  other arithmetic  6.52 us (6%)
  Pallas kernels  4.45 us (4%)
  matrix products  1.97 us (2%)
    ppermute x3, starting transfers between devices, row_sum(): lax.ppermute(values, axis, [(j, j ^ step) for j in range(count)])  14.4 us
    all_to_all x1, waiting for transfers between devices, on_device(): lax.all_to_all(outgoing, 'gx', split_axis=1, concat_axis=1, tiled=True)  13.5 us
    all_to_all x1, waiting for transfers between devices, on_device(): lax.all_to_all(answered.reshape(count_x, count_y * capacity), 'gx', split...  11.9 us
    all_to_all x1, starting transfers between devices, on_device(): lax.all_to_all(outgoing, 'gx', split_axis=1, concat_axis=1, tiled=True)  11.8 us
    ppermute x1, starting transfers between devices, exchange_halos(): lax.ppermute(faces_x[0], 'gx', [((i + 1) % count_x, i) for i in range(cou...  9.81 us
    all_to_all x1, starting transfers between devices, on_device(): lax.all_to_all(answered.reshape(count_x, count_y * capacity), 'gx', split...  8.63 us
    ppermute x3, waiting for transfers between devices, row_sum(): lax.ppermute(values, axis, [(j, j ^ step) for j in range(count)])  5.57 us
    ppermute x1, starting transfers between devices, exchange_halos(): lax.ppermute(faces_x[1], 'gx', [(i, (i + 1) % count_x) for i in range(cou...  4.5 us
  transfers between devices with their start and end apart: 9, of which 5 were waited for; matrix products, arithmetic and copies ran while one was open for 7% of the time, Pallas kernels for 0%

profile of v14, /device:TPU:1, one launch (start us, length us, event | category | flops | bytes accessed | tf_op | source)
XLA Modules:
  0.0 111.9 jit_solution(6079151376522676172)
XLA Ops:
  0.6 1.1 fusion.27
  1.7 0.8 fusion.21
  2.5 4.5 %collective-permute-start = (f32[19,3,1,128]{3,2,1,0:T(1,128)S(1)}, f32[19,3,1,128]{3,2,1,0:T(1,128)S(1)}, u32[]{:S(2)}, u32[]{:S(2)}) collective-permute-start(f32[19,3,1,128]{3,2,1,0:T(1,128)S(1)} %pad_maximum_fusion.2), channel_id=1, source_target_pairs={{0,8},{8,16},{16,24},{24,32},{32,40},{40,48},{48,56},{56,64},{64,7... | collective-permute-start | bytes 87560 | tf_op jit(solution)/shard_map/ppermute | solution.py:126
  7.1 9.8 %collective-permute-start.1 = (f32[19,3,1,128]{3,2,1,0:T(1,128)S(1)}, f32[19,3,1,128]{3,2,1,0:T(1,128)S(1)}, u32[]{:S(2)}, u32[]{:S(2)}) collective-permute-start(f32[19,3,1,128]{3,2,1,0:T(1,128)S(1)} %pad_maximum_fusion.3), channel_id=1, source_target_pairs={{8,0},{16,8},{24,16},{32,24},{40,32},{48,40},{56,48},{64,56},{72,6... | collective-permute-start | bytes 87560 | tf_op jit(solution)/shard_map/ppermute | solution.py:127
  16.9 1.0 fusion.29
  17.8 1.0 slice_reduce_fusion
  18.9 1.8 %fusion.26 = (f32[18,3,32,1]{3,2,1,0:T(8,128)S(1)}, f32[18,3,32,1]{3,2,1,0:T(8,128)S(1)}) fusion(f32[19,3,32,128]{3,2,1,0:T(8,128)} %pop_ref.1), kind=kLoop, calls=%fused_computation.84 | loop fusion | bytes 27648 | tf_op jit(solution)/shard_map/slice | solution.py:119
  23.0 1.3 %collective-permute-start.3 = (f32[19,3,34,1]{2,3,1,0:T(1,128)S(1)}, f32[19,3,34,1]{2,3,1,0:T(1,128)S(1)}, u32[]{:S(2)}, u32[]{:S(2)}) collective-permute-start(f32[19,3,34,1]{2,3,1,0:T(1,128)S(1)} %pad_maximum_fusion.5), channel_id=1, source_target_pairs={{1,0},{2,1},{3,2},{4,3},{5,4},{6,5},{7,6},{9,8},{10,9},{11,10},{12... | collective-permute-start | bytes 23264 | tf_op jit(solution)/shard_map/ppermute | solution.py:140
  24.5 4.0 %collective-permute-start.2 = (f32[19,3,34,1]{2,3,1,0:T(1,128)S(1)}, f32[19,3,34,1]{2,3,1,0:T(1,128)S(1)}, u32[]{:S(2)}, u32[]{:S(2)}) collective-permute-start(f32[19,3,34,1]{2,3,1,0:T(1,128)S(1)} %pad_maximum_fusion.4), channel_id=1, source_target_pairs={{0,1},{1,2},{2,3},{3,4},{4,5},{5,6},{6,7},{8,9},{9,10},{10,11},{11... | collective-permute-start | bytes 23264 | tf_op jit(solution)/shard_map/ppermute | solution.py:139
  28.5 1.6 %copy.55.yhi_ref = f32[19,3,34,1]{3,2,1,0:T(8,128)} copy(f32[19,3,34,1]{2,3,1,0:T(1,128)S(1)} %collective-permute-done.3) | data formatting | bytes 15504 | tf_op jit(solution)/shard_map/ppermute | solution.py:140
  30.1 1.5 %copy.54.ylo_ref = f32[19,3,34,1]{3,2,1,0:T(8,128)} copy(f32[19,3,34,1]{2,3,1,0:T(1,128)S(1)} %collective-permute-done.2) | data formatting | bytes 15504 | tf_op jit(solution)/shard_map/ppermute | solution.py:139
  31.6 4.5 %shard_map.103 = (f32[19,3,32,128]{3,2,1,0:T(8,128)}, f32[3,32,128]{2,1,0:T(8,128)}) custom-call(f32[19,3,32,128]{3,2,1,0:T(8,128)} %pop_ref.1, s32[3,32,128]{2,1,0:T(8,128)} %solid_ref.1, f32[19,3,1,128]{3,2,1,0:T(1,128)} %copy-done, f32[19,3,1,128]{3,2,1,0:T(1,128)} %copy-done.1, f32[19,3,34,1]{3,2,1,0:T(8,128)} %copy.54.ylo_ref, ...), custom_call_target="tpu_custom_call" | custom-call | tf_op jit(solution)/shard_map/pallas_call | solution.py:355
  36.1 0.8 bitcast_reduce-precision_fusion
  36.9 2.0 %fusion.4 = f32[3,4,128]{2,1,0:T(4,128)S(1)} fusion(s32[96,128]{1,0:T(8,128)S(1)} %get-tuple-element.22, bf16[3,96,128]{2,1,0:T(8,128)(2,1)S(1)} %pad_maximum_fusion, pred[4,96,128]{2,0,1:T(4,128)(4,1)S(1)} %iota_compare_fusion.5), kind=kOutput, calls=%fused_computation.8 | convolution fusion | flops 39469056 | bytes 178176 | tf_op jit(solution)/shard_map/khry,ryl->khl/dot_general | solution.py:222
  38.9 0.8 select_reduce_fusion.2
  39.9 0.7 copy.56
  40.6 11.8 %all-to-all-start = ((f32[2,96,16]{2,0,1:T(2,128)}), f32[2,96,16]{2,0,1:T(2,128)S(1)}, u32[]{:S(2)}, u32[]{:S(2)}) async-start(f32[2,96,16]{2,0,1:T(2,128)} %copy.56), calls=%async_computation | async-start | bytes 196608 | tf_op jit(solution)/shard_map/all_to_all | solution.py:169
  52.4 13.5 %all-to-all-done = f32[2,96,16]{2,0,1:T(2,128)S(1)} async-done(((f32[2,96,16]{2,0,1:T(2,128)}), f32[2,96,16]{2,0,1:T(2,128)S(1)}, u32[]{:S(2)}, u32[]{:S(2)}) %all-to-all-start) | async-done | bytes 12320 | tf_op jit(solution)/shard_map/all_to_all | solution.py:169
  67.0 9.3 %collective-permute-start.4 = (f32[2,8,128]{2,1,0:T(8,128)S(1)}, f32[2,8,128]{2,1,0:T(8,128)S(1)}, u32[]{:S(2)}, u32[]{:S(2)}) collective-permute-start(f32[2,8,128]{2,1,0:T(8,128)S(1)} %pad_maximum_fusion.6), channel_id=1, source_target_pairs={{0,4},{1,5},{2,6},{3,7},{4,0},{5,1},{6,2},{7,3},{8,12},{9,13},{10,... | collective-permute-start | bytes 24584 | tf_op jit(solution)/shard_map/ppermute | solution.py:195
  76.3 1.0 collective-permute-done.4
  77.4 2.8 %collective-permute-start.5 = (f32[2,8,128]{2,1,0:T(8,128)S(1)}, f32[2,8,128]{2,1,0:T(8,128)S(1)}, u32[]{:S(2)}, u32[]{:S(2)}) collective-permute-start(f32[2,8,128]{2,1,0:T(8,128)S(1)} %fusion.25), channel_id=1, source_target_pairs={{0,2},{1,3},{2,0},{3,1},{4,6},{5,7},{6,4},{7,5},{8,10},{9,11},{10,... | collective-permute-start | bytes 24584 | tf_op jit(solution)/shard_map/ppermute | solution.py:195
  80.2 2.5 %collective-permute-done.5 = f32[2,8,128]{2,1,0:T(8,128)S(1)} collective-permute-done((f32[2,8,128]{2,1,0:T(8,128)S(1)}, f32[2,8,128]{2,1,0:T(8,128)S(1)}, u32[]{:S(2)}, u32[]{:S(2)}) %collective-permute-start.5) | collective-permute-done | bytes 8224 | tf_op jit(solution)/shard_map/ppermute | solution.py:195
  82.6 2.3 %collective-permute-start.6 = (f32[2,8,128]{2,1,0:T(8,128)S(1)}, f32[2,8,128]{2,1,0:T(8,128)S(1)}, u32[]{:S(2)}, u32[]{:S(2)}) collective-permute-start(f32[2,8,128]{2,1,0:T(8,128)S(1)} %fusion.31), channel_id=1, source_target_pairs={{0,1},{1,0},{2,3},{3,2},{4,5},{5,4},{6,7},{7,6},{8,9},{9,8},{10,11... | collective-permute-start | bytes 24584 | tf_op jit(solution)/shard_map/ppermute | solution.py:195
  85.0 2.1 %collective-permute-done.6 = f32[2,8,128]{2,1,0:T(8,128)S(1)} collective-permute-done((f32[2,8,128]{2,1,0:T(8,128)S(1)}, f32[2,8,128]{2,1,0:T(8,128)S(1)}, u32[]{:S(2)}, u32[]{:S(2)}) %collective-permute-start.6) | collective-permute-done | bytes 8224 | tf_op jit(solution)/shard_map/ppermute | solution.py:195
  87.0 0.6 select_reduce_fusion.3
  87.7 0.7 copy.62
  88.4 8.6 %all-to-all-start.1 = ((f32[96,1,16]{2,1,0:T(1,128)}), f32[96,1,16]{2,1,0:T(1,128)S(1)}, u32[]{:S(2)}, u32[]{:S(2)}) async-start(f32[96,1,16]{2,1,0:T(1,128)} %copy.62), calls=%async_computation.1 | async-start | bytes 98304 | tf_op jit(solution)/shard_map/all_to_all | solution.py:183
  97.1 0.5 dynamic-slice_bitcast_fusion
  97.6 11.9 %all-to-all-done.1 = f32[96,1,16]{2,1,0:T(1,128)S(1)} async-done(((f32[96,1,16]{2,1,0:T(1,128)}), f32[96,1,16]{2,1,0:T(1,128)S(1)}, u32[]{:S(2)}, u32[]{:S(2)}) %all-to-all-start.1) | async-done | bytes 6176 | tf_op jit(solution)/shard_map/all_to_all | solution.py:183
  109.4 0.5 broadcast.213
  110.0 0.8 reduce.7
  110.8 1.1 select_reduce_fusion
  (61 shorter events, 3.8 us)
Async XLA Ops:
  2.5 20.0 %collective-permute-start = (f32[19,3,1,128]{3,2,1,0:T(1,128)S(1)}, f32[19,3,1,128]{3,2,1,0:T(1,128)S(1)}, u32[]{:S(2)}, u32[]{:S(2)}) collective-permute-start(f32[19,3,1,128]{3,2,1,0:T(1,128)S(1)} %pad_maximum_fusion.2), channel_id=1, source_target_pairs={{0,8},{8,16},{16,24},{24,32},{32,40},{40,48},{48,56},{56,64},{64,7... | collective-permute-start | bytes 87560 | tf_op jit(solution)/shard_map/ppermute | solution.py:126
  7.1 15.6 %collective-permute-start.1 = (f32[19,3,1,128]{3,2,1,0:T(1,128)S(1)}, f32[19,3,1,128]{3,2,1,0:T(1,128)S(1)}, u32[]{:S(2)}, u32[]{:S(2)}) collective-permute-start(f32[19,3,1,128]{3,2,1,0:T(1,128)S(1)} %pad_maximum_fusion.3), channel_id=1, source_target_pairs={{8,0},{16,8},{24,16},{32,24},{40,32},{48,40},{56,48},{64,56},{72,6... | collective-permute-start | bytes 87560 | tf_op jit(solution)/shard_map/ppermute | solution.py:127
  18.9 2.1 %copy-start.2 = (s32[3,32,128]{2,1,0:T(8,128)S(1)}, s32[3,32,128]{2,1,0:T(8,128)}, u32[]{:S(2)}) copy-start(s32[3,32,128]{2,1,0:T(8,128)} %param.10) | copy-start | bytes 147460
  18.9 2.2 %copy-start.5 = (s32[512]{0:T(512)S(1)}, s32[512]{0:T(512)}, u32[]{:S(2)}) copy-start(s32[512]{0:T(512)} %param.11) | copy-start | bytes 6148
  18.9 2.5 %copy-start.4 = (s32[6,128]{1,0:T(8,128)S(1)}, s32[6,128]{1,0:T(8,128)}, u32[]{:S(2)}) copy-start(s32[6,128]{1,0:T(8,128)} %param.15) | copy-start | bytes 9220
  18.9 2.5 %copy-start.6 = (f32[128]{0:T(128)S(1)}, f32[128]{0:T(128)}, u32[]{:S(2)}) copy-start(f32[128]{0:T(128)} %param.12) | copy-start | bytes 1540
  18.9 2.8 %copy-start.3 = (f32[6,128]{1,0:T(8,128)S(1)}, f32[6,128]{1,0:T(8,128)}, u32[]{:S(2)}) copy-start(f32[6,128]{1,0:T(8,128)} %param.14) | copy-start | bytes 9220
  21.3 7.1 %copy-start.7 = (f32[128]{0:T(128)S(1)}, f32[128]{0:T(128)}, u32[]{:S(2)}) copy-start(f32[128]{0:T(128)} %param.13) | copy-start | bytes 1540
  22.5 9.1 %copy-start = (f32[19,3,1,128]{3,2,1,0:T(1,128)}, f32[19,3,1,128]{3,2,1,0:T(1,128)S(1)}, u32[]{:S(2)}) copy-start(f32[19,3,1,128]{3,2,1,0:T(1,128)S(1)} %collective-permute-done.xlo_ref) | copy-start | bytes 87556
  22.7 9.0 %copy-start.1 = (f32[19,3,1,128]{3,2,1,0:T(1,128)}, f32[19,3,1,128]{3,2,1,0:T(1,128)S(1)}, u32[]{:S(2)}) copy-start(f32[19,3,1,128]{3,2,1,0:T(1,128)S(1)} %collective-permute-done.1.xhi_ref) | copy-start | bytes 87556
  23.0 5.5 %collective-permute-start.3 = (f32[19,3,34,1]{2,3,1,0:T(1,128)S(1)}, f32[19,3,34,1]{2,3,1,0:T(1,128)S(1)}, u32[]{:S(2)}, u32[]{:S(2)}) collective-permute-start(f32[19,3,34,1]{2,3,1,0:T(1,128)S(1)} %pad_maximum_fusion.5), channel_id=1, source_target_pairs={{1,0},{2,1},{3,2},{4,3},{5,4},{6,5},{7,6},{9,8},{10,9},{11,10},{12... | collective-permute-start | bytes 23264 | tf_op jit(solution)/shard_map/ppermute | solution.py:140
  24.5 5.6 %collective-permute-start.2 = (f32[19,3,34,1]{2,3,1,0:T(1,128)S(1)}, f32[19,3,34,1]{2,3,1,0:T(1,128)S(1)}, u32[]{:S(2)}, u32[]{:S(2)}) collective-permute-start(f32[19,3,34,1]{2,3,1,0:T(1,128)S(1)} %pad_maximum_fusion.4), channel_id=1, source_target_pairs={{0,1},{1,2},{2,3},{3,4},{4,5},{5,6},{6,7},{8,9},{9,10},{10,11},{11... | collective-permute-start | bytes 23264 | tf_op jit(solution)/shard_map/ppermute | solution.py:139
  40.6 25.4 %all-to-all-start = ((f32[2,96,16]{2,0,1:T(2,128)}), f32[2,96,16]{2,0,1:T(2,128)S(1)}, u32[]{:S(2)}, u32[]{:S(2)}) async-start(f32[2,96,16]{2,0,1:T(2,128)} %copy.56), calls=%async_computation | async-start | bytes 196608 | tf_op jit(solution)/shard_map/all_to_all | solution.py:169
  67.0 10.4 %collective-permute-start.4 = (f32[2,8,128]{2,1,0:T(8,128)S(1)}, f32[2,8,128]{2,1,0:T(8,128)S(1)}, u32[]{:S(2)}, u32[]{:S(2)}) collective-permute-start(f32[2,8,128]{2,1,0:T(8,128)S(1)} %pad_maximum_fusion.6), channel_id=1, source_target_pairs={{0,4},{1,5},{2,6},{3,7},{4,0},{5,1},{6,2},{7,3},{8,12},{9,13},{10,... | collective-permute-start | bytes 24584 | tf_op jit(solution)/shard_map/ppermute | solution.py:195
  77.4 5.3 %collective-permute-start.5 = (f32[2,8,128]{2,1,0:T(8,128)S(1)}, f32[2,8,128]{2,1,0:T(8,128)S(1)}, u32[]{:S(2)}, u32[]{:S(2)}) collective-permute-start(f32[2,8,128]{2,1,0:T(8,128)S(1)} %fusion.25), channel_id=1, source_target_pairs={{0,2},{1,3},{2,0},{3,1},{4,6},{5,7},{6,4},{7,5},{8,10},{9,11},{10,... | collective-permute-start | bytes 24584 | tf_op jit(solution)/shard_map/ppermute | solution.py:195
  82.6 4.4 %collective-permute-start.6 = (f32[2,8,128]{2,1,0:T(8,128)S(1)}, f32[2,8,128]{2,1,0:T(8,128)S(1)}, u32[]{:S(2)}, u32[]{:S(2)}) collective-permute-start(f32[2,8,128]{2,1,0:T(8,128)S(1)} %fusion.31), channel_id=1, source_target_pairs={{0,1},{1,0},{2,3},{3,2},{4,5},{5,4},{6,7},{7,6},{8,9},{9,8},{10,11... | collective-permute-start | bytes 24584 | tf_op jit(solution)/shard_map/ppermute | solution.py:195
  88.4 21.0 %all-to-all-start.1 = ((f32[96,1,16]{2,1,0:T(1,128)}), f32[96,1,16]{2,1,0:T(1,128)S(1)}, u32[]{:S(2)}, u32[]{:S(2)}) async-start(f32[96,1,16]{2,1,0:T(1,128)} %copy.62), calls=%async_computation.1 | async-start | bytes 98304 | tf_op jit(solution)/shard_map/all_to_all | solution.py:183
